TPU v7x, 512 devices: a whole 4x8x8 slice. The times are simulated.
512 devices in a mesh: seq: 16 (over z, core), mlp: 8 (over y), tp: 4 (over x).
Axes of the slice: x: 4, y: 8, z: 8, core: 2. Of those that a mesh axis runs over, the one named last changes fastest.
Arguments:
- hidden: bfloat16 [64, 2048], P('mlp'), may hold values from -6 to 6
- lengths: int32 [64], P('mlp'), may hold values from 4 to 8192, as said below
- attention_gain: bfloat16 [2048], replicated, may hold values from 0.099609375 to 1.8984375
- query_weight: bfloat16 [2048, 2048], P('seq', 'tp'), may hold values from -0.125 to 0.125
- key_weight: bfloat16 [2048, 512], P('seq', 'tp'), may hold values from -0.125 to 0.125
- value_weight: bfloat16 [2048, 512], P('seq', 'tp'), may hold values from -0.125 to 0.125
- cached_keys: bfloat16 [64, 8192, 512], P('mlp', 'seq', 'tp'), may hold values from -800 to 800
- cached_values: bfloat16 [64, 8192, 512], P('mlp', 'seq', 'tp'), may hold values from -8 to 8
- output_weight: bfloat16 [2048, 2048], P('tp', 'seq'), may hold values from -0.125 to 0.125
- feedforward_gain: bfloat16 [2048], replicated, may hold values from 0.099609375 to 1.8984375
- gate_weight: bfloat16 [2048, 8192], P('mlp', ('seq', 'tp')), may hold values from -0.125 to 0.125
- up_weight: bfloat16 [2048, 8192], P('mlp', ('seq', 'tp')), may hold values from -0.125 to 0.125
- down_weight: bfloat16 [8192, 2048], P(('seq', 'tp'), 'mlp'), may hold values from -0.0625 to 0.0625
Outputs:
- updated_hidden: bfloat16 [64, 2048], P('mlp')
- new_keys: bfloat16 [64, 512], P('mlp', 'tp')
- new_values: bfloat16 [64, 512], P('mlp', 'tp')
Inputs may be any that keep to these rules, and one draw needn't show every extreme that they name: `lengths`: one request in every draw has exactly 8192 cached tokens.
All inputs are finite; a program needn't handle non-finite values.
Results may differ from a plain program's by a relative error of at most 0.012.
Values may be sent and summed in bfloat16 or wider, within the bound.
No kernel may reach another device: no remote copies, remote signals or barrier semaphores. Data moves between devices by JAX's collectives and lax.ppermute only.
A program may use at most 64 MiB of HBM per device.

v0:
```python
import jax
import jax.numpy as jnp
from jax import lax
from jax.sharding import PartitionSpec as P

HD = 64


def merged(x, axis, combine):
    everything = jax.tree.map(lambda part: lax.all_gather(part, axis), x)
    initial = jax.tree.map(lambda part: part[0], everything)

    def hop(k, so_far):
        return combine(so_far, jax.tree.map(lambda part: part[k], everything))

    return lax.fori_loop(1, lax.axis_size(axis), hop, initial)


def rms_norm(vectors, weights):
    mean_square = jnp.mean(vectors * vectors, axis=-1, keepdims=True)
    return vectors * lax.rsqrt(mean_square + 1e-05) * weights.astype(jnp.float32)


def rotate(vectors, positions):
    half_dim = vectors.shape[-1] // 2
    inverse = 500000.0 ** (-(jnp.arange(half_dim, dtype=jnp.float32) * 2.0 / vectors.shape[-1]))
    angles = positions.astype(jnp.float32)[:, None] * inverse[None, :]
    cosine = jnp.cos(angles)[:, None, :]
    sine_part = jnp.sin(angles)[:, None, :]
    first_half = vectors[..., :half_dim]
    second_half = vectors[..., half_dim:]
    return jnp.concatenate(
        [
            first_half * cosine - second_half * sine_part,
            second_half * cosine + first_half * sine_part,
        ],
        axis=-1,
    )


def combine(first, second):
    first_max, first_sum, first_acc = first
    second_max, second_sum, second_acc = second
    joint_max = jnp.maximum(first_max, second_max)
    first_scale = jnp.exp(first_max - joint_max)
    second_scale = jnp.exp(second_max - joint_max)
    return (
        joint_max,
        first_sum * first_scale + second_sum * second_scale,
        first_acc * first_scale[..., None] + second_acc * second_scale[..., None],
    )


def per_device(
    hidden,
    lengths,
    attention_gain,
    query_weight,
    key_weight,
    value_weight,
    cached_keys,
    cached_values,
    output_weight,
    feedforward_gain,
    gate_weight,
    up_weight,
    down_weight,
):
    requests = hidden.shape[0]
    stream = hidden.astype(jnp.float32)
    normed = rms_norm(stream, attention_gain).astype(jnp.bfloat16)
    column_width = query_weight.shape[0]
    own_columns = lax.dynamic_slice_in_dim(
        normed, lax.axis_index("seq") * column_width, column_width, 1
    )
    partial_query = jnp.dot(own_columns, query_weight, preferred_element_type=jnp.float32)
    partial_key = jnp.dot(own_columns, key_weight, preferred_element_type=jnp.float32)
    partial_value = jnp.dot(own_columns, value_weight, preferred_element_type=jnp.float32)
    queries_raw, keys_raw, values_raw = lax.psum((partial_query, partial_key, partial_value), "seq")
    local_heads = query_weight.shape[1] // HD
    key_heads = key_weight.shape[1] // HD
    group_size = local_heads // key_heads
    queries = rotate(queries_raw.reshape(requests, local_heads, HD), lengths).astype(jnp.bfloat16)
    new_keys = (
        rotate(keys_raw.reshape(requests, key_heads, HD), lengths)
        .reshape(requests, key_heads * HD)
        .astype(jnp.bfloat16)
    )
    new_values = values_raw.astype(jnp.bfloat16)
    grouped = queries.reshape(requests, key_heads, group_size, HD)
    block_span = cached_keys.shape[1]
    key_blocks = cached_keys.reshape(requests, block_span, key_heads, HD)
    value_blocks = cached_values.reshape(requests, block_span, key_heads, HD)
    score_scale = HD ** (-0.5)
    first_position = lax.axis_index("seq") * block_span
    positions = first_position + jnp.arange(block_span, dtype=jnp.int32)
    valid_mask = (positions[None, :] < lengths[:, None])[:, None, None, :]
    scores = (
        jnp.einsum("rgqd,rpgd->rgqp", grouped, key_blocks, preferred_element_type=jnp.float32)
        * score_scale
    )
    block_max = jnp.max(jnp.where(valid_mask, scores, -1e30), axis=-1)
    exp_weights = jnp.where(valid_mask, jnp.exp(scores - block_max[..., None]), 0.0)
    block_sum = jnp.sum(exp_weights, axis=-1)
    block_acc = jnp.einsum(
        "rgqp,rpgd->rgqd",
        exp_weights.astype(jnp.bfloat16),
        value_blocks,
        preferred_element_type=jnp.float32,
    )
    merged_max, merged_sum, merged_acc = merged((block_max, block_sum, block_acc), "seq", combine)
    query_float = grouped.astype(jnp.float32)
    self_score = (
        jnp.sum(
            query_float * new_keys.astype(jnp.float32).reshape(requests, key_heads, 1, HD), axis=-1
        )
        * score_scale
    )
    overall_max = jnp.maximum(merged_max, self_score)
    rescale = jnp.exp(merged_max - overall_max)
    self_weight = jnp.exp(self_score - overall_max)
    total_weight = merged_sum * rescale + self_weight
    weighted_sum = merged_acc * rescale[..., None] + self_weight[..., None] * new_values.astype(
        jnp.float32
    ).reshape(requests, key_heads, 1, HD)
    attended = (
        (weighted_sum / total_weight[..., None])
        .reshape(requests, local_heads * HD)
        .astype(jnp.bfloat16)
    )
    partial_output = jnp.dot(attended, output_weight, preferred_element_type=jnp.float32)
    projected = lax.psum(partial_output, "tp").astype(jnp.bfloat16)
    projected = lax.all_gather(projected, "seq", axis=1, tiled=True)
    mixed_stream = stream + projected.astype(jnp.float32)
    mlp_input = rms_norm(mixed_stream, feedforward_gain).astype(jnp.bfloat16)
    slab_rows = gate_weight.shape[0]
    every_row = lax.all_gather(mlp_input, "mlp", axis=0, tiled=True)
    columns = lax.dynamic_slice_in_dim(every_row, lax.axis_index("mlp") * slab_rows, slab_rows, 1)
    gate_part = jnp.dot(columns, gate_weight, preferred_element_type=jnp.float32)
    upward_part = jnp.dot(columns, up_weight, preferred_element_type=jnp.float32)
    gate_total, upward_total = lax.psum((gate_part, upward_part), "mlp")
    activated = (jax.nn.silu(gate_total) * upward_total).astype(jnp.bfloat16)
    down_part = jnp.dot(activated, down_weight, preferred_element_type=jnp.float32)
    down_total = lax.psum(down_part, ("seq", "tp")).astype(jnp.bfloat16)
    returned = lax.all_to_all(down_total, "mlp", split_axis=0, concat_axis=1, tiled=True)
    updated_hidden = (mixed_stream + returned.astype(jnp.float32)).astype(jnp.bfloat16)
    return (updated_hidden, new_keys, new_values)


def solution(mesh):
    return jax.shard_map(
        per_device,
        mesh=mesh,
        in_specs=(
            P("mlp", None),
            P("mlp"),
            P(),
            P("seq", "tp"),
            P("seq", "tp"),
            P("seq", "tp"),
            P("mlp", "seq", "tp"),
            P("mlp", "seq", "tp"),
            P("tp", "seq"),
            P(),
            P("mlp", ("seq", "tp")),
            P("mlp", ("seq", "tp")),
            P(("seq", "tp"), "mlp"),
        ),
        out_specs=(P("mlp", None), P("mlp", "tp"), P("mlp", "tp")),
        check_vma=False,
    )
```

profile of v0, /device:TPU:1, one launch (start us, length us, event | category | flops | bytes accessed | tf_op | source)
XLA Modules:
  0.0 513.4 jit_solution(9470498176692144958)
XLA Ops:
  7.2 0.8 convert_element_type.78
  8.1 0.1 multiply_reduce_fusion.1
  8.2 0.8 dynamic-slice
  9.0 0.2 fusion.31
  9.3 0.7 copy-done.10
  9.9 0.2 fusion.29
  10.2 0.5 copy-done.11
  10.7 0.2 fusion.33
  10.9 0.5 copy-done.9
  11.4 1.6 copy.49
  13.0 0.5 copy.50
  13.6 0.1 multiply_cosine_fusion
  13.7 52.1 %all-reduce = (f32[8,8,64]{2,1,0:T(8,128)S(1)}, f32[8,2,64]{2,1,0:T(2,128)S(1)}, bf16[8,128]{1,0:T(8,128)(2,1)S(1)}) all-reduce(f32[8,8,64]{2,1,0:T(8,128)S(1)} %reshape.146, f32[8,2,64]{2,1,0:T(2,128)S(1)} %reshape.149, f32[8,128]{1,0:T(8,128)S(1)} %fusion.33), channel_id=1, replica_groups=mesh['seq'=16,'mlp'=8,'tp'=4] {'seq'}, use_global_device_ids=true, to_apply=%region_1.0 | all-reduce | flops 6144 | bytes 47104 | tf_op jit(solution)/shard_map/psum | solution.py:79
  65.9 0.4 select_reduce_fusion
  66.3 17.9 %all-gather = f32[128,2,4]{2,1,0:T(2,128)S(1)} all-gather(f32[8,2,4]{2,1,0:T(2,128)S(1)} %get-tuple-element.239), channel_id=2, replica_groups=mesh['seq'=16,'mlp'=8,'tp'=4] {'seq'}, dimensions={0}, use_global_device_ids=true | all-gather | bytes 4352 | tf_op jit(solution)/shard_map/all_gather | solution.py:10
  84.1 0.2 fusion.4
  84.3 0.4 fusion.5
  84.8 17.5 %all-gather.2 = f32[128,2,4,64]{3,2,1,0:T(4,128)S(1)} all-gather(f32[8,2,4,64]{3,2,1,0:T(4,128)S(1)} %fusion.5), channel_id=4, replica_groups=mesh['seq'=16,'mlp'=8,'tp'=4] {'seq'}, dimensions={0}, use_global_device_ids=true | all-gather | bytes 278528 | tf_op jit(solution)/shard_map/all_gather | solution.py:10
  102.3 14.8 %all-gather.1 = f32[128,2,4]{2,1,0:T(2,128)S(1)} all-gather(f32[8,2,4]{2,1,0:T(2,128)S(1)} %fusion.4), channel_id=3, replica_groups=mesh['seq'=16,'mlp'=8,'tp'=4] {'seq'}, dimensions={0}, use_global_device_ids=true | all-gather | bytes 4352 | tf_op jit(solution)/shard_map/all_gather | solution.py:10
  117.1 0.3 copy.56
  117.5 0.3 copy.55
  117.8 5.7 %while.19 = (s32[]{:T(128)}, f32[8,2,4]{0,2,1:T(4,128)S(1)}, f32[8,2,4]{0,2,1:T(4,128)S(1)}, f32[8,2,4,64]{3,2,1,0:T(4,128)S(1)}, f32[16,8,2,4]{1,3,2,0:T(4,128)...) while((s32[]{:T(128)}, f32[8,2,4]{0,2,1:T(4,128)S(1)}, ...), condition=%wide.region_5.6_spmd, body=%wide.region_4.5_spmd.sunk | while | flops 12677 | bytes 52887 | solution.py:16
  117.9 0.1 copy.67
  118.1 0.1 fusion.49
  118.3 0.1 copy.67
  118.4 0.1 fusion.49
  118.8 0.1 fusion.49
  119.0 0.1 copy.67
  119.2 0.1 fusion.49
  119.4 0.1 copy.67
  119.6 0.1 fusion.49
  119.9 0.1 fusion.49
  120.1 0.1 copy.67
  120.3 0.1 fusion.49
  120.7 0.1 fusion.49
  120.9 0.1 copy.67
  121.1 0.1 fusion.49
  121.3 0.1 copy.67
  121.5 0.1 fusion.49
  121.8 0.1 fusion.49
  122.0 0.1 copy.67
  122.2 0.1 fusion.49
  122.6 0.1 fusion.49
  123.0 0.1 fusion.49
  123.3 0.1 fusion.49
  123.7 0.2 multiply_reduce_fusion.2
  123.8 0.1 copy.57
  124.0 0.1 copy.58
  124.3 0.1 fusion.10
  124.6 0.1 fusion.35
  124.7 8.5 %psum.52 = bf16[8,128]{1,0:T(8,128)(2,1)S(1)} all-reduce(f32[8,128]{1,0:T(8,128)S(1)} %fusion.35), channel_id=1, replica_groups=mesh['seq'=16,'mlp'=8,'tp'=4] {'tp'}, use_global_device_ids=true, to_apply=%region_9.10 | all-reduce | flops 1024 | bytes 6144 | tf_op jit(solution)/shard_map/psum | solution.py:132
  133.2 17.9 %all_gather.30 = bf16[8,2048]{1,0:T(8,128)(2,1)S(1)} all-gather(bf16[8,128]{1,0:T(8,128)(2,1)S(1)} %psum.52), channel_id=1, replica_groups=mesh['seq'=16,'mlp'=8,'tp'=4] {'seq'}, dimensions={1}, use_global_device_ids=true | all-gather | bytes 34816 | tf_op jit(solution)/shard_map/all_gather | solution.py:133
  151.0 0.1 multiply_reduce_fusion
  151.3 20.1 %all_gather.31 = bf16[64,2048]{1,0:T(8,128)(2,1)S(1)} all-gather(bf16[8,2048]{1,0:T(8,128)(2,1)S(1)} %multiply_convert_fusion), channel_id=1, replica_groups=mesh['seq'=16,'mlp'=8,'tp'=4] {'mlp'}, dimensions={0}, use_global_device_ids=true | all-gather | bytes 294912 | tf_op jit(solution)/shard_map/all_gather | solution.py:137
  171.4 0.7 fusion.13
  172.2 0.1 copy-done.6
  172.3 0.8 fusion.11
  173.0 72.6 %all-reduce.4.cloned.1.call-done = (f32[64,128]{1,0:T(8,128)}, f32[64,128]{1,0:T(8,128)}) async-done(((f32[64,128]{1,0:T(8,128)}, f32[64,128]{1,0:T(8,128)}), (f32[64,128]{1,0:T(8,128)}, f32[64,128]{1,0:T(8,128)})) %all-reduce.4.cloned.1.call-update) | async-done | bytes 65552 | tf_op jit(solution)/shard_map/psum | solution.py:141
  245.7 0.9 fusion.15
  246.6 248.5 %psum.55 = bf16[64,256]{1,0:T(8,128)(2,1)} all-reduce(f32[64,256]{1,0:T(8,128)S(1)} %fusion.15), channel_id=1, replica_groups=mesh['seq'=16,'mlp'=8,'tp'=4] {'seq','tp'}, use_global_device_ids=true, to_apply=%region_13.14 | all-reduce | flops 16384 | bytes 98304 | tf_op jit(solution)/shard_map/psum | solution.py:144
  495.1 3.9 all-to-all-start
  499.0 0.7 convert_element_type.99
  499.7 6.2 %all-to-all-done = bf16[8,8,256]{2,1,0:T(8,128)(2,1)S(1)} async-done(((bf16[8,8,256]{2,1,0:T(8,128)(2,1)}), bf16[8,8,256]{2,1,0:T(8,128)(2,1)S(1)}, u32[]{:S(2)}, u32[]{:S(2)}) %all-to-all-start) | async-done | bytes 32800 | tf_op jit(solution)/shard_map/all_to_all | solution.py:145
  505.9 0.6 add_convert_fusion
  (83 shorter events, 3.7 us)
Async XLA Ops:
  7.2 1.8 copy-start
  7.2 238.5 %all-reduce.4.cloned.1.call-start = ((), (), s32[]{:S(2)}) async-start(), calls=%async_computation.1 | async-start | bytes 131072 | tf_op jit(solution)/shard_map/psum | solution.py:141
  7.2 0.8 copy-start.2
  9.2 0.8 copy-start.10
  9.9 0.8 copy-start.11
  10.7 0.7 copy-start.9
  11.4 1.6 copy-start.1
  65.8 58.5 %copy-start.8 = (bf16[8,128]{1,0:T(8,128)(2,1)}, bf16[8,128]{1,0:T(8,128)(2,1)S(1)}, u32[]{:S(2)}) copy-start(bf16[8,128]{1,0:T(8,128)(2,1)S(1)} %get-tuple-element.221) | copy-start | bytes 6148
  123.7 0.9 copy-start.3
  124.7 26.5 %copy-start.7 = (bf16[2048]{0:T(1024)(128)(2,1)S(1)}, bf16[2048]{0:T(1024)(128)(2,1)}, u32[]{:S(2)}) copy-start(bf16[2048]{0:T(1024)(128)(2,1)} %param.24) | copy-start | bytes 12292
  151.3 20.1 %copy-start.5 = (bf16[256,128]{1,0:T(8,128)(2,1)S(1)}, bf16[256,128]{1,0:T(8,128)(2,1)}, u32[]{:S(2)}) copy-start(bf16[256,128]{1,0:T(8,128)(2,1)} %param.25) | copy-start | bytes 196612
  171.4 0.8 copy-start.6
  173.0 72.7 %copy-start.4 = (bf16[128,256]{1,0:T(8,128)(2,1)S(1)}, bf16[128,256]{1,0:T(8,128)(2,1)}, u32[]{:S(2)}) copy-start(bf16[128,256]{1,0:T(8,128)(2,1)} %param.27) | copy-start | bytes 196612
  495.1 10.8 %all-to-all-start = ((bf16[8,8,256]{2,1,0:T(8,128)(2,1)}), bf16[8,8,256]{2,1,0:T(8,128)(2,1)S(1)}, u32[]{:S(2)}, u32[]{:S(2)}) async-start(bf16[8,8,256]{2,1,0:T(8,128)(2,1)} %bitcast.25), calls=%async_computation | async-start | bytes 65536 | tf_op jit(solution)/shard_map/all_to_all | solution.py:145
Sparse Core Ops, SparseCore 0:
  173.2 72.4 all-reduce.3
where the time goes:
time: 518 us; the launch traced here: 513 us
  blocking collectives  397 us (77%)
  waiting for transfers between devices  78.9 us (15%)
  between operations  14.2 us (3%)
  local copies, waits for them, and re-layouts  9.53 us (2%)
  other arithmetic  5.37 us (1%)
    psum x1, blocking collectives, per_device(): down_total = lax.psum(down_part, ('seq', 'tp')).astype(jnp.bfloat16)  249 us
    psum x1, waiting for transfers between devices, per_device(): gate_total, upward_total = lax.psum((gate_part, upward_part), 'mlp')  72.6 us
    psum x1, blocking collectives, per_device(): lax.psum((partial_query, partial_key, partial_value), 'seq')  52.1 us
    all_gather x3, blocking collectives, merged(): everything = jax.tree.map(lambda part: lax.all_gather(part, axis), x)  50.2 us
    all_gather x1, blocking collectives, per_device(): every_row = lax.all_gather(mlp_input, 'mlp', axis=0, tiled=True)  20.1 us
    all_gather x1, blocking collectives, per_device(): projected = lax.all_gather(projected, 'seq', axis=1, tiled=True)  17.9 us
  transfers between devices with their start and end apart: 2, of which 2 were waited for; matrix products, arithmetic and copies ran while one was open for 0% of the time, Pallas kernels for 0%

commit v1 on v0

v1 whole, which is shorter than its diff:
```python
import jax
import jax.numpy as jnp
from jax import lax
from jax.sharding import PartitionSpec as P

HD = 64


def rms_norm(vectors, weights):
    mean_square = jnp.mean(vectors * vectors, axis=-1, keepdims=True)
    return vectors * lax.rsqrt(mean_square + 1e-05) * weights.astype(jnp.float32)


def rotate(vectors, positions):
    half_dim = vectors.shape[-1] // 2
    inverse = 500000.0 ** (-(jnp.arange(half_dim, dtype=jnp.float32) * 2.0 / vectors.shape[-1]))
    angles = positions.astype(jnp.float32)[:, None] * inverse[None, :]
    cosine = jnp.cos(angles)[:, None, :]
    sine_part = jnp.sin(angles)[:, None, :]
    first_half = vectors[..., :half_dim]
    second_half = vectors[..., half_dim:]
    return jnp.concatenate(
        [
            first_half * cosine - second_half * sine_part,
            second_half * cosine + first_half * sine_part,
        ],
        axis=-1,
    )


def gathered_sum(x, axis):
    return jnp.sum(lax.all_gather(x, axis), axis=0)


def butterfly_sum(x, axis):
    size = lax.axis_size(axis)
    step = 1
    while step < size:
        pairs = [(i, i ^ step) for i in range(size)]
        x = x + lax.ppermute(x, axis, pairs)
        step *= 2
    return x


def per_device(
    hidden,
    lengths,
    attention_gain,
    query_weight,
    key_weight,
    value_weight,
    cached_keys,
    cached_values,
    output_weight,
    feedforward_gain,
    gate_weight,
    up_weight,
    down_weight,
):
    hidden_units = gate_weight.shape[1]
    with jax.named_scope("mlp_weight_gather"):
        slab = jnp.concatenate([gate_weight, up_weight, down_weight.T], axis=1)
        full_slab = lax.all_gather(slab, "mlp", axis=0, tiled=True)
    gate_full = full_slab[:, :hidden_units]
    up_full = full_slab[:, hidden_units : 2 * hidden_units]
    down_full = full_slab[:, 2 * hidden_units :].T

    requests = hidden.shape[0]
    stream = hidden.astype(jnp.float32)
    normed = rms_norm(stream, attention_gain).astype(jnp.bfloat16)
    column_width = query_weight.shape[0]
    own_columns = lax.dynamic_slice_in_dim(
        normed, lax.axis_index("seq") * column_width, column_width, 1
    )
    query_width = query_weight.shape[1]
    key_width = key_weight.shape[1]
    with jax.named_scope("qkv_projection"):
        partial = jnp.concatenate(
            [
                jnp.dot(own_columns, query_weight, preferred_element_type=jnp.float32),
                jnp.dot(own_columns, key_weight, preferred_element_type=jnp.float32),
                jnp.dot(own_columns, value_weight, preferred_element_type=jnp.float32),
            ],
            axis=1,
        )
        total = gathered_sum(partial, "seq")
    queries_raw = total[:, :query_width]
    keys_raw = total[:, query_width : query_width + key_width]
    values_raw = total[:, query_width + key_width :]
    local_heads = query_width // HD
    key_heads = key_width // HD
    group_size = local_heads // key_heads
    queries = rotate(queries_raw.reshape(requests, local_heads, HD), lengths).astype(jnp.bfloat16)
    new_keys = (
        rotate(keys_raw.reshape(requests, key_heads, HD), lengths)
        .reshape(requests, key_heads * HD)
        .astype(jnp.bfloat16)
    )
    new_values = values_raw.astype(jnp.bfloat16)
    grouped = queries.reshape(requests, key_heads, group_size, HD)
    block_span = cached_keys.shape[1]
    key_blocks = cached_keys.reshape(requests, block_span, key_heads, HD)
    value_blocks = cached_values.reshape(requests, block_span, key_heads, HD)
    score_scale = HD ** (-0.5)
    first_position = lax.axis_index("seq") * block_span
    positions = first_position + jnp.arange(block_span, dtype=jnp.int32)
    valid_mask = (positions[None, :] < lengths[:, None])[:, None, None, :]
    with jax.named_scope("local_attention"):
        scores = (
            jnp.einsum("rgqd,rpgd->rgqp", grouped, key_blocks, preferred_element_type=jnp.float32)
            * score_scale
        )
        block_max = jnp.max(jnp.where(valid_mask, scores, -1e30), axis=-1)
        exp_weights = jnp.where(valid_mask, jnp.exp(scores - block_max[..., None]), 0.0)
        block_sum = jnp.sum(exp_weights, axis=-1)
        block_acc = jnp.einsum(
            "rgqp,rpgd->rgqd",
            exp_weights.astype(jnp.bfloat16),
            value_blocks,
            preferred_element_type=jnp.float32,
        )
    with jax.named_scope("softmax_merge"):
        state = jnp.concatenate([block_max[..., None], block_sum[..., None], block_acc], axis=-1)
        every_state = lax.all_gather(state, "seq")
        every_max = every_state[..., 0]
        every_sum = every_state[..., 1]
        every_acc = every_state[..., 2:]
        query_float = grouped.astype(jnp.float32)
        self_score = (
            jnp.sum(
                query_float * new_keys.astype(jnp.float32).reshape(requests, key_heads, 1, HD),
                axis=-1,
            )
            * score_scale
        )
        overall_max = jnp.maximum(jnp.max(every_max, axis=0), self_score)
        rescale = jnp.exp(every_max - overall_max[None])
        self_weight = jnp.exp(self_score - overall_max)
        total_weight = jnp.sum(every_sum * rescale, axis=0) + self_weight
        weighted_sum = jnp.sum(every_acc * rescale[..., None], axis=0) + self_weight[
            ..., None
        ] * new_values.astype(jnp.float32).reshape(requests, key_heads, 1, HD)
        attended = (
            (weighted_sum / total_weight[..., None])
            .reshape(requests, local_heads * HD)
            .astype(jnp.bfloat16)
        )
    with jax.named_scope("output_projection"):
        partial_output = jnp.dot(attended, output_weight, preferred_element_type=jnp.float32)
        projected = lax.psum(partial_output, "tp").astype(jnp.bfloat16)
        projected = lax.all_gather(projected, "seq", axis=1, tiled=True)
    mixed_stream = stream + projected.astype(jnp.float32)
    mlp_input = rms_norm(mixed_stream, feedforward_gain).astype(jnp.bfloat16)
    with jax.named_scope("feed_forward"):
        gate = jnp.dot(mlp_input, gate_full, preferred_element_type=jnp.float32)
        upward = jnp.dot(mlp_input, up_full, preferred_element_type=jnp.float32)
        activated = (jax.nn.silu(gate) * upward).astype(jnp.bfloat16)
        down_part = jnp.dot(activated, down_full, preferred_element_type=jnp.float32)
    with jax.named_scope("down_reduction"):
        down_total = butterfly_sum(butterfly_sum(down_part, "tp"), "seq").astype(jnp.bfloat16)
    updated_hidden = (mixed_stream + down_total.astype(jnp.float32)).astype(jnp.bfloat16)
    return (updated_hidden, new_keys, new_values)


def solution(mesh):
    return jax.shard_map(
        per_device,
        mesh=mesh,
        in_specs=(
            P("mlp", None),
            P("mlp"),
            P(),
            P("seq", "tp"),
            P("seq", "tp"),
            P("seq", "tp"),
            P("mlp", "seq", "tp"),
            P("mlp", "seq", "tp"),
            P("tp", "seq"),
            P(),
            P("mlp", ("seq", "tp")),
            P("mlp", ("seq", "tp")),
            P(("seq", "tp"), "mlp"),
        ),
        out_specs=(P("mlp", None), P("mlp", "tp"), P("mlp", "tp")),
        check_vma=False,
    )
```

time: 518 us -> 140 us (0.27)
  the two profiles are of different devices: /device:TPU:1 before, /device:TPU:16 now
where the time goes in v1:
time: 140 us
  blocking collectives  66.4 us (47%)
  waiting for transfers between devices  25 us (18%)
  starting transfers between devices  15.2 us (11%)
  between operations  14.4 us (10%)
  local copies, waits for them, and re-layouts  6.45 us (5%)
  matrix products  6.21 us (4%)
  other arithmetic  5.96 us (4%)
    ppermute x6, waiting for transfers between devices, butterfly_sum(): x = x + lax.ppermute(x, axis, pairs)  25 us
    all_gather x1, blocking collectives, gathered_sum(): return jnp.sum(lax.all_gather(x, axis), axis=0)  24.2 us
    all_gather x1, blocking collectives, per_device(): every_state = lax.all_gather(state, 'seq')  15.9 us
    all_gather x1, blocking collectives, per_device(): projected = lax.all_gather(projected, 'seq', axis=1, tiled=True)  15.9 us
    ppermute x6, starting transfers between devices, butterfly_sum(): x = x + lax.ppermute(x, axis, pairs)  15.1 us
    psum x1, blocking collectives, per_device(): projected = lax.psum(partial_output, 'tp').astype(jnp.bfloat16)  10.5 us
    unnamed x23, local copies, waits for them, and re-layouts  3.53 us
  transfers between devices with their start and end apart: 7, of which 6 were waited for; matrix products, arithmetic and copies ran while one was open for 8% of the time, Pallas kernels for 0%

profile of v1, /device:TPU:16, one launch (start us, length us, event | category | flops | bytes accessed | tf_op | source)
XLA Modules:
  0.0 139.6 jit_solution(2580115369153613888)
XLA Ops:
  7.2 0.0 copy-start
  7.2 0.0 all-gather.4.cloned.1.call-start
  7.2 1.0 copy.119
  8.3 0.9 copy.120
  9.2 1.5 %pad_maximum_fusion = bf16[256,384]{0,1:T(8,128)(2,1)} fusion(bf16[256,128]{0,1:T(8,128)(2,1)} %bitcast.40, bf16[256,128]{0,1:T(8,128)(2,1)S(1)} %copy.120, bf16[256,128]{0,1:T(8,128)(2,1)S(1)} %copy.119), kind=kLoop, calls=%fused_computation.12 | loop fusion | flops 589824 | bytes 393216 | tf_op jit(solution)/shard_map/mlp_weight_gather/concatenate | solution.py:62
  10.8 0.0 all-gather.4.cloned.1.call-update
  10.8 0.8 convert_element_type.70
  11.5 0.9 multiply_reduce_fusion.1
  12.5 0.8 dynamic-slice
  13.2 0.2 fusion.33
  13.4 0.9 fusion.31
  14.3 1.0 fusion.35
  15.4 24.2 %all-gather = f32[128,768]{1,0:T(8,128)S(1)} all-gather(f32[8,768]{1,0:T(8,128)S(1)} %pad_maximum_fusion.2), channel_id=2, replica_groups=mesh['seq'=16,'mlp'=8,'tp'=4] {'seq'}, dimensions={0}, use_global_device_ids=true | all-gather | bytes 417792 | tf_op jit(solution)/shard_map/qkv_projection/all_gather | solution.py:32
  39.6 0.0 copy-start.5
  39.6 0.1 reshape.164
  39.7 0.1 broadcast_compare_fusion
  39.8 0.5 copy.105
  40.4 0.5 copy.108
  40.9 0.1 multiply_cosine_fusion
  41.0 0.1 subtract_convert_fusion
  41.1 0.4 select_reduce_fusion
  41.5 0.4 fusion.10
  41.9 0.2 fusion.9
  42.2 0.2 copy.110
  42.4 0.2 copy.109
  42.6 0.1 pad_maximum_fusion.1
  42.7 15.9 %all-gather.1 = f32[128,2,4,66]{3,2,1,0:T(4,128)S(1)} all-gather(f32[8,2,4,66]{3,2,1,0:T(4,128)S(1)} %pad_maximum_fusion.1), channel_id=3, replica_groups=mesh['seq'=16,'mlp'=8,'tp'=4] {'seq'}, dimensions={0}, use_global_device_ids=true | all-gather | bytes 287232 | tf_op jit(solution)/shard_map/softmax_merge/all_gather | solution.py:124
  58.6 0.1 copy.129
  58.7 0.1 reshape.167
  58.8 0.1 multiply_subtract_fusion
  58.9 0.1 fusion.29
  59.0 0.2 multiply_reduce_fusion.2
  59.2 0.1 copy.114
  59.3 0.3 fusion.30
  59.6 0.5 copy.117
  60.0 0.5 copy.126
  60.5 0.1 exponential_bitcast_fusion
  60.6 0.1 copy.115
  60.7 0.1 reshape.168
  60.8 0.2 fusion.17
  60.9 0.3 fusion.7
  61.3 0.1 divide_convert_fusion
  61.4 0.1 convert_element_type.79
  61.5 0.1 fusion.37
  61.7 10.5 %psum.7 = bf16[8,128]{1,0:T(8,128)(2,1)S(1)} all-reduce(f32[8,128]{1,0:T(8,128)S(1)} %fusion.37), channel_id=1, replica_groups=mesh['seq'=16,'mlp'=8,'tp'=4] {'tp'}, use_global_device_ids=true, to_apply=%region_8.9 | all-reduce | flops 1024 | bytes 6144 | tf_op jit(solution)/shard_map/output_projection/psum | solution.py:150
  72.1 15.9 %all_gather.22 = bf16[8,2048]{1,0:T(8,128)(2,1)S(1)} all-gather(bf16[8,128]{1,0:T(8,128)(2,1)S(1)} %psum.7), channel_id=1, replica_groups=mesh['seq'=16,'mlp'=8,'tp'=4] {'seq'}, dimensions={1}, use_global_device_ids=true | all-gather | bytes 34816 | tf_op jit(solution)/shard_map/output_projection/all_gather | solution.py:151
  88.0 0.1 multiply_reduce_fusion
  88.1 0.0 all-gather.4.cloned.1.call-done
  88.1 1.3 fusion.5
  89.5 1.8 %fusion.1 = f32[8,2048]{1,0:T(8,128)S(1)} fusion(bf16[2048,384]{0,1:T(8,128)(2,1)} %all-gather.4.cloned.1.call-done, f32[8,128]{1,0:T(8,128)S(1)} %fusion.5, f32[2048]{0:T(1024)S(1)} %convert_element_type.82, f32[8]{0:T(128)S(1)} %add_rsqrt_fusion, bf16[8,2048]{1,0:T(8,128)(2,1)S(1)} %all_gather.22, bf16[8,2048]{1,0:T(8,128)(2,1)S(1)} %copy-done.3), kind=kOutput, calls=%fused_computation.3 | convolution fusion | flops 8493056 | bytes 1191968 | tf_op jit(solution)/shard_map/feed_forward/dot_general | solution.py:158
  91.2 1.9 %collective-permute-start = (f32[8,2048]{1,0:T(8,128)S(1)}, f32[8,2048]{1,0:T(8,128)S(1)}, u32[]{:S(2)}, u32[]{:S(2)}) collective-permute-start(f32[8,2048]{1,0:T(8,128)S(1)} %fusion.1), channel_id=1, source_target_pairs={{0,1},{1,0},{2,3},{3,2},{4,5},{5,4},{6,7},{7,6},{8,9},{9,8},{10,11... | collective-permute-start | bytes 196616 | tf_op jit(solution)/shard_map/down_reduction/ppermute | solution.py:40
  93.2 4.3 %collective-permute-done = f32[8,2048]{1,0:T(8,128)S(1)} collective-permute-done((f32[8,2048]{1,0:T(8,128)S(1)}, f32[8,2048]{1,0:T(8,128)S(1)}, u32[]{:S(2)}, u32[]{:S(2)}) %collective-permute-start) | collective-permute-done | bytes 65568 | tf_op jit(solution)/shard_map/down_reduction/ppermute | solution.py:40
  97.5 2.8 %collective-permute-start.1 = (f32[8,2048]{1,0:T(8,128)S(1)}, f32[8,2048]{1,0:T(8,128)S(1)}, u32[]{:S(2)}, u32[]{:S(2)}) collective-permute-start(f32[8,2048]{1,0:T(8,128)S(1)} %add.88), channel_id=1, source_target_pairs={{0,2},{1,3},{2,0},{3,1},{4,6},{5,7},{6,4},{7,5},{8,10},{9,11},{10,... | collective-permute-start | bytes 196616 | tf_op jit(solution)/shard_map/down_reduction/ppermute | solution.py:40
  100.3 4.9 %collective-permute-done.1 = f32[8,2048]{1,0:T(8,128)S(1)} collective-permute-done((f32[8,2048]{1,0:T(8,128)S(1)}, f32[8,2048]{1,0:T(8,128)S(1)}, u32[]{:S(2)}, u32[]{:S(2)}) %collective-permute-start.1) | collective-permute-done | bytes 65568 | tf_op jit(solution)/shard_map/down_reduction/ppermute | solution.py:40
  105.2 1.9 %collective-permute-start.2 = (f32[8,2048]{1,0:T(8,128)S(1)}, f32[8,2048]{1,0:T(8,128)S(1)}, u32[]{:S(2)}, u32[]{:S(2)}) collective-permute-start(f32[8,2048]{1,0:T(8,128)S(1)} %add.89), channel_id=1, source_target_pairs={{0,32},{32,0},{64,96},{96,64},{128,160},{160,128},{192,224},{224,1... | collective-permute-start | bytes 196616 | tf_op jit(solution)/shard_map/down_reduction/ppermute | solution.py:40
  107.1 1.2 collective-permute-done.2
  108.3 2.3 %collective-permute-start.3 = (f32[8,2048]{1,0:T(8,128)S(1)}, f32[8,2048]{1,0:T(8,128)S(1)}, u32[]{:S(2)}, u32[]{:S(2)}) collective-permute-start(f32[8,2048]{1,0:T(8,128)S(1)} %add.90), channel_id=1, source_target_pairs={{0,64},{32,96},{64,0},{96,32},{128,192},{160,224},{192,128},{224,1... | collective-permute-start | bytes 196616 | tf_op jit(solution)/shard_map/down_reduction/ppermute | solution.py:40
  110.6 3.9 %collective-permute-done.3 = f32[8,2048]{1,0:T(8,128)S(1)} collective-permute-done((f32[8,2048]{1,0:T(8,128)S(1)}, f32[8,2048]{1,0:T(8,128)S(1)}, u32[]{:S(2)}, u32[]{:S(2)}) %collective-permute-start.3) | collective-permute-done | bytes 65568 | tf_op jit(solution)/shard_map/down_reduction/ppermute | solution.py:40
  114.5 2.2 %collective-permute-start.4 = (f32[8,2048]{1,0:T(8,128)S(1)}, f32[8,2048]{1,0:T(8,128)S(1)}, u32[]{:S(2)}, u32[]{:S(2)}) collective-permute-start(f32[8,2048]{1,0:T(8,128)S(1)} %add.91), channel_id=1, source_target_pairs={{0,128},{32,160},{64,192},{96,224},{128,0},{160,32},{192,64},{224,... | collective-permute-start | bytes 196616 | tf_op jit(solution)/shard_map/down_reduction/ppermute | solution.py:40
  116.7 5.4 %collective-permute-done.4 = f32[8,2048]{1,0:T(8,128)S(1)} collective-permute-done((f32[8,2048]{1,0:T(8,128)S(1)}, f32[8,2048]{1,0:T(8,128)S(1)}, u32[]{:S(2)}, u32[]{:S(2)}) %collective-permute-start.4) | collective-permute-done | bytes 65568 | tf_op jit(solution)/shard_map/down_reduction/ppermute | solution.py:40
  122.1 4.1 %collective-permute-start.5 = (f32[8,2048]{1,0:T(8,128)S(1)}, f32[8,2048]{1,0:T(8,128)S(1)}, u32[]{:S(2)}, u32[]{:S(2)}) collective-permute-start(f32[8,2048]{1,0:T(8,128)S(1)} %add.92), channel_id=1, source_target_pairs={{0,256},{32,288},{64,320},{96,352},{128,384},{160,416},{192,448},{... | collective-permute-start | bytes 196616 | tf_op jit(solution)/shard_map/down_reduction/ppermute | solution.py:40
  126.2 0.7 convert_element_type.88
  126.8 5.3 %collective-permute-done.5 = f32[8,2048]{1,0:T(8,128)S(1)} collective-permute-done((f32[8,2048]{1,0:T(8,128)S(1)}, f32[8,2048]{1,0:T(8,128)S(1)}, u32[]{:S(2)}, u32[]{:S(2)}) %collective-permute-start.5) | collective-permute-done | bytes 65568 | tf_op jit(solution)/shard_map/down_reduction/ppermute | solution.py:40
  132.1 0.6 add_convert_fusion
  (37 shorter events, 0.2 us)
Async XLA Ops:
  7.2 6.1 %copy-start = (bf16[128,512]{1,0:T(8,128)(2,1)S(1)}, bf16[128,512]{1,0:T(8,128)(2,1)}, u32[]{:S(2)}) copy-start(bf16[128,512]{1,0:T(8,128)(2,1)} %param.16) | copy-start | bytes 393220
  7.2 32.5 %copy-start.8 = (s32[8]{0:T(128)S(1)}, s32[8]{0:T(128)}, u32[]{:S(2)}) copy-start(s32[8]{0:T(128)} %param.14) | copy-start | bytes 100
  7.2 32.6 %copy-start.1 = (bf16[8,512,128]{2,1,0:T(8,128)(2,1)S(1)}, bf16[8,512,128]{2,1,0:T(8,128)(2,1)}, u32[]{:S(2)}) copy-start(bf16[8,512,128]{2,1,0:T(8,128)(2,1)} %param.19) | copy-start | bytes 3145732
  7.2 80.9 %all-gather.4.cloned.1.call-start = ((), (), s32[]{:S(2)}) async-start(), calls=%async_computation | async-start | bytes 1769472 | tf_op jit(solution)/shard_map/mlp_weight_gather/all_gather | solution.py:63
  14.3 26.0 %copy-start.2 = (bf16[8,512,128]{2,1,0:T(8,128)(2,1)S(1)}, bf16[8,512,128]{2,1,0:T(8,128)(2,1)}, u32[]{:S(2)}) copy-start(bf16[8,512,128]{2,1,0:T(8,128)(2,1)} %param.20) | copy-start | bytes 3145732
  39.6 2.5 %copy-start.5 = (f32[8,768]{1,0:T(8,128)}, f32[8,768]{1,0:T(8,128)S(1)}, u32[]{:S(2)}) copy-start(f32[8,768]{1,0:T(8,128)S(1)} %bitcast_reduce_fusion) | copy-start | bytes 73732
  42.2 18.5 %copy-start.6 = (bf16[8,128]{1,0:T(8,128)(2,1)}, bf16[8,128]{1,0:T(8,128)(2,1)S(1)}, u32[]{:S(2)}) copy-start(bf16[8,128]{1,0:T(8,128)(2,1)S(1)} %slice.86) | copy-start | bytes 6148
  42.2 16.5 %slice-start = ((f32[8,768]{1,0:T(8,128)}), f32[8,128]{1,0:T(8,128)S(1)}, s32[]{:S(2)}) async-start(f32[8,768]{1,0:T(8,128)} %copy-done.5), calls=%async_computation.1 | async-start | bytes 8192 | tf_op jit(solution)/shard_map/slice | solution.py:88
  59.5 2.0 %copy-start.7 = (bf16[2048]{0:T(1024)(128)(2,1)S(1)}, bf16[2048]{0:T(1024)(128)(2,1)}, u32[]{:S(2)}) copy-start(bf16[2048]{0:T(1024)(128)(2,1)} %param.22) | copy-start | bytes 12292
  59.5 2.0 %copy-start.4 = (bf16[512,128]{1,0:T(8,128)(2,1)S(1)}, bf16[512,128]{1,0:T(8,128)(2,1)}, u32[]{:S(2)}) copy-start(bf16[512,128]{1,0:T(8,128)(2,1)} %param.21) | copy-start | bytes 393220
  59.6 28.4 %copy-start.3 = (bf16[8,2048]{1,0:T(8,128)(2,1)S(1)}, bf16[8,2048]{1,0:T(8,128)(2,1)}, u32[]{:S(2)}) copy-start(bf16[8,2048]{1,0:T(8,128)(2,1)} %param.13) | copy-start | bytes 98308
  91.2 6.2 %collective-permute-start = (f32[8,2048]{1,0:T(8,128)S(1)}, f32[8,2048]{1,0:T(8,128)S(1)}, u32[]{:S(2)}, u32[]{:S(2)}) collective-permute-start(f32[8,2048]{1,0:T(8,128)S(1)} %fusion.1), channel_id=1, source_target_pairs={{0,1},{1,0},{2,3},{3,2},{4,5},{5,4},{6,7},{7,6},{8,9},{9,8},{10,11... | collective-permute-start | bytes 196616 | tf_op jit(solution)/shard_map/down_reduction/ppermute | solution.py:40
  97.5 7.7 %collective-permute-start.1 = (f32[8,2048]{1,0:T(8,128)S(1)}, f32[8,2048]{1,0:T(8,128)S(1)}, u32[]{:S(2)}, u32[]{:S(2)}) collective-permute-start(f32[8,2048]{1,0:T(8,128)S(1)} %add.88), channel_id=1, source_target_pairs={{0,2},{1,3},{2,0},{3,1},{4,6},{5,7},{6,4},{7,5},{8,10},{9,11},{10,... | collective-permute-start | bytes 196616 | tf_op jit(solution)/shard_map/down_reduction/ppermute | solution.py:40
  105.2 3.1 %collective-permute-start.2 = (f32[8,2048]{1,0:T(8,128)S(1)}, f32[8,2048]{1,0:T(8,128)S(1)}, u32[]{:S(2)}, u32[]{:S(2)}) collective-permute-start(f32[8,2048]{1,0:T(8,128)S(1)} %add.89), channel_id=1, source_target_pairs={{0,32},{32,0},{64,96},{96,64},{128,160},{160,128},{192,224},{224,1... | collective-permute-start | bytes 196616 | tf_op jit(solution)/shard_map/down_reduction/ppermute | solution.py:40
  108.3 6.2 %collective-permute-start.3 = (f32[8,2048]{1,0:T(8,128)S(1)}, f32[8,2048]{1,0:T(8,128)S(1)}, u32[]{:S(2)}, u32[]{:S(2)}) collective-permute-start(f32[8,2048]{1,0:T(8,128)S(1)} %add.90), channel_id=1, source_target_pairs={{0,64},{32,96},{64,0},{96,32},{128,192},{160,224},{192,128},{224,1... | collective-permute-start | bytes 196616 | tf_op jit(solution)/shard_map/down_reduction/ppermute | solution.py:40
  114.5 7.5 %collective-permute-start.4 = (f32[8,2048]{1,0:T(8,128)S(1)}, f32[8,2048]{1,0:T(8,128)S(1)}, u32[]{:S(2)}, u32[]{:S(2)}) collective-permute-start(f32[8,2048]{1,0:T(8,128)S(1)} %add.91), channel_id=1, source_target_pairs={{0,128},{32,160},{64,192},{96,224},{128,0},{160,32},{192,64},{224,... | collective-permute-start | bytes 196616 | tf_op jit(solution)/shard_map/down_reduction/ppermute | solution.py:40
  122.1 10.1 %collective-permute-start.5 = (f32[8,2048]{1,0:T(8,128)S(1)}, f32[8,2048]{1,0:T(8,128)S(1)}, u32[]{:S(2)}, u32[]{:S(2)}) collective-permute-start(f32[8,2048]{1,0:T(8,128)S(1)} %add.92), channel_id=1, source_target_pairs={{0,256},{32,288},{64,320},{96,352},{128,384},{160,416},{192,448},{... | collective-permute-start | bytes 196616 | tf_op jit(solution)/shard_map/down_reduction/ppermute | solution.py:40
Sparse Core Ops, SparseCore 0:
  10.9 49.3 all-gather.3

commit v2 on v1

--- a/solution.py
+++ b/solution.py
@@ -30,6 +30,23 @@
 
 def gathered_sum(x, axis):
     return jnp.sum(lax.all_gather(x, axis), axis=0)
+
+
+def gather_blocks(x, axis):
+    size = lax.axis_size(axis)
+    me = lax.axis_index(axis)
+    held = x[None]
+    step = 1
+    while step < size:
+        other = lax.ppermute(held, axis, [(i, i ^ step) for i in range(size)])
+        upper = (me // step) % 2 == 1
+        held = jnp.where(
+            upper,
+            jnp.concatenate([other, held], axis=0),
+            jnp.concatenate([held, other], axis=0),
+        )
+        step *= 2
+    return held
 
 
 def butterfly_sum(x, axis):
@@ -57,13 +74,16 @@
     up_weight,
     down_weight,
 ):
-    hidden_units = gate_weight.shape[1]
+    slab_rows, hidden_units = gate_weight.shape
     with jax.named_scope("mlp_weight_gather"):
-        slab = jnp.concatenate([gate_weight, up_weight, down_weight.T], axis=1)
-        full_slab = lax.all_gather(slab, "mlp", axis=0, tiled=True)
-    gate_full = full_slab[:, :hidden_units]
-    up_full = full_slab[:, hidden_units : 2 * hidden_units]
-    down_full = full_slab[:, 2 * hidden_units :].T
+        slab = jnp.stack(
+            [gate_weight, up_weight, down_weight.reshape(slab_rows, hidden_units)], axis=0
+        )
+        blocks = gather_blocks(slab, "mlp")
+    slabs = blocks.shape[0]
+    gate_full = blocks[:, 0].reshape(slabs * slab_rows, hidden_units)
+    up_full = blocks[:, 1].reshape(slabs * slab_rows, hidden_units)
+    down_blocks = blocks[:, 2].reshape(slabs, hidden_units, slab_rows)
 
     requests = hidden.shape[0]
     stream = hidden.astype(jnp.float32)
@@ -155,9 +175,11 @@
         gate = jnp.dot(mlp_input, gate_full, preferred_element_type=jnp.float32)
         upward = jnp.dot(mlp_input, up_full, preferred_element_type=jnp.float32)
         activated = (jax.nn.silu(gate) * upward).astype(jnp.bfloat16)
-        down_part = jnp.dot(activated, down_full, preferred_element_type=jnp.float32)
+        down_part = jnp.einsum(
+            "rh,jhc->rjc", activated, down_blocks, preferred_element_type=jnp.float32
+        ).reshape(requests, slabs * slab_rows)
     with jax.named_scope("down_reduction"):
-        down_total = butterfly_sum(butterfly_sum(down_part, "tp"), "seq").astype(jnp.bfloat16)
+        down_total = butterfly_sum(gathered_sum(down_part, "tp"), "seq").astype(jnp.bfloat16)
     updated_hidden = (mixed_stream + down_total.astype(jnp.float32)).astype(jnp.bfloat16)
     return (updated_hidden, new_keys, new_values)
 

time: 140 us -> 164 us (1.17)
  the two profiles are of different devices: /device:TPU:16 before, /device:TPU:1 now
where the time goes in v2:
time: 164 us; the launch traced here: 161 us
  blocking collectives  78.5 us (48%)
  waiting for transfers between devices  36.1 us (22%)
  starting transfers between devices  28.6 us (17%)
  other arithmetic  6.82 us (4%)
  local copies, waits for them, and re-layouts  6.29 us (4%)
  matrix products  3.79 us (2%)
    all_gather x2, blocking collectives, gathered_sum(): return jnp.sum(lax.all_gather(x, axis), axis=0)  35.1 us
    ppermute x3, waiting for transfers between devices, gather_blocks(): other = lax.ppermute(held, axis, [(i, i ^ step) for i in range(size)])  24.5 us
    all_gather x1, blocking collectives, per_device(): projected = lax.all_gather(projected, 'seq', axis=1, tiled=True)  18.4 us
    all_gather x1, blocking collectives, per_device(): every_state = lax.all_gather(state, 'seq')  15.9 us
    ppermute x3, starting transfers between devices, gather_blocks(): other = lax.ppermute(held, axis, [(i, i ^ step) for i in range(size)])  14.3 us
    ppermute x4, starting transfers between devices, butterfly_sum(): x = x + lax.ppermute(x, axis, pairs)  14.3 us
    ppermute x4, waiting for transfers between devices, butterfly_sum(): x = x + lax.ppermute(x, axis, pairs)  11.5 us
    psum x1, blocking collectives, per_device(): projected = lax.psum(partial_output, 'tp').astype(jnp.bfloat16)  9.04 us
  transfers between devices with their start and end apart: 7, of which 6 were waited for; matrix products, arithmetic and copies ran while one was open for 7% of the time, Pallas kernels for 0%

profile of v2, /device:TPU:1, one launch (start us, length us, event | category | flops | bytes accessed | tf_op | source)
XLA Modules:
  0.0 161.1 jit_solution(15652032731097320502)
XLA Ops:
  0.7 1.0 reshape.177
  1.6 0.9 maximum_bitcast_fusion
  2.5 4.0 %collective-permute-start = (bf16[1,3,256,128]{3,2,1,0:T(8,128)(2,1)S(1)}, bf16[1,3,256,128]{3,2,1,0:T(8,128)(2,1)}, u32[]{:S(2)}, u32[]{:S(2)}) collective-permute-start(bf16[1,3,256,128]{3,2,1,0:T(8,128)(2,1)S(1)} %maximum_bitcast_fusion), channel_id=1, source_target_pairs={{0,4},{4,0},{8,12},{12,8},{16,20},{20,16},{24,28},{28,24},{1,5},{5... | collective-permute-start | bytes 589832 | tf_op jit(solution)/shard_map/mlp_weight_gather/ppermute | solution.py:41
  6.6 0.8 convert_element_type.70
  7.3 0.9 multiply_reduce_fusion.1
  8.2 0.8 dynamic-slice
  9.0 0.2 fusion.26
  9.2 0.9 fusion.24
  10.1 1.0 fusion.28
  11.2 25.0 %all-gather = f32[128,768]{1,0:T(8,128)S(1)} all-gather(f32[8,768]{1,0:T(8,128)S(1)} %pad_maximum_fusion.1), channel_id=2, replica_groups=mesh['seq'=16,'mlp'=8,'tp'=4] {'seq'}, dimensions={0}, use_global_device_ids=true | all-gather | bytes 417792 | tf_op jit(solution)/shard_map/qkv_projection/all_gather | solution.py:32
  36.4 0.5 copy.107
  36.9 0.5 copy.110
  37.5 0.1 multiply_cosine_fusion
  37.6 0.1 subtract_convert_fusion
  37.7 0.4 select_reduce_fusion
  38.1 0.2 fusion.2
  38.3 0.4 fusion.3
  38.7 0.2 copy.112
  38.9 0.2 copy.111
  39.1 0.1 pad_maximum_fusion
  39.3 15.9 %all-gather.1 = f32[128,2,4,66]{3,2,1,0:T(4,128)S(1)} all-gather(f32[8,2,4,66]{3,2,1,0:T(4,128)S(1)} %pad_maximum_fusion), channel_id=3, replica_groups=mesh['seq'=16,'mlp'=8,'tp'=4] {'seq'}, dimensions={0}, use_global_device_ids=true | all-gather | bytes 287232 | tf_op jit(solution)/shard_map/softmax_merge/all_gather | solution.py:144
  55.2 0.1 copy.130
  55.3 0.3 fusion.23
  55.6 0.3 slice-done
  55.9 0.1 reshape.176
  55.9 0.1 multiply_subtract_fusion
  56.0 0.1 fusion.21
  56.1 0.2 multiply_reduce_fusion.2
  56.3 0.1 copy.116
  56.4 0.5 copy.119
  56.9 0.5 copy.127
  57.3 0.1 exponential_bitcast_fusion
  57.5 1.1 maximum_select_fusion.2
  58.6 4.2 %collective-permute-start.1 = (bf16[2,3,256,128]{3,2,1,0:T(8,128)(2,1)S(1)}, bf16[2,3,256,128]{3,2,1,0:T(8,128)(2,1)S(1)}, u32[]{:S(2)}, u32[]{:S(2)}) collective-permute-start(bf16[2,3,256,128]{3,2,1,0:T(8,128)(2,1)S(1)} %maximum_select_fusion.2), channel_id=1, source_target_pairs={{0,8},{4,12},{8,0},{12,4},{16,24},{20,28},{24,16},{28,20},{1,9},{5... | collective-permute-start | bytes 1179656 | tf_op jit(solution)/shard_map/mlp_weight_gather/ppermute | solution.py:41
  62.8 0.2 fusion.10
  63.1 0.1 reshape.178
  63.2 0.3 fusion
  63.6 17.2 %collective-permute-done.1 = bf16[2,3,256,128]{3,2,1,0:T(8,128)(2,1)S(1)} collective-permute-done((bf16[2,3,256,128]{3,2,1,0:T(8,128)(2,1)S(1)}, bf16[2,3,256,128]{3,2,1,0:T(8,128)(2,1)S(1)}, u32[]{:S(2)}, u32[]{:S(2)}) %collective-permute-start.1) | collective-permute-done | bytes 393248 | tf_op jit(solution)/shard_map/mlp_weight_gather/ppermute | solution.py:41
  80.8 0.1 maximum_select_fusion.1
  80.9 6.1 %collective-permute-start.2 = (bf16[4,3,256,128]{3,2,1,0:T(8,128)(2,1)S(1)}, bf16[4,3,256,128]{3,2,1,0:T(8,128)(2,1)S(1)}, u32[]{:S(2)}, u32[]{:S(2)}) collective-permute-start(bf16[4,3,256,128]{3,2,1,0:T(8,128)(2,1)S(1)} %maximum_select_fusion.1), channel_id=1, source_target_pairs={{0,16},{4,20},{8,24},{12,28},{16,0},{20,4},{24,8},{28,12},{1,17},{... | collective-permute-start | bytes 2359304 | tf_op jit(solution)/shard_map/mlp_weight_gather/ppermute | solution.py:41
  87.0 0.1 divide_convert_fusion
  87.1 0.1 convert_element_type.79
  87.2 0.1 fusion.30
  87.4 9.0 %psum.7 = bf16[8,128]{1,0:T(8,128)(2,1)S(1)} all-reduce(f32[8,128]{1,0:T(8,128)S(1)} %fusion.30), channel_id=1, replica_groups=mesh['seq'=16,'mlp'=8,'tp'=4] {'tp'}, use_global_device_ids=true, to_apply=%region_8.9 | all-reduce | flops 1024 | bytes 6144 | tf_op jit(solution)/shard_map/output_projection/psum | solution.py:170
  96.4 18.4 %all_gather.22 = bf16[8,2048]{1,0:T(8,128)(2,1)S(1)} all-gather(bf16[8,128]{1,0:T(8,128)(2,1)S(1)} %psum.7), channel_id=1, replica_groups=mesh['seq'=16,'mlp'=8,'tp'=4] {'seq'}, dimensions={1}, use_global_device_ids=true | all-gather | bytes 34816 | tf_op jit(solution)/shard_map/output_projection/all_gather | solution.py:171
  114.8 0.1 multiply_reduce_fusion
  115.0 7.4 %collective-permute-done.2 = bf16[4,3,256,128]{3,2,1,0:T(8,128)(2,1)S(1)} collective-permute-done((bf16[4,3,256,128]{3,2,1,0:T(8,128)(2,1)S(1)}, bf16[4,3,256,128]{3,2,1,0:T(8,128)(2,1)S(1)}, u32[]{:S(2)}, u32[]{:S(2)}) %collective-permute-start.2) | collective-permute-done | bytes 786464 | tf_op jit(solution)/shard_map/mlp_weight_gather/ppermute | solution.py:41
  122.3 0.2 maximum_select_fusion
  122.6 0.1 fusion.22
  122.7 0.2 reshape_squeeze.11
  122.9 0.3 copy.121
  123.1 0.2 fusion.19
  123.4 0.4 fusion.13
  123.8 10.1 %all-gather.2 = f32[32,2048]{1,0:T(8,128)S(1)} all-gather(f32[8,2048]{1,0:T(8,128)S(1)} %fusion.13), channel_id=4, replica_groups=mesh['seq'=16,'mlp'=8,'tp'=4] {'tp'}, dimensions={0}, use_global_device_ids=true | all-gather | bytes 327680 | tf_op jit(solution)/shard_map/down_reduction/all_gather | solution.py:32
  134.0 5.8 %collective-permute-start.3 = (f32[8,2048]{1,0:T(8,128)S(1)}, f32[8,2048]{1,0:T(8,128)S(1)}, u32[]{:S(2)}, u32[]{:S(2)}) collective-permute-start(f32[8,2048]{1,0:T(8,128)S(1)} %bitcast_reduce_fusion.1), channel_id=1, source_target_pairs={{0,32},{32,0},{64,96},{96,64},{128,160},{160,128},{192,224},{224,1... | collective-permute-start | bytes 196616 | tf_op jit(solution)/shard_map/down_reduction/ppermute | solution.py:57
  139.7 0.9 collective-permute-done.3
  140.6 3.3 %collective-permute-start.4 = (f32[8,2048]{1,0:T(8,128)S(1)}, f32[8,2048]{1,0:T(8,128)S(1)}, u32[]{:S(2)}, u32[]{:S(2)}) collective-permute-start(f32[8,2048]{1,0:T(8,128)S(1)} %add.98), channel_id=1, source_target_pairs={{0,64},{32,96},{64,0},{96,32},{128,192},{160,224},{192,128},{224,1... | collective-permute-start | bytes 196616 | tf_op jit(solution)/shard_map/down_reduction/ppermute | solution.py:57
  143.9 1.7 %collective-permute-done.4 = f32[8,2048]{1,0:T(8,128)S(1)} collective-permute-done((f32[8,2048]{1,0:T(8,128)S(1)}, f32[8,2048]{1,0:T(8,128)S(1)}, u32[]{:S(2)}, u32[]{:S(2)}) %collective-permute-start.4) | collective-permute-done | bytes 65568 | tf_op jit(solution)/shard_map/down_reduction/ppermute | solution.py:57
  145.7 1.9 %collective-permute-start.5 = (f32[8,2048]{1,0:T(8,128)S(1)}, f32[8,2048]{1,0:T(8,128)S(1)}, u32[]{:S(2)}, u32[]{:S(2)}) collective-permute-start(f32[8,2048]{1,0:T(8,128)S(1)} %add.99), channel_id=1, source_target_pairs={{0,128},{32,160},{64,192},{96,224},{128,0},{160,32},{192,64},{224,... | collective-permute-start | bytes 196616 | tf_op jit(solution)/shard_map/down_reduction/ppermute | solution.py:57
  147.6 4.0 %collective-permute-done.5 = f32[8,2048]{1,0:T(8,128)S(1)} collective-permute-done((f32[8,2048]{1,0:T(8,128)S(1)}, f32[8,2048]{1,0:T(8,128)S(1)}, u32[]{:S(2)}, u32[]{:S(2)}) %collective-permute-start.5) | collective-permute-done | bytes 65568 | tf_op jit(solution)/shard_map/down_reduction/ppermute | solution.py:57
  151.6 3.3 %collective-permute-start.6 = (f32[8,2048]{1,0:T(8,128)S(1)}, f32[8,2048]{1,0:T(8,128)S(1)}, u32[]{:S(2)}, u32[]{:S(2)}) collective-permute-start(f32[8,2048]{1,0:T(8,128)S(1)} %add.100), channel_id=1, source_target_pairs={{0,256},{32,288},{64,320},{96,352},{128,384},{160,416},{192,448},{... | collective-permute-start | bytes 196616 | tf_op jit(solution)/shard_map/down_reduction/ppermute | solution.py:57
  154.9 0.7 convert_element_type.88
  155.5 5.0 %collective-permute-done.6 = f32[8,2048]{1,0:T(8,128)S(1)} collective-permute-done((f32[8,2048]{1,0:T(8,128)S(1)}, f32[8,2048]{1,0:T(8,128)S(1)}, u32[]{:S(2)}, u32[]{:S(2)}) %collective-permute-start.6) | collective-permute-done | bytes 65568 | tf_op jit(solution)/shard_map/down_reduction/ppermute | solution.py:57
  160.5 0.6 add_convert_fusion
  (43 shorter events, 0.4 us)
Async XLA Ops:
  0.6 8.4 %copy-start = (bf16[128,512]{1,0:T(8,128)(2,1)S(1)}, bf16[128,512]{1,0:T(8,128)(2,1)}, u32[]{:S(2)}) copy-start(bf16[128,512]{1,0:T(8,128)(2,1)} %param.16) | copy-start | bytes 393220
  0.6 35.7 %copy-start.9 = (s32[8]{0:T(128)S(1)}, s32[8]{0:T(128)}, u32[]{:S(2)}) copy-start(s32[8]{0:T(128)} %param.14) | copy-start | bytes 100
  0.7 35.7 %copy-start.2 = (bf16[8,512,128]{2,1,0:T(8,128)(2,1)S(1)}, bf16[8,512,128]{2,1,0:T(8,128)(2,1)}, u32[]{:S(2)}) copy-start(bf16[8,512,128]{2,1,0:T(8,128)(2,1)} %param.19) | copy-start | bytes 3145732
  2.5 54.9 %collective-permute-start = (bf16[1,3,256,128]{3,2,1,0:T(8,128)(2,1)S(1)}, bf16[1,3,256,128]{3,2,1,0:T(8,128)(2,1)}, u32[]{:S(2)}, u32[]{:S(2)}) collective-permute-start(bf16[1,3,256,128]{3,2,1,0:T(8,128)(2,1)S(1)} %maximum_bitcast_fusion), channel_id=1, source_target_pairs={{0,4},{4,0},{8,12},{12,8},{16,20},{20,16},{24,28},{28,24},{1,5},{5... | collective-permute-start | bytes 589832 | tf_op jit(solution)/shard_map/mlp_weight_gather/ppermute | solution.py:41
  10.1 26.8 %copy-start.3 = (bf16[8,512,128]{2,1,0:T(8,128)(2,1)S(1)}, bf16[8,512,128]{2,1,0:T(8,128)(2,1)}, u32[]{:S(2)}) copy-start(bf16[8,512,128]{2,1,0:T(8,128)(2,1)} %param.20) | copy-start | bytes 3145732
  36.2 1.3 copy-start.5
  55.2 0.7 slice-start
  55.9 7.1 %copy-start.6 = (f32[8,768]{1,0:T(8,128)S(1)}, f32[8,768]{1,0:T(8,128)}, u32[]{:S(2)}) copy-start(f32[8,768]{1,0:T(8,128)} %copy-done.5) | copy-start | bytes 73732
  57.4 29.8 %copy-start.8 = (bf16[2048]{0:T(1024)(128)(2,1)S(1)}, bf16[2048]{0:T(1024)(128)(2,1)}, u32[]{:S(2)}) copy-start(bf16[2048]{0:T(1024)(128)(2,1)} %param.22) | copy-start | bytes 12292
  57.4 29.8 %copy-start.4 = (bf16[512,128]{1,0:T(8,128)(2,1)S(1)}, bf16[512,128]{1,0:T(8,128)(2,1)}, u32[]{:S(2)}) copy-start(bf16[512,128]{1,0:T(8,128)(2,1)} %param.21) | copy-start | bytes 393220
  58.6 56.2 %copy-start.1 = (bf16[8,2048]{1,0:T(8,128)(2,1)S(1)}, bf16[8,2048]{1,0:T(8,128)(2,1)}, u32[]{:S(2)}) copy-start(bf16[8,2048]{1,0:T(8,128)(2,1)} %param.13) | copy-start | bytes 98308
  58.6 22.2 %collective-permute-start.1 = (bf16[2,3,256,128]{3,2,1,0:T(8,128)(2,1)S(1)}, bf16[2,3,256,128]{3,2,1,0:T(8,128)(2,1)S(1)}, u32[]{:S(2)}, u32[]{:S(2)}) collective-permute-start(bf16[2,3,256,128]{3,2,1,0:T(8,128)(2,1)S(1)} %maximum_select_fusion.2), channel_id=1, source_target_pairs={{0,8},{4,12},{8,0},{12,4},{16,24},{20,28},{24,16},{28,20},{1,9},{5... | collective-permute-start | bytes 1179656 | tf_op jit(solution)/shard_map/mlp_weight_gather/ppermute | solution.py:41
  63.0 59.6 %copy-start.7 = (bf16[8,128]{1,0:T(8,128)(2,1)}, bf16[8,128]{1,0:T(8,128)(2,1)S(1)}, u32[]{:S(2)}) copy-start(bf16[8,128]{1,0:T(8,128)(2,1)S(1)} %slice.79) | copy-start | bytes 6148
  80.9 41.4 %collective-permute-start.2 = (bf16[4,3,256,128]{3,2,1,0:T(8,128)(2,1)S(1)}, bf16[4,3,256,128]{3,2,1,0:T(8,128)(2,1)S(1)}, u32[]{:S(2)}, u32[]{:S(2)}) collective-permute-start(bf16[4,3,256,128]{3,2,1,0:T(8,128)(2,1)S(1)} %maximum_select_fusion.1), channel_id=1, source_target_pairs={{0,16},{4,20},{8,24},{12,28},{16,0},{20,4},{24,8},{28,12},{1,17},{... | collective-permute-start | bytes 2359304 | tf_op jit(solution)/shard_map/mlp_weight_gather/ppermute | solution.py:41
  134.0 6.6 %collective-permute-start.3 = (f32[8,2048]{1,0:T(8,128)S(1)}, f32[8,2048]{1,0:T(8,128)S(1)}, u32[]{:S(2)}, u32[]{:S(2)}) collective-permute-start(f32[8,2048]{1,0:T(8,128)S(1)} %bitcast_reduce_fusion.1), channel_id=1, source_target_pairs={{0,32},{32,0},{64,96},{96,64},{128,160},{160,128},{192,224},{224,1... | collective-permute-start | bytes 196616 | tf_op jit(solution)/shard_map/down_reduction/ppermute | solution.py:57
  140.6 5.0 %collective-permute-start.4 = (f32[8,2048]{1,0:T(8,128)S(1)}, f32[8,2048]{1,0:T(8,128)S(1)}, u32[]{:S(2)}, u32[]{:S(2)}) collective-permute-start(f32[8,2048]{1,0:T(8,128)S(1)} %add.98), channel_id=1, source_target_pairs={{0,64},{32,96},{64,0},{96,32},{128,192},{160,224},{192,128},{224,1... | collective-permute-start | bytes 196616 | tf_op jit(solution)/shard_map/down_reduction/ppermute | solution.py:57
  145.7 5.9 %collective-permute-start.5 = (f32[8,2048]{1,0:T(8,128)S(1)}, f32[8,2048]{1,0:T(8,128)S(1)}, u32[]{:S(2)}, u32[]{:S(2)}) collective-permute-start(f32[8,2048]{1,0:T(8,128)S(1)} %add.99), channel_id=1, source_target_pairs={{0,128},{32,160},{64,192},{96,224},{128,0},{160,32},{192,64},{224,... | collective-permute-start | bytes 196616 | tf_op jit(solution)/shard_map/down_reduction/ppermute | solution.py:57
  151.6 8.9 %collective-permute-start.6 = (f32[8,2048]{1,0:T(8,128)S(1)}, f32[8,2048]{1,0:T(8,128)S(1)}, u32[]{:S(2)}, u32[]{:S(2)}) collective-permute-start(f32[8,2048]{1,0:T(8,128)S(1)} %add.100), channel_id=1, source_target_pairs={{0,256},{32,288},{64,320},{96,352},{128,384},{160,416},{192,448},{... | collective-permute-start | bytes 196616 | tf_op jit(solution)/shard_map/down_reduction/ppermute | solution.py:57

commit v3 on v2

--- a/solution.py
+++ b/solution.py
@@ -32,31 +32,12 @@
     return jnp.sum(lax.all_gather(x, axis), axis=0)
 
 
-def gather_blocks(x, axis):
-    size = lax.axis_size(axis)
-    me = lax.axis_index(axis)
-    held = x[None]
-    step = 1
-    while step < size:
-        other = lax.ppermute(held, axis, [(i, i ^ step) for i in range(size)])
-        upper = (me // step) % 2 == 1
-        held = jnp.where(
-            upper,
-            jnp.concatenate([other, held], axis=0),
-            jnp.concatenate([held, other], axis=0),
-        )
-        step *= 2
-    return held
-
-
-def butterfly_sum(x, axis):
-    size = lax.axis_size(axis)
-    step = 1
-    while step < size:
-        pairs = [(i, i ^ step) for i in range(size)]
-        x = x + lax.ppermute(x, axis, pairs)
-        step *= 2
-    return x
+def gather_by_exchange(x, axes):
+    count = 1
+    for axis in axes:
+        count *= lax.axis_size(axis)
+    copies = jnp.broadcast_to(x[None], (count,) + x.shape)
+    return lax.all_to_all(copies, axes, 0, 0, tiled=True)
 
 
 def per_device(
@@ -79,7 +60,7 @@
         slab = jnp.stack(
             [gate_weight, up_weight, down_weight.reshape(slab_rows, hidden_units)], axis=0
         )
-        blocks = gather_blocks(slab, "mlp")
+        blocks = lax.all_gather(slab, "mlp")
     slabs = blocks.shape[0]
     gate_full = blocks[:, 0].reshape(slabs * slab_rows, hidden_units)
     up_full = blocks[:, 1].reshape(slabs * slab_rows, hidden_units)
@@ -167,8 +148,16 @@
         )
     with jax.named_scope("output_projection"):
         partial_output = jnp.dot(attended, output_weight, preferred_element_type=jnp.float32)
-        projected = lax.psum(partial_output, "tp").astype(jnp.bfloat16)
-        projected = lax.all_gather(projected, "seq", axis=1, tiled=True)
+        every_partial = gather_by_exchange(partial_output.astype(jnp.bfloat16), ("seq", "tp"))
+        column_blocks = lax.axis_size("seq")
+        projected = (
+            every_partial.reshape(column_blocks, lax.axis_size("tp"), requests, -1)
+            .astype(jnp.float32)
+            .sum(axis=1)
+            .astype(jnp.bfloat16)
+            .transpose(1, 0, 2)
+            .reshape(requests, -1)
+        )
     mixed_stream = stream + projected.astype(jnp.float32)
     mlp_input = rms_norm(mixed_stream, feedforward_gain).astype(jnp.bfloat16)
     with jax.named_scope("feed_forward"):
@@ -179,7 +168,11 @@
             "rh,jhc->rjc", activated, down_blocks, preferred_element_type=jnp.float32
         ).reshape(requests, slabs * slab_rows)
     with jax.named_scope("down_reduction"):
-        down_total = butterfly_sum(gathered_sum(down_part, "tp"), "seq").astype(jnp.bfloat16)
+        reducers = lax.axis_size("seq") * lax.axis_size("tp")
+        pieces = down_part.reshape(requests, reducers, -1).transpose(1, 0, 2)
+        own_piece = lax.all_to_all(pieces, ("seq", "tp"), 0, 0, tiled=True).sum(axis=0)
+        every_piece = gather_by_exchange(own_piece.astype(jnp.bfloat16), ("seq", "tp"))
+        down_total = every_piece.transpose(1, 0, 2).reshape(requests, -1)
     updated_hidden = (mixed_stream + down_total.astype(jnp.float32)).astype(jnp.bfloat16)
     return (updated_hidden, new_keys, new_values)
 

time: 164 us -> 122 us (0.74); the launches traced: 161 us -> 121 us
  blocking collectives: 78.5 us -> 55.9 us
  waiting for transfers between devices: 36.1 us -> 18.6 us
  starting transfers between devices: 28.6 us -> 11.5 us
  between operations: 1.05 us -> 14.4 us
  local copies, waits for them, and re-layouts: 6.29 us -> 10.1 us
    ppermute x7 -> x0, waiting for transfers between devices: 36.1 us -> none  [the longest x3 24.5 us: gather_blocks(): other = lax.ppermute(held, axis, [(i, i ^ step) for i in range(size)])]
    ppermute x7 -> x0, starting transfers between devices: 28.6 us -> none  [the longest x3 14.3 us: gather_blocks(): other = lax.ppermute(held, axis, [(i, i ^ step) for i in range(size)])]
    all_to_all x0 -> x2, waiting for transfers between devices: none -> 18.6 us  [gather_by_exchange(): return lax.all_to_all(copies, axes, 0, 0, tiled=True)]
    all_gather x1 -> x0, blocking collectives: 18.4 us -> none  [per_device(): projected = lax.all_gather(projected, 'seq', axis=1, tiled=True)]
    all_to_all x0 -> x1, blocking collectives: none -> 14.5 us  [per_device(): lax.all_to_all(pieces, ('seq', 'tp'), 0, 0, tiled=True).sum(axis=0)]
    all_to_all x0 -> x2, starting transfers between devices: none -> 11.5 us  [gather_by_exchange(): return lax.all_to_all(copies, axes, 0, 0, tiled=True)]
    all_gather x2 -> x1, blocking collectives: 35.1 us -> 25.5 us  [gathered_sum(): return jnp.sum(lax.all_gather(x, axis), axis=0)]
    psum x1 -> x0, blocking collectives: 9.04 us -> none  [per_device(): projected = lax.psum(partial_output, 'tp').astype(jnp.bfloat16)]
  transfers between devices with their start and end apart: 7 -> 3, of which waited for: 6 -> 2; matrix products, arithmetic and copies ran while one was open for 7% -> 10% of each run, Pallas kernels for 0% -> 0%
where the time goes in v3:
time: 122 us; the launch traced here: 121 us
  blocking collectives  55.9 us (46%)
  waiting for transfers between devices  18.6 us (15%)
  between operations  14.4 us (12%)
  starting transfers between devices  11.5 us (9%)
  local copies, waits for them, and re-layouts  10.1 us (8%)
  other arithmetic  6.87 us (6%)
  matrix products  4.02 us (3%)
    all_gather x1, blocking collectives, gathered_sum(): return jnp.sum(lax.all_gather(x, axis), axis=0)  25.5 us
    all_to_all x2, waiting for transfers between devices, gather_by_exchange(): return lax.all_to_all(copies, axes, 0, 0, tiled=True)  18.6 us
    all_gather x1, blocking collectives, per_device(): every_state = lax.all_gather(state, 'seq')  15.9 us
    all_to_all x1, blocking collectives, per_device(): lax.all_to_all(pieces, ('seq', 'tp'), 0, 0, tiled=True).sum(axis=0)  14.5 us
    all_to_all x2, starting transfers between devices, gather_by_exchange(): return lax.all_to_all(copies, axes, 0, 0, tiled=True)  11.5 us
    unnamed x25, local copies, waits for them, and re-layouts  2.69 us
  transfers between devices with their start and end apart: 3, of which 2 were waited for; matrix products, arithmetic and copies ran while one was open for 10% of the time, Pallas kernels for 0%

profile of v3, /device:TPU:1, one launch (start us, length us, event | category | flops | bytes accessed | tf_op | source)
XLA Modules:
  0.0 121.4 jit_solution(12726739449365617617)
XLA Ops:
  7.2 0.0 all-gather.5.cloned.1.call-start
  7.2 1.0 reshape.187
  8.2 1.6 %pad_maximum_fusion = bf16[3,256,128]{2,1,0:T(8,128)(2,1)} fusion(bf16[1,256,128]{2,1,0:T(8,128)(2,1)S(1)} %reshape.187, bf16[1,256,128]{2,1,0:T(8,128)(2,1)} %bitcast.82, bf16[1,256,128]{2,1,0:T(8,128)(2,1)} %bitcast.83), kind=kLoop, calls=%fused_computation.13 | loop fusion | flops 196608 | bytes 393216 | tf_op jit(solution)/shard_map/mlp_weight_gather/stack | solution.py:60
  9.8 0.8 convert_element_type.88
  10.6 0.9 multiply_reduce_fusion.1
  11.5 0.8 dynamic-slice
  12.2 0.2 fusion.31
  12.4 0.9 fusion.29
  13.4 1.0 fusion.33
  14.4 25.5 %all-gather = f32[128,768]{1,0:T(8,128)S(1)} all-gather(f32[8,768]{1,0:T(8,128)S(1)} %pad_maximum_fusion.2), channel_id=2, replica_groups=mesh['seq'=16,'mlp'=8,'tp'=4] {'seq'}, dimensions={0}, use_global_device_ids=true | all-gather | bytes 417792 | tf_op jit(solution)/shard_map/qkv_projection/all_gather | solution.py:32
  40.0 0.1 reshape.182
  40.1 0.1 broadcast_compare_fusion
  40.2 0.5 copy.161
  40.7 0.5 copy.164
  41.3 0.1 multiply_cosine_fusion
  41.4 0.1 subtract_convert_fusion
  41.5 0.4 select_reduce_fusion
  41.9 0.2 fusion.5
  42.1 0.4 fusion.6
  42.5 0.2 copy.166
  42.7 0.2 copy.165
  42.9 0.1 pad_maximum_fusion.1
  43.1 15.9 %all-gather.1 = f32[128,2,4,66]{3,2,1,0:T(4,128)S(1)} all-gather(f32[8,2,4,66]{3,2,1,0:T(4,128)S(1)} %pad_maximum_fusion.1), channel_id=3, replica_groups=mesh['seq'=16,'mlp'=8,'tp'=4] {'seq'}, dimensions={0}, use_global_device_ids=true | all-gather | bytes 287232 | tf_op jit(solution)/shard_map/softmax_merge/all_gather | solution.py:125
  59.0 0.1 copy.194
  59.1 0.1 reshape.185
  59.2 0.1 multiply_subtract_fusion
  59.3 0.1 fusion.26
  59.3 0.2 multiply_reduce_fusion.2
  59.5 0.1 copy.170
  59.6 0.3 fusion.28
  59.9 0.5 copy.173
  60.4 0.5 copy.188
  60.8 0.1 exponential_bitcast_fusion
  60.9 0.1 copy.171
  61.0 0.1 reshape.188
  61.1 0.2 fusion.13
  61.3 0.3 fusion.2
  61.7 0.1 divide_convert_fusion
  61.8 0.1 convert_element_type.97
  61.9 0.1 convolution_convert_fusion
  62.0 0.7 broadcast_in_dim.31
  62.7 6.1 %all-to-all-start = ((bf16[64,8,128]{2,1,0:T(8,128)(2,1)}), bf16[64,8,128]{2,1,0:T(8,128)(2,1)S(1)}, u32[]{:S(2)}, u32[]{:S(2)}) async-start(bf16[64,8,128]{2,1,0:T(8,128)(2,1)} %broadcast_in_dim.31), calls=%async_computation | async-start | bytes 262144 | tf_op jit(solution)/shard_map/output_projection/all_to_all | solution.py:40
  68.8 10.0 %all-to-all-done = bf16[64,8,128]{2,1,0:T(8,128)(2,1)S(1)} async-done(((bf16[64,8,128]{2,1,0:T(8,128)(2,1)}), bf16[64,8,128]{2,1,0:T(8,128)(2,1)S(1)}, u32[]{:S(2)}, u32[]{:S(2)}) %all-to-all-start) | async-done | bytes 131104 | tf_op jit(solution)/shard_map/output_projection/all_to_all | solution.py:40
  78.9 0.1 multiply_reduce_fusion
  79.1 1.5 %fusion.27 = (bf16[8,1,256,128]{3,2,1,0:T(8,128)(2,1)S(1)}, bf16[8,1,256,128]{3,2,0,1:T(8,128)(2,1)S(1)}, bf16[8,1,256,128]{3,2,1,0:T(8,128)(2,1)S(1)}) fusion(bf16[8,3,256,128]{3,2,1,0:T(8,128)(2,1)} %bitcast.75), kind=kLoop, calls=%fused_computation.68 | loop fusion | bytes 3145728 | tf_op jit(solution)/shard_map/slice | solution.py:65
  80.5 0.2 reshape_squeeze.11
  80.7 0.3 copy.176
  81.0 0.2 fusion.24
  81.2 0.7 convolution_bitcast_fusion
  81.9 0.2 copy.178
  82.1 0.2 reshape.195
  82.3 14.5 %all_to_all.15 = f32[64,1,256]{2,1,0:T(1,128)S(1)} all-to-all(f32[64,1,256]{2,1,0:T(1,128)S(1)} %reshape.195), channel_id=1, replica_groups=mesh['seq'=16,'mlp'=8,'tp'=4] {'seq','tp'}, dimensions={0} | all-to-all | bytes 131072 | tf_op jit(solution)/shard_map/down_reduction/all_to_all | solution.py:173
  96.7 0.5 broadcast.121
  97.3 0.8 reduce.2
  98.1 0.1 reshape.196
  98.2 0.1 reduce_sum.92
  98.3 0.7 reshape.197
  99.0 5.3 %all-to-all-start.2 = ((bf16[64,2,128]{2,1,0:T(2,128)(2,1)}), bf16[64,2,128]{2,1,0:T(2,128)(2,1)S(1)}, u32[]{:S(2)}, u32[]{:S(2)}) async-start(bf16[64,2,128]{2,1,0:T(2,128)(2,1)} %reshape.197), calls=%async_computation.2 | async-start | bytes 65536 | tf_op jit(solution)/shard_map/down_reduction/all_to_all | solution.py:40
  104.4 0.7 convert_element_type.110
  105.0 8.6 %all-to-all-done.2 = bf16[64,2,128]{2,1,0:T(2,128)(2,1)S(1)} async-done(((bf16[64,2,128]{2,1,0:T(2,128)(2,1)}), bf16[64,2,128]{2,1,0:T(2,128)(2,1)S(1)}, u32[]{:S(2)}, u32[]{:S(2)}) %all-to-all-start.2) | async-done | bytes 32800 | tf_op jit(solution)/shard_map/down_reduction/all_to_all | solution.py:40
  113.6 0.1 reshape.198
  113.7 0.1 copy.181
  113.8 0.1 reshape.190
  113.9 0.6 add_convert_fusion
  (39 shorter events, 0.3 us)
Async XLA Ops:
  7.2 5.1 %copy-start = (bf16[128,512]{1,0:T(8,128)(2,1)S(1)}, bf16[128,512]{1,0:T(8,128)(2,1)}, u32[]{:S(2)}) copy-start(bf16[128,512]{1,0:T(8,128)(2,1)} %param.16) | copy-start | bytes 393220
  7.2 32.9 %copy-start.8 = (s32[8]{0:T(128)S(1)}, s32[8]{0:T(128)}, u32[]{:S(2)}) copy-start(s32[8]{0:T(128)} %param.14) | copy-start | bytes 100
  7.2 33.0 %copy-start.2 = (bf16[8,512,128]{2,1,0:T(8,128)(2,1)S(1)}, bf16[8,512,128]{2,1,0:T(8,128)(2,1)}, u32[]{:S(2)}) copy-start(bf16[8,512,128]{2,1,0:T(8,128)(2,1)} %param.19) | copy-start | bytes 3145732
  7.2 71.8 %all-gather.5.cloned.1.call-start = ((), (), s32[]{:S(2)}) async-start(), calls=%async_computation.3 | async-start | bytes 1769472 | tf_op jit(solution)/shard_map/mlp_weight_gather/all_gather | solution.py:63
  13.4 27.4 %copy-start.3 = (bf16[8,512,128]{2,1,0:T(8,128)(2,1)S(1)}, bf16[8,512,128]{2,1,0:T(8,128)(2,1)}, u32[]{:S(2)}) copy-start(bf16[8,512,128]{2,1,0:T(8,128)(2,1)} %param.20) | copy-start | bytes 3145732
  40.0 1.3 %copy-start.5 = (f32[8,768]{1,0:T(8,128)}, f32[8,768]{1,0:T(8,128)S(1)}, u32[]{:S(2)}) copy-start(f32[8,768]{1,0:T(8,128)S(1)} %bitcast_reduce_fusion) | copy-start | bytes 73732
  40.0 21.0 %copy-start.6 = (bf16[8,128]{1,0:T(8,128)(2,1)}, bf16[8,128]{1,0:T(8,128)(2,1)S(1)}, u32[]{:S(2)}) copy-start(bf16[8,128]{1,0:T(8,128)(2,1)S(1)} %slice.80) | copy-start | bytes 6148
  42.1 17.0 %slice-start = ((f32[8,768]{1,0:T(8,128)}), f32[8,128]{1,0:T(8,128)S(1)}, s32[]{:S(2)}) async-start(f32[8,768]{1,0:T(8,128)} %copy-done.5), calls=%async_computation.4 | async-start | bytes 8192 | tf_op jit(solution)/shard_map/slice | solution.py:89
  59.9 2.0 %copy-start.4 = (bf16[512,128]{1,0:T(8,128)(2,1)S(1)}, bf16[512,128]{1,0:T(8,128)(2,1)}, u32[]{:S(2)}) copy-start(bf16[512,128]{1,0:T(8,128)(2,1)} %param.21) | copy-start | bytes 393220
  59.9 8.9 %copy-start.7 = (bf16[2048]{0:T(1024)(128)(2,1)S(1)}, bf16[2048]{0:T(1024)(128)(2,1)}, u32[]{:S(2)}) copy-start(bf16[2048]{0:T(1024)(128)(2,1)} %param.22) | copy-start | bytes 12292
  59.9 19.0 %copy-start.1 = (bf16[8,2048]{1,0:T(8,128)(2,1)S(1)}, bf16[8,2048]{1,0:T(8,128)(2,1)}, u32[]{:S(2)}) copy-start(bf16[8,2048]{1,0:T(8,128)(2,1)} %param.13) | copy-start | bytes 98308
  62.7 16.2 %all-to-all-start = ((bf16[64,8,128]{2,1,0:T(8,128)(2,1)}), bf16[64,8,128]{2,1,0:T(8,128)(2,1)S(1)}, u32[]{:S(2)}, u32[]{:S(2)}) async-start(bf16[64,8,128]{2,1,0:T(8,128)(2,1)} %broadcast_in_dim.31), calls=%async_computation | async-start | bytes 262144 | tf_op jit(solution)/shard_map/output_projection/all_to_all | solution.py:40
  99.0 14.6 %all-to-all-start.2 = ((bf16[64,2,128]{2,1,0:T(2,128)(2,1)}), bf16[64,2,128]{2,1,0:T(2,128)(2,1)S(1)}, u32[]{:S(2)}, u32[]{:S(2)}) async-start(bf16[64,2,128]{2,1,0:T(2,128)(2,1)} %reshape.197), calls=%async_computation.2 | async-start | bytes 65536 | tf_op jit(solution)/shard_map/down_reduction/all_to_all | solution.py:40
Sparse Core Ops, SparseCore 0:
  10.1 43.2 all-gather.4

commit v4 on v3

--- a/solution.py
+++ b/solution.py
@@ -57,14 +57,14 @@
 ):
     slab_rows, hidden_units = gate_weight.shape
     with jax.named_scope("mlp_weight_gather"):
-        slab = jnp.stack(
-            [gate_weight, up_weight, down_weight.reshape(slab_rows, hidden_units)], axis=0
+        slab = jnp.concatenate(
+            [jnp.concatenate([gate_weight, up_weight], axis=1), down_weight], axis=0
         )
         blocks = lax.all_gather(slab, "mlp")
     slabs = blocks.shape[0]
-    gate_full = blocks[:, 0].reshape(slabs * slab_rows, hidden_units)
-    up_full = blocks[:, 1].reshape(slabs * slab_rows, hidden_units)
-    down_blocks = blocks[:, 2].reshape(slabs, hidden_units, slab_rows)
+    gate_full = blocks[:, :slab_rows, :hidden_units].reshape(slabs * slab_rows, hidden_units)
+    up_full = blocks[:, :slab_rows, hidden_units:].reshape(slabs * slab_rows, hidden_units)
+    down_blocks = blocks[:, slab_rows:, :]
 
     requests = hidden.shape[0]
     stream = hidden.astype(jnp.float32)

time: 122 us -> 121 us (level)
  local copies, waits for them, and re-layouts: 10.1 us -> 8.58 us
    concatenate x0 -> x1, other arithmetic: none -> 1.68 us  [per_device(): jnp.concatenate([jnp.concatenate([gate_weight, up_weight], axis=1), down_...]
    another operation x2 -> x1, other arithmetic: 1.65 us -> 0.09 us  [the longest x1 1.57 us: per_device(): jnp.stack([gate_weight, up_weight, down_weight.reshape(slab_rows, hidden_...]
where the time goes in v4:
time: 121 us
  blocking collectives  55.9 us (46%)
  waiting for transfers between devices  18.6 us (15%)
  between operations  14.4 us (12%)
  starting transfers between devices  11.5 us (10%)
  local copies, waits for them, and re-layouts  8.58 us (7%)
  other arithmetic  6.99 us (6%)
  matrix products  4.69 us (4%)
    all_gather x1, blocking collectives, gathered_sum(): return jnp.sum(lax.all_gather(x, axis), axis=0)  25.5 us
    all_to_all x2, waiting for transfers between devices, gather_by_exchange(): return lax.all_to_all(copies, axes, 0, 0, tiled=True)  18.6 us
    all_gather x1, blocking collectives, per_device(): every_state = lax.all_gather(state, 'seq')  15.9 us
    all_to_all x1, blocking collectives, per_device(): lax.all_to_all(pieces, ('seq', 'tp'), 0, 0, tiled=True).sum(axis=0)  14.5 us
    all_to_all x2, starting transfers between devices, gather_by_exchange(): return lax.all_to_all(copies, axes, 0, 0, tiled=True)  11.5 us
    unnamed x25, local copies, waits for them, and re-layouts  2.68 us
  transfers between devices with their start and end apart: 3, of which 2 were waited for; matrix products, arithmetic and copies ran while one was open for 10% of the time, Pallas kernels for 0%

profile of v4, /device:TPU:1, one launch (start us, length us, event | category | flops | bytes accessed | tf_op | source)
XLA Modules:
  0.0 120.7 jit_solution(4221673708893539754)
XLA Ops:
  7.2 0.0 all-gather.5.cloned.1.call-start
  7.2 1.7 %pad_maximum_fusion = bf16[384,256]{1,0:T(8,128)(2,1)} fusion(bf16[128,256]{1,0:T(8,128)(2,1)} %param.25, bf16[256,128]{1,0:T(8,128)(2,1)} %param.24, bf16[256,128]{1,0:T(8,128)(2,1)} %param.23), kind=kLoop, calls=%fused_computation.12 | loop fusion | flops 589824 | bytes 393216 | tf_op jit(solution)/shard_map/mlp_weight_gather/concatenate | solution.py:60
  8.9 0.0 all-gather.5.cloned.1.call-update
  9.0 0.8 convert_element_type.88
  9.7 0.9 multiply_reduce_fusion.1
  10.6 0.8 dynamic-slice
  11.4 0.2 fusion.32
  11.6 0.9 fusion.30
  12.5 0.9 fusion.34
  13.5 25.5 %all-gather = f32[128,768]{1,0:T(8,128)S(1)} all-gather(f32[8,768]{1,0:T(8,128)S(1)} %pad_maximum_fusion.2), channel_id=2, replica_groups=mesh['seq'=16,'mlp'=8,'tp'=4] {'seq'}, dimensions={0}, use_global_device_ids=true | all-gather | bytes 417792 | tf_op jit(solution)/shard_map/qkv_projection/all_gather | solution.py:32
  39.1 0.1 reshape.186
  39.2 0.1 broadcast_compare_fusion
  39.3 0.5 copy.124
  39.8 0.1 multiply_cosine_fusion
  39.9 0.1 subtract_convert_fusion
  40.0 0.4 select_reduce_fusion
  40.4 0.2 fusion.6
  40.6 0.2 copy.129
  40.8 0.5 copy.127
  41.4 0.4 fusion.7
  41.8 0.2 copy.128
  42.0 0.1 pad_maximum_fusion.1
  42.1 15.9 %all-gather.1 = f32[128,2,4,66]{3,2,1,0:T(4,128)S(1)} all-gather(f32[8,2,4,66]{3,2,1,0:T(4,128)S(1)} %pad_maximum_fusion.1), channel_id=3, replica_groups=mesh['seq'=16,'mlp'=8,'tp'=4] {'seq'}, dimensions={0}, use_global_device_ids=true | all-gather | bytes 287232 | tf_op jit(solution)/shard_map/softmax_merge/all_gather | solution.py:125
  58.0 0.1 copy.149
  58.1 0.1 reshape.189
  58.2 0.1 multiply_subtract_fusion
  58.3 0.1 fusion.27
  58.4 0.2 multiply_reduce_fusion.2
  58.6 0.1 copy.133
  58.7 0.3 fusion.29
  59.0 0.5 copy.136
  59.4 0.5 copy.146
  59.9 0.1 exponential_bitcast_fusion
  60.0 0.1 copy.134
  60.1 0.1 reshape.194
  60.2 0.2 fusion.14
  60.3 0.3 fusion.4
  60.7 0.1 divide_convert_fusion
  60.8 0.1 convert_element_type.97
  60.9 0.1 convolution_convert_fusion
  61.0 0.7 broadcast_in_dim.31
  61.7 6.1 %all-to-all-start = ((bf16[64,8,128]{2,1,0:T(8,128)(2,1)}), bf16[64,8,128]{2,1,0:T(8,128)(2,1)S(1)}, u32[]{:S(2)}, u32[]{:S(2)}) async-start(bf16[64,8,128]{2,1,0:T(8,128)(2,1)} %broadcast_in_dim.31), calls=%async_computation | async-start | bytes 262144 | tf_op jit(solution)/shard_map/output_projection/all_to_all | solution.py:40
  67.9 10.0 %all-to-all-done = bf16[64,8,128]{2,1,0:T(8,128)(2,1)S(1)} async-done(((bf16[64,8,128]{2,1,0:T(8,128)(2,1)}), bf16[64,8,128]{2,1,0:T(8,128)(2,1)S(1)}, u32[]{:S(2)}, u32[]{:S(2)}) %all-to-all-start) | async-done | bytes 131104 | tf_op jit(solution)/shard_map/output_projection/all_to_all | solution.py:40
  77.9 0.1 multiply_reduce_fusion
  78.1 0.0 all-gather.5.cloned.1.call-done
  78.1 1.3 %fusion.28 = (bf16[8,256,128]{2,1,0:T(8,128)(2,1)S(1)}, bf16[8,256,128]{2,1,0:T(8,128)(2,1)S(1)}) fusion(bf16[8,384,256]{2,1,0:T(8,128)(2,1)} %bitcast.62), kind=kLoop, calls=%fused_computation.67 | loop fusion | bytes 2097152 | tf_op jit(solution)/shard_map/slice | solution.py:65
  79.4 0.2 fusion.25
  79.6 1.4 %fusion.2 = f32[8,8,256]{2,0,1:T(8,128)S(1)} fusion(bf16[2048,128]{1,0:T(8,128)(2,1)S(1)} %bitcast.60, bf16[8,384,256]{2,1,0:T(8,128)(2,1)} %bitcast.63, f32[8,128]{1,0:T(8,128)S(1)} %fusion.25, f32[2048]{0:T(1024)S(1)} %convert_element_type.102, f32[8]{0:T(128)S(1)} %add_rsqrt_fusion, bf16[16,8,128]{2,1,0:T(8,128)(2,1)S(1)} %bitcast_reduce_fusion.1, ...), kind=kOutput, calls=%fused_computation.5 | convolution fusion | flops 8493056 | bytes 1191968 | tf_op jit(solution)/shard_map/feed_forward/rh,jhc->rjc/dot_general | solution.py:167
  81.1 0.1 reshape.193
  81.2 0.2 copy.139
  81.4 0.2 reshape.201
  81.6 14.5 %all_to_all.15 = f32[64,1,256]{2,1,0:T(1,128)S(1)} all-to-all(f32[64,1,256]{2,1,0:T(1,128)S(1)} %reshape.201), channel_id=1, replica_groups=mesh['seq'=16,'mlp'=8,'tp'=4] {'seq','tp'}, dimensions={0} | all-to-all | bytes 131072 | tf_op jit(solution)/shard_map/down_reduction/all_to_all | solution.py:173
  96.0 0.5 broadcast.121
  96.5 0.8 reduce.2
  97.3 0.1 reshape.202
  97.5 0.1 reduce_sum.92
  97.6 0.7 reshape.203
  98.3 5.3 %all-to-all-start.2 = ((bf16[64,2,128]{2,1,0:T(2,128)(2,1)}), bf16[64,2,128]{2,1,0:T(2,128)(2,1)S(1)}, u32[]{:S(2)}, u32[]{:S(2)}) async-start(bf16[64,2,128]{2,1,0:T(2,128)(2,1)} %reshape.203), calls=%async_computation.2 | async-start | bytes 65536 | tf_op jit(solution)/shard_map/down_reduction/all_to_all | solution.py:40
  103.6 0.7 convert_element_type.110
  104.3 8.6 %all-to-all-done.2 = bf16[64,2,128]{2,1,0:T(2,128)(2,1)S(1)} async-done(((bf16[64,2,128]{2,1,0:T(2,128)(2,1)}), bf16[64,2,128]{2,1,0:T(2,128)(2,1)S(1)}, u32[]{:S(2)}, u32[]{:S(2)}) %all-to-all-start.2) | async-done | bytes 32800 | tf_op jit(solution)/shard_map/down_reduction/all_to_all | solution.py:40
  112.9 0.1 reshape.204
  113.0 0.1 copy.140
  113.1 0.1 reshape.196
  113.2 0.6 add_convert_fusion
  (38 shorter events, 0.3 us)
Async XLA Ops:
  7.2 4.2 %copy-start = (bf16[128,512]{1,0:T(8,128)(2,1)S(1)}, bf16[128,512]{1,0:T(8,128)(2,1)}, u32[]{:S(2)}) copy-start(bf16[128,512]{1,0:T(8,128)(2,1)} %param.16) | copy-start | bytes 393220
  7.2 32.0 %copy-start.8 = (s32[8]{0:T(128)S(1)}, s32[8]{0:T(128)}, u32[]{:S(2)}) copy-start(s32[8]{0:T(128)} %param.14) | copy-start | bytes 100
  7.2 32.1 %copy-start.2 = (bf16[8,512,128]{2,1,0:T(8,128)(2,1)S(1)}, bf16[8,512,128]{2,1,0:T(8,128)(2,1)}, u32[]{:S(2)}) copy-start(bf16[8,512,128]{2,1,0:T(8,128)(2,1)} %param.19) | copy-start | bytes 3145732
  7.2 70.9 %all-gather.5.cloned.1.call-start = ((), (), s32[]{:S(2)}) async-start(), calls=%async_computation.3 | async-start | bytes 1769472 | tf_op jit(solution)/shard_map/mlp_weight_gather/all_gather | solution.py:63
  39.0 1.4 %copy-start.5 = (f32[8,768]{1,0:T(8,128)}, f32[8,768]{1,0:T(8,128)S(1)}, u32[]{:S(2)}) copy-start(f32[8,768]{1,0:T(8,128)S(1)} %bitcast_reduce_fusion) | copy-start | bytes 73732
  39.1 21.0 %copy-start.6 = (bf16[8,128]{1,0:T(8,128)(2,1)}, bf16[8,128]{1,0:T(8,128)(2,1)S(1)}, u32[]{:S(2)}) copy-start(bf16[8,128]{1,0:T(8,128)(2,1)S(1)} %slice.81) | copy-start | bytes 6148
  39.2 1.6 %copy-start.3 = (bf16[8,512,128]{2,1,0:T(8,128)(2,1)S(1)}, bf16[8,512,128]{2,1,0:T(8,128)(2,1)}, u32[]{:S(2)}) copy-start(bf16[8,512,128]{2,1,0:T(8,128)(2,1)} %param.20) | copy-start | bytes 3145732
  41.3 16.8 %slice-start = ((f32[8,768]{1,0:T(8,128)}), f32[8,128]{1,0:T(8,128)S(1)}, s32[]{:S(2)}) async-start(f32[8,768]{1,0:T(8,128)} %copy-done.5), calls=%async_computation.4 | async-start | bytes 8192 | tf_op jit(solution)/shard_map/slice | solution.py:89
  58.9 2.0 %copy-start.4 = (bf16[512,128]{1,0:T(8,128)(2,1)S(1)}, bf16[512,128]{1,0:T(8,128)(2,1)}, u32[]{:S(2)}) copy-start(bf16[512,128]{1,0:T(8,128)(2,1)} %param.21) | copy-start | bytes 393220
  59.0 8.9 %copy-start.7 = (bf16[2048]{0:T(1024)(128)(2,1)S(1)}, bf16[2048]{0:T(1024)(128)(2,1)}, u32[]{:S(2)}) copy-start(bf16[2048]{0:T(1024)(128)(2,1)} %param.22) | copy-start | bytes 12292
  59.0 19.0 %copy-start.1 = (bf16[8,2048]{1,0:T(8,128)(2,1)S(1)}, bf16[8,2048]{1,0:T(8,128)(2,1)}, u32[]{:S(2)}) copy-start(bf16[8,2048]{1,0:T(8,128)(2,1)} %param.13) | copy-start | bytes 98308
  61.7 16.2 %all-to-all-start = ((bf16[64,8,128]{2,1,0:T(8,128)(2,1)}), bf16[64,8,128]{2,1,0:T(8,128)(2,1)S(1)}, u32[]{:S(2)}, u32[]{:S(2)}) async-start(bf16[64,8,128]{2,1,0:T(8,128)(2,1)} %broadcast_in_dim.31), calls=%async_computation | async-start | bytes 262144 | tf_op jit(solution)/shard_map/output_projection/all_to_all | solution.py:40
  98.3 14.6 %all-to-all-start.2 = ((bf16[64,2,128]{2,1,0:T(2,128)(2,1)}), bf16[64,2,128]{2,1,0:T(2,128)(2,1)S(1)}, u32[]{:S(2)}, u32[]{:S(2)}) async-start(bf16[64,2,128]{2,1,0:T(2,128)(2,1)} %reshape.203), calls=%async_computation.2 | async-start | bytes 65536 | tf_op jit(solution)/shard_map/down_reduction/all_to_all | solution.py:40
Sparse Core Ops, SparseCore 0:
  10.1 43.1 all-gather.4

commit v5 on v4

--- a/solution.py
+++ b/solution.py
@@ -100,47 +100,55 @@
     new_values = values_raw.astype(jnp.bfloat16)
     grouped = queries.reshape(requests, key_heads, group_size, HD)
     block_span = cached_keys.shape[1]
-    key_blocks = cached_keys.reshape(requests, block_span, key_heads, HD)
-    value_blocks = cached_values.reshape(requests, block_span, key_heads, HD)
     score_scale = HD ** (-0.5)
     first_position = lax.axis_index("seq") * block_span
     positions = first_position + jnp.arange(block_span, dtype=jnp.int32)
-    valid_mask = (positions[None, :] < lengths[:, None])[:, None, None, :]
+    valid_mask = (positions[None, :] < lengths[:, None])[:, None, :]
+    own_head = jnp.arange(key_heads)[:, None] == jnp.arange(key_heads)[None, :]
     with jax.named_scope("local_attention"):
+        padded_queries = jnp.where(
+            own_head[None, :, None, :, None],
+            grouped[:, :, :, None, :],
+            jnp.zeros((), grouped.dtype),
+        ).reshape(requests, key_heads * group_size, key_heads * HD)
         scores = (
-            jnp.einsum("rgqd,rpgd->rgqp", grouped, key_blocks, preferred_element_type=jnp.float32)
+            jnp.einsum(
+                "rmk,rpk->rmp", padded_queries, cached_keys, preferred_element_type=jnp.float32
+            )
             * score_scale
         )
         block_max = jnp.max(jnp.where(valid_mask, scores, -1e30), axis=-1)
         exp_weights = jnp.where(valid_mask, jnp.exp(scores - block_max[..., None]), 0.0)
         block_sum = jnp.sum(exp_weights, axis=-1)
-        block_acc = jnp.einsum(
-            "rgqp,rpgd->rgqd",
+        every_head_acc = jnp.einsum(
+            "rmp,rpk->rmk",
             exp_weights.astype(jnp.bfloat16),
-            value_blocks,
+            cached_values,
             preferred_element_type=jnp.float32,
-        )
+        ).reshape(requests, key_heads * group_size, key_heads, HD)
+        own_block = jnp.repeat(own_head, group_size, axis=0)
+        block_acc = jnp.sum(jnp.where(own_block[None, :, :, None], every_head_acc, 0.0), axis=2)
     with jax.named_scope("softmax_merge"):
         state = jnp.concatenate([block_max[..., None], block_sum[..., None], block_acc], axis=-1)
         every_state = lax.all_gather(state, "seq")
         every_max = every_state[..., 0]
         every_sum = every_state[..., 1]
         every_acc = every_state[..., 2:]
-        query_float = grouped.astype(jnp.float32)
-        self_score = (
-            jnp.sum(
-                query_float * new_keys.astype(jnp.float32).reshape(requests, key_heads, 1, HD),
-                axis=-1,
-            )
-            * score_scale
-        )
+        query_float = grouped.astype(jnp.float32).reshape(requests, local_heads, HD)
+        head_keys = jnp.repeat(
+            new_keys.astype(jnp.float32).reshape(requests, key_heads, HD), group_size, axis=1
+        )
+        head_values = jnp.repeat(
+            new_values.astype(jnp.float32).reshape(requests, key_heads, HD), group_size, axis=1
+        )
+        self_score = jnp.sum(query_float * head_keys, axis=-1) * score_scale
         overall_max = jnp.maximum(jnp.max(every_max, axis=0), self_score)
         rescale = jnp.exp(every_max - overall_max[None])
         self_weight = jnp.exp(self_score - overall_max)
         total_weight = jnp.sum(every_sum * rescale, axis=0) + self_weight
-        weighted_sum = jnp.sum(every_acc * rescale[..., None], axis=0) + self_weight[
-            ..., None
-        ] * new_values.astype(jnp.float32).reshape(requests, key_heads, 1, HD)
+        weighted_sum = (
+            jnp.sum(every_acc * rescale[..., None], axis=0) + self_weight[..., None] * head_values
+        )
         attended = (
             (weighted_sum / total_weight[..., None])
             .reshape(requests, local_heads * HD)

time: 121 us -> 122 us (level)
    unnamed x25 -> x19, local copies, waits for them, and re-layouts: 2.68 us -> 1.63 us
where the time goes in v5:
time: 122 us; the launch traced here: 121 us
  blocking collectives  55.9 us (46%)
  waiting for transfers between devices  18.6 us (15%)
  between operations  14.4 us (12%)
  starting transfers between devices  11.5 us (9%)
  local copies, waits for them, and re-layouts  8.22 us (7%)
  other arithmetic  7.08 us (6%)
  matrix products  5.52 us (5%)
    all_gather x1, blocking collectives, gathered_sum(): return jnp.sum(lax.all_gather(x, axis), axis=0)  25.5 us
    all_to_all x2, waiting for transfers between devices, gather_by_exchange(): return lax.all_to_all(copies, axes, 0, 0, tiled=True)  18.6 us
    all_gather x1, blocking collectives, per_device(): every_state = lax.all_gather(state, 'seq')  15.9 us
    all_to_all x1, blocking collectives, per_device(): lax.all_to_all(pieces, ('seq', 'tp'), 0, 0, tiled=True).sum(axis=0)  14.5 us
    all_to_all x2, starting transfers between devices, gather_by_exchange(): return lax.all_to_all(copies, axes, 0, 0, tiled=True)  11.5 us
  transfers between devices with their start and end apart: 3, of which 2 were waited for; matrix products, arithmetic and copies ran while one was open for 10% of the time, Pallas kernels for 0%

profile of v5, /device:TPU:1, one launch (start us, length us, event | category | flops | bytes accessed | tf_op | source)
XLA Modules:
  0.0 121.2 jit_solution(11687460640247441021)
XLA Ops:
  7.2 1.7 %pad_maximum_fusion = bf16[384,256]{1,0:T(8,128)(2,1)} fusion(bf16[128,256]{1,0:T(8,128)(2,1)} %param.25, bf16[256,128]{1,0:T(8,128)(2,1)} %param.24, bf16[256,128]{1,0:T(8,128)(2,1)} %param.23), kind=kLoop, calls=%fused_computation.11 | loop fusion | flops 589824 | bytes 393216 | tf_op jit(solution)/shard_map/mlp_weight_gather/concatenate | solution.py:60
  8.9 0.8 convert_element_type.87
  9.7 1.0 multiply_reduce_fusion.1
  10.7 0.8 dynamic-slice
  11.5 1.1 fusion.35
  12.5 0.9 fusion.33
  13.5 0.9 fusion.37
  14.4 25.5 %all-gather = f32[128,768]{1,0:T(8,128)S(1)} all-gather(f32[8,768]{1,0:T(8,128)S(1)} %pad_maximum_fusion.2), channel_id=2, replica_groups=mesh['seq'=16,'mlp'=8,'tp'=4] {'seq'}, dimensions={0}, use_global_device_ids=true | all-gather | bytes 417792 | tf_op jit(solution)/shard_map/qkv_projection/all_gather | solution.py:32
  40.1 0.1 reshape.233
  40.1 0.1 reshape.231
  40.2 0.1 multiply_cosine_fusion
  40.3 0.1 multiply_subtract_fusion
  40.4 0.1 subtract_convert_fusion
  40.5 0.1 fusion.31
  40.6 0.2 multiply_reduce_fusion.2
  40.8 0.1 broadcast_in_dim.113
  40.9 0.1 broadcast_compare_fusion
  41.0 0.1 copy.86
  41.1 0.1 broadcast_in_dim.109
  41.2 0.1 broadcast_in_dim.110
  41.3 0.5 select_reduce_fusion
  41.7 0.2 fusion.6
  41.9 0.1 copy.89
  42.0 0.3 fusion.7
  42.3 0.1 reshape.232
  42.4 0.1 copy.88
  42.6 0.1 copy.92
  42.7 0.2 select_reduce_fusion.1
  42.9 0.1 pad_maximum_fusion.1
  43.0 15.9 %all-gather.1 = f32[128,8,66]{2,1,0:T(8,128)S(1)} all-gather(f32[8,8,66]{2,1,0:T(8,128)S(1)} %pad_maximum_fusion.1), channel_id=3, replica_groups=mesh['seq'=16,'mlp'=8,'tp'=4] {'seq'}, dimensions={0}, use_global_device_ids=true | all-gather | bytes 287232 | tf_op jit(solution)/shard_map/softmax_merge/all_gather | solution.py:133
  58.9 0.3 slice_reduce_fusion
  59.2 0.5 copy.102
  59.7 0.1 exponential_bitcast_fusion
  59.8 0.1 copy.94
  59.9 0.3 fusion.4
  60.3 0.5 copy.96
  60.8 0.2 fusion.14
  61.0 0.1 div.31
  61.2 0.1 mul.223
  61.3 0.1 reshape.242
  61.4 0.1 reshape.236
  61.5 0.1 convolution_convert_fusion
  61.6 0.7 broadcast_in_dim.125
  62.3 6.1 %all-to-all-start = ((bf16[64,8,128]{2,1,0:T(8,128)(2,1)}), bf16[64,8,128]{2,1,0:T(8,128)(2,1)S(1)}, u32[]{:S(2)}, u32[]{:S(2)}) async-start(bf16[64,8,128]{2,1,0:T(8,128)(2,1)} %broadcast_in_dim.125), calls=%async_computation | async-start | bytes 262144 | tf_op jit(solution)/shard_map/output_projection/all_to_all | solution.py:40
  68.4 10.0 %all-to-all-done = bf16[64,8,128]{2,1,0:T(8,128)(2,1)S(1)} async-done(((bf16[64,8,128]{2,1,0:T(8,128)(2,1)}), bf16[64,8,128]{2,1,0:T(8,128)(2,1)S(1)}, u32[]{:S(2)}, u32[]{:S(2)}) %all-to-all-start) | async-done | bytes 131104 | tf_op jit(solution)/shard_map/output_projection/all_to_all | solution.py:40
  78.5 0.1 multiply_reduce_fusion
  78.7 1.3 %fusion.32 = (bf16[8,256,128]{2,1,0:T(8,128)(2,1)S(1)}, bf16[8,256,128]{2,1,0:T(8,128)(2,1)S(1)}) fusion(bf16[8,384,256]{2,1,0:T(8,128)(2,1)} %bitcast.58), kind=kLoop, calls=%fused_computation.72 | loop fusion | bytes 2097152 | tf_op jit(solution)/shard_map/slice | solution.py:65
  79.9 0.2 fusion.29
  80.2 1.4 %fusion.2 = f32[8,8,256]{2,0,1:T(8,128)S(1)} fusion(bf16[2048,128]{1,0:T(8,128)(2,1)S(1)} %bitcast.56, bf16[8,384,256]{2,1,0:T(8,128)(2,1)} %bitcast.59, f32[8,128]{1,0:T(8,128)S(1)} %fusion.29, f32[2048]{0:T(1024)S(1)} %convert_element_type.100, f32[8]{0:T(128)S(1)} %add_rsqrt_fusion, bf16[16,8,128]{2,1,0:T(8,128)(2,1)S(1)} %bitcast_reduce_fusion.1, ...), kind=kOutput, calls=%fused_computation.5 | convolution fusion | flops 8493056 | bytes 1191968 | tf_op jit(solution)/shard_map/feed_forward/rh,jhc->rjc/dot_general | solution.py:175
  81.7 0.1 reshape.240
  81.8 0.2 copy.98
  81.9 0.2 reshape.249
  82.1 14.5 %all_to_all.15 = f32[64,1,256]{2,1,0:T(1,128)S(1)} all-to-all(f32[64,1,256]{2,1,0:T(1,128)S(1)} %reshape.249), channel_id=1, replica_groups=mesh['seq'=16,'mlp'=8,'tp'=4] {'seq','tp'}, dimensions={0} | all-to-all | bytes 131072 | tf_op jit(solution)/shard_map/down_reduction/all_to_all | solution.py:181
  96.6 0.5 broadcast.132
  97.1 0.8 reduce.3
  97.9 0.1 reshape.250
  98.0 0.1 reduce_sum.105
  98.1 0.7 reshape.251
  98.8 5.3 %all-to-all-start.2 = ((bf16[64,2,128]{2,1,0:T(2,128)(2,1)}), bf16[64,2,128]{2,1,0:T(2,128)(2,1)S(1)}, u32[]{:S(2)}, u32[]{:S(2)}) async-start(bf16[64,2,128]{2,1,0:T(2,128)(2,1)} %reshape.251), calls=%async_computation.2 | async-start | bytes 65536 | tf_op jit(solution)/shard_map/down_reduction/all_to_all | solution.py:40
  104.2 0.7 convert_element_type.108
  104.9 8.6 %all-to-all-done.2 = bf16[64,2,128]{2,1,0:T(2,128)(2,1)S(1)} async-done(((bf16[64,2,128]{2,1,0:T(2,128)(2,1)}), bf16[64,2,128]{2,1,0:T(2,128)(2,1)S(1)}, u32[]{:S(2)}, u32[]{:S(2)}) %all-to-all-start.2) | async-done | bytes 32800 | tf_op jit(solution)/shard_map/down_reduction/all_to_all | solution.py:40
  113.4 0.1 reshape.252
  113.6 0.1 reshape.244
  113.8 0.6 add_convert_fusion
  (44 shorter events, 0.7 us)
Async XLA Ops:
  7.2 34.1 %copy-start = (bf16[8,512,128]{2,1,0:T(8,128)(2,1)S(1)}, bf16[8,512,128]{2,1,0:T(8,128)(2,1)}, u32[]{:S(2)}) copy-start(bf16[8,512,128]{2,1,0:T(8,128)(2,1)} %param.19) | copy-start | bytes 3145732
  7.2 33.0 %copy-start.6 = (s32[8]{0:T(128)S(1)}, s32[8]{0:T(128)}, u32[]{:S(2)}) copy-start(s32[8]{0:T(128)} %param.14) | copy-start | bytes 100
  7.2 71.5 %all-gather.5.cloned.1.call-start = ((), (), s32[]{:S(2)}) async-start(), calls=%async_computation.3 | async-start | bytes 1769472 | tf_op jit(solution)/shard_map/mlp_weight_gather/all_gather | solution.py:63
  9.7 32.3 %copy-start.2 = (bf16[8,512,128]{2,1,0:T(8,128)(2,1)S(1)}, bf16[8,512,128]{2,1,0:T(8,128)(2,1)}, u32[]{:S(2)}) copy-start(bf16[8,512,128]{2,1,0:T(8,128)(2,1)} %param.20) | copy-start | bytes 3145732
  40.0 21.2 %copy-start.4 = (bf16[8,128]{1,0:T(8,128)(2,1)}, bf16[8,128]{1,0:T(8,128)(2,1)S(1)}, u32[]{:S(2)}) copy-start(bf16[8,128]{1,0:T(8,128)(2,1)S(1)} %slice.81) | copy-start | bytes 6148
  59.2 2.3 %copy-start.3 = (bf16[512,128]{1,0:T(8,128)(2,1)S(1)}, bf16[512,128]{1,0:T(8,128)(2,1)}, u32[]{:S(2)}) copy-start(bf16[512,128]{1,0:T(8,128)(2,1)} %param.21) | copy-start | bytes 393220
  59.2 9.2 %copy-start.5 = (bf16[2048]{0:T(1024)(128)(2,1)S(1)}, bf16[2048]{0:T(1024)(128)(2,1)}, u32[]{:S(2)}) copy-start(bf16[2048]{0:T(1024)(128)(2,1)} %param.22) | copy-start | bytes 12292
  59.2 19.3 %copy-start.1 = (bf16[8,2048]{1,0:T(8,128)(2,1)S(1)}, bf16[8,2048]{1,0:T(8,128)(2,1)}, u32[]{:S(2)}) copy-start(bf16[8,2048]{1,0:T(8,128)(2,1)} %param.13) | copy-start | bytes 98308
  62.3 16.2 %all-to-all-start = ((bf16[64,8,128]{2,1,0:T(8,128)(2,1)}), bf16[64,8,128]{2,1,0:T(8,128)(2,1)S(1)}, u32[]{:S(2)}, u32[]{:S(2)}) async-start(bf16[64,8,128]{2,1,0:T(8,128)(2,1)} %broadcast_in_dim.125), calls=%async_computation | async-start | bytes 262144 | tf_op jit(solution)/shard_map/output_projection/all_to_all | solution.py:40
  98.8 14.6 %all-to-all-start.2 = ((bf16[64,2,128]{2,1,0:T(2,128)(2,1)}), bf16[64,2,128]{2,1,0:T(2,128)(2,1)S(1)}, u32[]{:S(2)}, u32[]{:S(2)}) async-start(bf16[64,2,128]{2,1,0:T(2,128)(2,1)} %reshape.251), calls=%async_computation.2 | async-start | bytes 65536 | tf_op jit(solution)/shard_map/down_reduction/all_to_all | solution.py:40
Sparse Core Ops, SparseCore 0:
  10.1 43.2 all-gather.4

commit v6 on v4

--- a/solution.py
+++ b/solution.py
@@ -56,15 +56,18 @@
     down_weight,
 ):
     slab_rows, hidden_units = gate_weight.shape
+    halves = slab_rows // hidden_units
     with jax.named_scope("mlp_weight_gather"):
         slab = jnp.concatenate(
-            [jnp.concatenate([gate_weight, up_weight], axis=1), down_weight], axis=0
+            [gate_weight, up_weight]
+            + [down_weight[:, i * hidden_units : (i + 1) * hidden_units] for i in range(halves)],
+            axis=0,
         )
         blocks = lax.all_gather(slab, "mlp")
     slabs = blocks.shape[0]
-    gate_full = blocks[:, :slab_rows, :hidden_units].reshape(slabs * slab_rows, hidden_units)
-    up_full = blocks[:, :slab_rows, hidden_units:].reshape(slabs * slab_rows, hidden_units)
-    down_blocks = blocks[:, slab_rows:, :]
+    gate_full = blocks[:, :slab_rows].reshape(slabs * slab_rows, hidden_units)
+    up_full = blocks[:, slab_rows : 2 * slab_rows].reshape(slabs * slab_rows, hidden_units)
+    down_blocks = blocks[:, 2 * slab_rows :].reshape(slabs, halves, hidden_units, hidden_units)
 
     requests = hidden.shape[0]
     stream = hidden.astype(jnp.float32)
@@ -165,7 +168,7 @@
         upward = jnp.dot(mlp_input, up_full, preferred_element_type=jnp.float32)
         activated = (jax.nn.silu(gate) * upward).astype(jnp.bfloat16)
         down_part = jnp.einsum(
-            "rh,jhc->rjc", activated, down_blocks, preferred_element_type=jnp.float32
+            "rh,jihc->rjic", activated, down_blocks, preferred_element_type=jnp.float32
         ).reshape(requests, slabs * slab_rows)
     with jax.named_scope("down_reduction"):
         reducers = lax.axis_size("seq") * lax.axis_size("tp")

time: 121 us -> 122 us (level)
  local copies, waits for them, and re-layouts: 8.58 us -> 9.82 us
where the time goes in v6:
time: 122 us; the launch traced here: 121 us
  blocking collectives  55.9 us (46%)
  waiting for transfers between devices  18.6 us (15%)
  between operations  14.4 us (12%)
  starting transfers between devices  11.5 us (9%)
  local copies, waits for them, and re-layouts  9.82 us (8%)
  other arithmetic  6.86 us (6%)
  matrix products  3.93 us (3%)
    all_gather x1, blocking collectives, gathered_sum(): return jnp.sum(lax.all_gather(x, axis), axis=0)  25.5 us
    all_to_all x2, waiting for transfers between devices, gather_by_exchange(): return lax.all_to_all(copies, axes, 0, 0, tiled=True)  18.6 us
    all_gather x1, blocking collectives, per_device(): every_state = lax.all_gather(state, 'seq')  15.9 us
    all_to_all x1, blocking collectives, per_device(): lax.all_to_all(pieces, ('seq', 'tp'), 0, 0, tiled=True).sum(axis=0)  14.5 us
    all_to_all x2, starting transfers between devices, gather_by_exchange(): return lax.all_to_all(copies, axes, 0, 0, tiled=True)  11.5 us
    unnamed x25, local copies, waits for them, and re-layouts  2.68 us
  transfers between devices with their start and end apart: 3, of which 2 were waited for; matrix products, arithmetic and copies ran while one was open for 10% of the time, Pallas kernels for 0%

profile of v6, /device:TPU:1, one launch (start us, length us, event | category | flops | bytes accessed | tf_op | source)
XLA Modules:
  0.0 121.0 jit_solution(7594341156971721533)
XLA Ops:
  7.2 0.0 all-gather.5.cloned.1.call-start
  7.2 0.9 fusion.29
  8.1 1.6 %pad_maximum_fusion = bf16[768,128]{1,0:T(8,128)(2,1)} fusion(bf16[128,128]{1,0:T(8,128)(2,1)S(1)} %get-tuple-element.14, bf16[128,128]{1,0:T(8,128)(2,1)S(1)} %get-tuple-element.13, bf16[256,128]{1,0:T(8,128)(2,1)} %param.24, bf16[256,128]{1,0:T(8,128)(2,1)} %param.23), kind=kLoop, calls=%fused_computation.12 | loop fusion | flops 786432 | bytes 393216 | tf_op jit(solution)/shard_map/mlp_weight_gather/concatenate | solution.py:61
  9.7 0.8 convert_element_type.88
  10.5 0.9 multiply_reduce_fusion.1
  11.4 0.8 dynamic-slice
  12.1 0.2 fusion.32
  12.3 0.9 fusion.30
  13.3 0.9 fusion.34
  14.2 25.5 %all-gather = f32[128,768]{1,0:T(8,128)S(1)} all-gather(f32[8,768]{1,0:T(8,128)S(1)} %pad_maximum_fusion.2), channel_id=2, replica_groups=mesh['seq'=16,'mlp'=8,'tp'=4] {'seq'}, dimensions={0}, use_global_device_ids=true | all-gather | bytes 417792 | tf_op jit(solution)/shard_map/qkv_projection/all_gather | solution.py:32
  39.8 0.1 reshape.188
  39.9 0.1 broadcast_compare_fusion
  40.0 0.5 copy.154
  40.5 0.1 multiply_cosine_fusion
  40.6 0.1 subtract_convert_fusion
  40.7 0.4 select_reduce_fusion
  41.1 0.2 fusion.5
  41.3 0.2 copy.159
  41.6 0.5 copy.157
  42.1 0.4 fusion.6
  42.5 0.2 copy.158
  42.7 0.1 pad_maximum_fusion.1
  42.9 15.9 %all-gather.1 = f32[128,2,4,66]{3,2,1,0:T(4,128)S(1)} all-gather(f32[8,2,4,66]{3,2,1,0:T(4,128)S(1)} %pad_maximum_fusion.1), channel_id=3, replica_groups=mesh['seq'=16,'mlp'=8,'tp'=4] {'seq'}, dimensions={0}, use_global_device_ids=true | all-gather | bytes 287232 | tf_op jit(solution)/shard_map/softmax_merge/all_gather | solution.py:128
  58.8 0.1 copy.185
  58.9 0.1 reshape.191
  59.0 0.1 multiply_subtract_fusion
  59.0 0.1 fusion.26
  59.1 0.2 multiply_reduce_fusion.2
  59.3 0.1 copy.163
  59.4 0.3 fusion.28
  59.7 0.5 copy.166
  60.2 0.5 copy.180
  60.6 0.1 exponential_bitcast_fusion
  60.7 0.1 copy.164
  60.8 0.1 reshape.196
  60.9 0.2 fusion.13
  61.1 0.3 fusion.2
  61.4 0.1 divide_convert_fusion
  61.6 0.1 convert_element_type.97
  61.7 0.1 convolution_convert_fusion
  61.8 0.7 broadcast_in_dim.31
  62.5 6.1 %all-to-all-start = ((bf16[64,8,128]{2,1,0:T(8,128)(2,1)}), bf16[64,8,128]{2,1,0:T(8,128)(2,1)S(1)}, u32[]{:S(2)}, u32[]{:S(2)}) async-start(bf16[64,8,128]{2,1,0:T(8,128)(2,1)} %broadcast_in_dim.31), calls=%async_computation | async-start | bytes 262144 | tf_op jit(solution)/shard_map/output_projection/all_to_all | solution.py:40
  68.6 10.0 %all-to-all-done = bf16[64,8,128]{2,1,0:T(8,128)(2,1)S(1)} async-done(((bf16[64,8,128]{2,1,0:T(8,128)(2,1)}), bf16[64,8,128]{2,1,0:T(8,128)(2,1)S(1)}, u32[]{:S(2)}, u32[]{:S(2)}) %all-to-all-start) | async-done | bytes 131104 | tf_op jit(solution)/shard_map/output_projection/all_to_all | solution.py:40
  78.7 0.1 multiply_reduce_fusion
  78.8 0.0 all-gather.5.cloned.1.call-done
  78.8 1.5 %fusion.27 = (bf16[8,256,128]{2,1,0:T(8,128)(2,1)S(1)}, bf16[8,256,128]{2,1,0:T(8,128)(2,1)S(1)}, bf16[8,256,128]{2,1,0:T(8,128)(2,1)S(1)}) fusion(bf16[8,768,128]{2,1,0:T(8,128)(2,1)} %bitcast.69), kind=kLoop, calls=%fused_computation.67 | loop fusion | bytes 3145728 | tf_op jit(solution)/shard_map/slice | solution.py:68
  80.3 0.3 copy.168
  80.6 0.2 fusion.24
  80.8 0.7 convolution_bitcast_fusion
  81.5 0.2 copy.170
  81.7 0.2 reshape.203
  81.9 14.5 %all_to_all.15 = f32[64,1,256]{2,1,0:T(1,128)S(1)} all-to-all(f32[64,1,256]{2,1,0:T(1,128)S(1)} %reshape.203), channel_id=1, replica_groups=mesh['seq'=16,'mlp'=8,'tp'=4] {'seq','tp'}, dimensions={0} | all-to-all | bytes 131072 | tf_op jit(solution)/shard_map/down_reduction/all_to_all | solution.py:176
  96.4 0.5 broadcast.121
  96.9 0.8 reduce.2
  97.7 0.1 reshape.204
  97.8 0.1 reduce_sum.92
  97.9 0.7 reshape.205
  98.6 5.3 %all-to-all-start.2 = ((bf16[64,2,128]{2,1,0:T(2,128)(2,1)}), bf16[64,2,128]{2,1,0:T(2,128)(2,1)S(1)}, u32[]{:S(2)}, u32[]{:S(2)}) async-start(bf16[64,2,128]{2,1,0:T(2,128)(2,1)} %reshape.205), calls=%async_computation.2 | async-start | bytes 65536 | tf_op jit(solution)/shard_map/down_reduction/all_to_all | solution.py:40
  104.0 0.7 convert_element_type.110
  104.6 8.6 %all-to-all-done.2 = bf16[64,2,128]{2,1,0:T(2,128)(2,1)S(1)} async-done(((bf16[64,2,128]{2,1,0:T(2,128)(2,1)}), bf16[64,2,128]{2,1,0:T(2,128)(2,1)S(1)}, u32[]{:S(2)}, u32[]{:S(2)}) %all-to-all-start.2) | async-done | bytes 32800 | tf_op jit(solution)/shard_map/down_reduction/all_to_all | solution.py:40
  113.2 0.1 reshape.206
  113.4 0.1 copy.173
  113.4 0.1 reshape.198
  113.6 0.6 add_convert_fusion
  (38 shorter events, 0.2 us)
Async XLA Ops:
  7.2 5.0 %copy-start = (bf16[128,512]{1,0:T(8,128)(2,1)S(1)}, bf16[128,512]{1,0:T(8,128)(2,1)}, u32[]{:S(2)}) copy-start(bf16[128,512]{1,0:T(8,128)(2,1)} %param.16) | copy-start | bytes 393220
  7.2 32.7 %copy-start.8 = (s32[8]{0:T(128)S(1)}, s32[8]{0:T(128)}, u32[]{:S(2)}) copy-start(s32[8]{0:T(128)} %param.14) | copy-start | bytes 100
  7.2 32.8 %copy-start.2 = (bf16[8,512,128]{2,1,0:T(8,128)(2,1)S(1)}, bf16[8,512,128]{2,1,0:T(8,128)(2,1)}, u32[]{:S(2)}) copy-start(bf16[8,512,128]{2,1,0:T(8,128)(2,1)} %param.19) | copy-start | bytes 3145732
  7.2 71.6 %all-gather.5.cloned.1.call-start = ((), (), s32[]{:S(2)}) async-start(), calls=%async_computation.3 | async-start | bytes 1769472 | tf_op jit(solution)/shard_map/mlp_weight_gather/all_gather | solution.py:66
  39.8 1.4 %copy-start.5 = (f32[8,768]{1,0:T(8,128)}, f32[8,768]{1,0:T(8,128)S(1)}, u32[]{:S(2)}) copy-start(f32[8,768]{1,0:T(8,128)S(1)} %bitcast_reduce_fusion) | copy-start | bytes 73732
  39.8 21.0 %copy-start.6 = (bf16[8,128]{1,0:T(8,128)(2,1)}, bf16[8,128]{1,0:T(8,128)(2,1)S(1)}, u32[]{:S(2)}) copy-start(bf16[8,128]{1,0:T(8,128)(2,1)S(1)} %slice.87) | copy-start | bytes 6148
  40.0 1.6 %copy-start.3 = (bf16[8,512,128]{2,1,0:T(8,128)(2,1)S(1)}, bf16[8,512,128]{2,1,0:T(8,128)(2,1)}, u32[]{:S(2)}) copy-start(bf16[8,512,128]{2,1,0:T(8,128)(2,1)} %param.20) | copy-start | bytes 3145732
  42.1 16.8 %slice-start = ((f32[8,768]{1,0:T(8,128)}), f32[8,128]{1,0:T(8,128)S(1)}, s32[]{:S(2)}) async-start(f32[8,768]{1,0:T(8,128)} %copy-done.5), calls=%async_computation.4 | async-start | bytes 8192 | tf_op jit(solution)/shard_map/slice | solution.py:92
  59.7 2.0 %copy-start.4 = (bf16[512,128]{1,0:T(8,128)(2,1)S(1)}, bf16[512,128]{1,0:T(8,128)(2,1)}, u32[]{:S(2)}) copy-start(bf16[512,128]{1,0:T(8,128)(2,1)} %param.21) | copy-start | bytes 393220
  59.7 8.9 %copy-start.7 = (bf16[2048]{0:T(1024)(128)(2,1)S(1)}, bf16[2048]{0:T(1024)(128)(2,1)}, u32[]{:S(2)}) copy-start(bf16[2048]{0:T(1024)(128)(2,1)} %param.22) | copy-start | bytes 12292
  59.7 19.0 %copy-start.1 = (bf16[8,2048]{1,0:T(8,128)(2,1)S(1)}, bf16[8,2048]{1,0:T(8,128)(2,1)}, u32[]{:S(2)}) copy-start(bf16[8,2048]{1,0:T(8,128)(2,1)} %param.13) | copy-start | bytes 98308
  62.5 16.2 %all-to-all-start = ((bf16[64,8,128]{2,1,0:T(8,128)(2,1)}), bf16[64,8,128]{2,1,0:T(8,128)(2,1)S(1)}, u32[]{:S(2)}, u32[]{:S(2)}) async-start(bf16[64,8,128]{2,1,0:T(8,128)(2,1)} %broadcast_in_dim.31), calls=%async_computation | async-start | bytes 262144 | tf_op jit(solution)/shard_map/output_projection/all_to_all | solution.py:40
  98.6 14.6 %all-to-all-start.2 = ((bf16[64,2,128]{2,1,0:T(2,128)(2,1)}), bf16[64,2,128]{2,1,0:T(2,128)(2,1)S(1)}, u32[]{:S(2)}, u32[]{:S(2)}) async-start(bf16[64,2,128]{2,1,0:T(2,128)(2,1)} %reshape.205), calls=%async_computation.2 | async-start | bytes 65536 | tf_op jit(solution)/shard_map/down_reduction/all_to_all | solution.py:40
Sparse Core Ops, SparseCore 0:
  10.1 43.2 all-gather.4

commit v7 on v4

--- a/solution.py
+++ b/solution.py
@@ -1,6 +1,8 @@
 import jax
 import jax.numpy as jnp
 from jax import lax
+from jax.experimental import pallas as pl
+from jax.experimental.pallas import tpu as pltpu
 from jax.sharding import PartitionSpec as P
 
 HD = 64
@@ -26,6 +28,43 @@
         ],
         axis=-1,
     )
+
+
+def projection_kernel(block_ref, hidden_ref, gain_ref, query_ref, key_ref, value_ref, out_ref):
+    width = query_ref.shape[0]
+    offset = pl.multiple_of(block_ref[0] * width, width)
+    stream = hidden_ref[...].astype(jnp.float32)
+    mean_square = jnp.mean(stream * stream, axis=-1, keepdims=True)
+    columns = hidden_ref[:, pl.ds(offset, width)].astype(jnp.float32)
+    gains = gain_ref[:, pl.ds(offset, width)].astype(jnp.float32)
+    normed = (columns * lax.rsqrt(mean_square + 1e-05) * gains).astype(jnp.bfloat16)
+    query_width = query_ref.shape[1]
+    key_width = key_ref.shape[1]
+    out_ref[:, :query_width] = jnp.dot(normed, query_ref[...], preferred_element_type=jnp.float32)
+    out_ref[:, query_width : query_width + key_width] = jnp.dot(
+        normed, key_ref[...], preferred_element_type=jnp.float32
+    )
+    out_ref[:, query_width + key_width :] = jnp.dot(
+        normed, value_ref[...], preferred_element_type=jnp.float32
+    )
+
+
+def partial_projection(block, hidden, gain, query_weight, key_weight, value_weight):
+    rows, features = hidden.shape
+    width = query_weight.shape[0]
+    total = query_weight.shape[1] + key_weight.shape[1] + value_weight.shape[1]
+    vmem = pl.BlockSpec(memory_space=pltpu.VMEM)
+    return pl.pallas_call(
+        projection_kernel,
+        out_shape=jax.ShapeDtypeStruct((rows, total), jnp.float32),
+        in_specs=[pl.BlockSpec(memory_space=pltpu.SMEM)] + [vmem] * 5,
+        out_specs=vmem,
+        cost_estimate=pl.CostEstimate(
+            flops=2 * rows * width * total,
+            bytes_accessed=2 * (rows * features + features + width * total) + 4 * rows * total,
+            transcendentals=rows,
+        ),
+    )(block, hidden, gain.reshape(1, features), query_weight, key_weight, value_weight)
 
 
 def gathered_sum(x, axis):
@@ -68,21 +107,12 @@
 
     requests = hidden.shape[0]
     stream = hidden.astype(jnp.float32)
-    normed = rms_norm(stream, attention_gain).astype(jnp.bfloat16)
-    column_width = query_weight.shape[0]
-    own_columns = lax.dynamic_slice_in_dim(
-        normed, lax.axis_index("seq") * column_width, column_width, 1
-    )
     query_width = query_weight.shape[1]
     key_width = key_weight.shape[1]
     with jax.named_scope("qkv_projection"):
-        partial = jnp.concatenate(
-            [
-                jnp.dot(own_columns, query_weight, preferred_element_type=jnp.float32),
-                jnp.dot(own_columns, key_weight, preferred_element_type=jnp.float32),
-                jnp.dot(own_columns, value_weight, preferred_element_type=jnp.float32),
-            ],
-            axis=1,
+        block = lax.axis_index("seq").astype(jnp.int32).reshape(1)
+        partial = partial_projection(
+            block, hidden, attention_gain, query_weight, key_weight, value_weight
         )
         total = gathered_sum(partial, "seq")
     queries_raw = total[:, :query_width]

time: 121 us -> 120 us (level)
  matrix products: 4.69 us -> 2.63 us
  Pallas kernels: 0 us -> 1.8 us
  other arithmetic: 6.99 us -> 5.32 us
    dot_general x3 -> x0, matrix products: 2.06 us -> none  [the longest x1 0.94 us: per_device(): jnp.dot(own_columns, value_weight, preferred_element_type=jnp.float32)]
    pallas_call x0 -> x1, Pallas kernels: none -> 1.8 us  [partial_projection(): pl.pallas_call(projection_kernel, out_shape=jax.ShapeDtypeStruct((rows, t...]
    reshape x0 -> x1, local copies, waits for them, and re-layouts: none -> 1.29 us  [partial_projection(): gain.reshape(1, features)]
    unnamed x25 -> x23, local copies, waits for them, and re-layouts: 2.68 us -> 2.68 us
  transfers between devices with their start and end apart: 3 -> 3, of which waited for: 2 -> 2; matrix products, arithmetic and copies ran while one was open for 10% -> 7% of each run, Pallas kernels for 0% -> 2%
where the time goes in v7:
time: 120 us
  blocking collectives  56.2 us (47%)
  waiting for transfers between devices  18.6 us (16%)
  between operations  14.4 us (12%)
  starting transfers between devices  11.5 us (10%)
  local copies, waits for them, and re-layouts  9.1 us (8%)
  other arithmetic  5.32 us (4%)
  matrix products  2.63 us (2%)
  Pallas kernels  1.8 us (2%)
    all_gather x1, blocking collectives, gathered_sum(): return jnp.sum(lax.all_gather(x, axis), axis=0)  25.8 us
    all_to_all x2, waiting for transfers between devices, gather_by_exchange(): return lax.all_to_all(copies, axes, 0, 0, tiled=True)  18.6 us
    all_gather x1, blocking collectives, per_device(): every_state = lax.all_gather(state, 'seq')  15.9 us
    all_to_all x1, blocking collectives, per_device(): lax.all_to_all(pieces, ('seq', 'tp'), 0, 0, tiled=True).sum(axis=0)  14.5 us
    all_to_all x2, starting transfers between devices, gather_by_exchange(): return lax.all_to_all(copies, axes, 0, 0, tiled=True)  11.5 us
    unnamed x23, local copies, waits for them, and re-layouts  2.68 us
  transfers between devices with their start and end apart: 3, of which 2 were waited for; matrix products, arithmetic and copies ran while one was open for 7% of the time, Pallas kernels for 2%

profile of v7, /device:TPU:1, one launch (start us, length us, event | category | flops | bytes accessed | tf_op | source)
XLA Modules:
  0.0 119.5 jit_solution(11417879421406805291)
XLA Ops:
  7.2 0.0 copy-start
  7.2 0.0 all-gather.5.cloned.1.call-start
  7.2 1.7 %pad_maximum_fusion = bf16[384,256]{1,0:T(8,128)(2,1)} fusion(bf16[128,256]{1,0:T(8,128)(2,1)} %param.25, bf16[256,128]{1,0:T(8,128)(2,1)} %param.24, bf16[256,128]{1,0:T(8,128)(2,1)} %param.23), kind=kLoop, calls=%fused_computation.12 | loop fusion | flops 589824 | bytes 393216 | tf_op jit(solution)/shard_map/mlp_weight_gather/concatenate | solution.py:99
  8.9 0.0 all-gather.5.cloned.1.call-update
  9.0 1.3 %reshape.184.gain_ref = bf16[1,2048]{1,0:T(2,128)(2,1)} reshape(bf16[2048]{0:T(1024)(128)(2,1)} %param.15) | data formatting | bytes 8192 | tf_op jit(solution)/shard_map/qkv_projection/reshape | solution.py:67
  10.3 1.8 %qkv_projection.1 = f32[8,768]{1,0:T(8,128)} custom-call(s32[1]{0:T(128)} %bitcast.block_ref, bf16[8,2048]{1,0:T(8,128)(2,1)} %hidden_ref.1, bf16[1,2048]{1,0:T(2,128)(2,1)} %reshape.184.gain_ref, bf16[128,512]{1,0:T(8,128)(2,1)} %query_ref.1, bf16[128,128]{1,0:T(8,128)(2,1)} %key_ref.1, bf16[128,128]{1,0:T(8,128)(2,1)} %value_ref.1), custom_call_target="tpu_custom_call" | custom-call | flops 1572864 | bytes 258048 | tf_op jit(solution)/shard_map/qkv_projection/pallas_call | solution.py:57
  12.1 25.8 %all-gather = f32[128,768]{1,0:T(8,128)S(1)} all-gather(f32[8,768]{1,0:T(8,128)} %qkv_projection.1), channel_id=2, replica_groups=mesh['seq'=16,'mlp'=8,'tp'=4] {'seq'}, dimensions={0}, use_global_device_ids=true | all-gather | bytes 417792 | tf_op jit(solution)/shard_map/qkv_projection/all_gather | solution.py:71
  37.9 0.0 copy-start.4
  37.9 0.0 copy-start.5
  37.9 0.1 reshape.185
  38.0 0.1 broadcast_compare_fusion
  38.1 0.5 copy.124
  38.6 0.1 multiply_cosine_fusion
  38.7 0.1 subtract_convert_fusion
  38.8 0.4 select_reduce_fusion
  39.2 0.2 fusion.6
  39.4 0.2 copy.129
  39.7 0.5 copy.127
  40.2 0.0 slice-start
  40.2 0.4 fusion.7
  40.6 0.2 copy.128
  40.8 0.1 pad_maximum_fusion.1
  41.0 15.9 %all-gather.1 = f32[128,2,4,66]{3,2,1,0:T(4,128)S(1)} all-gather(f32[8,2,4,66]{3,2,1,0:T(4,128)S(1)} %pad_maximum_fusion.1), channel_id=3, replica_groups=mesh['seq'=16,'mlp'=8,'tp'=4] {'seq'}, dimensions={0}, use_global_device_ids=true | all-gather | bytes 287232 | tf_op jit(solution)/shard_map/softmax_merge/all_gather | solution.py:155
  56.9 0.1 copy.149
  57.0 0.1 reshape.188
  57.1 0.1 multiply_subtract_fusion
  57.2 0.1 fusion.25
  57.2 0.2 multiply_reduce_fusion.1
  57.4 0.1 copy.133
  57.5 0.3 fusion.27
  57.8 0.5 copy.146
  58.3 0.5 copy.136
  58.7 0.1 exponential_bitcast_fusion
  58.8 0.1 copy.134
  58.9 0.1 reshape.193
  59.0 0.2 fusion.14
  59.2 0.3 fusion.4
  59.5 0.1 divide_convert_fusion
  59.6 0.1 convert_element_type.89
  59.7 0.1 convolution_convert_fusion
  59.9 0.7 broadcast_in_dim.31
  60.6 6.1 %all-to-all-start = ((bf16[64,8,128]{2,1,0:T(8,128)(2,1)}), bf16[64,8,128]{2,1,0:T(8,128)(2,1)S(1)}, u32[]{:S(2)}, u32[]{:S(2)}) async-start(bf16[64,8,128]{2,1,0:T(8,128)(2,1)} %broadcast_in_dim.31), calls=%async_computation | async-start | bytes 262144 | tf_op jit(solution)/shard_map/output_projection/all_to_all | solution.py:79
  66.7 10.0 %all-to-all-done = bf16[64,8,128]{2,1,0:T(8,128)(2,1)S(1)} async-done(((bf16[64,8,128]{2,1,0:T(8,128)(2,1)}), bf16[64,8,128]{2,1,0:T(8,128)(2,1)S(1)}, u32[]{:S(2)}, u32[]{:S(2)}) %all-to-all-start) | async-done | bytes 131104 | tf_op jit(solution)/shard_map/output_projection/all_to_all | solution.py:79
  76.8 0.1 multiply_reduce_fusion
  76.9 0.0 all-gather.5.cloned.1.call-done
  76.9 1.3 %fusion.26 = (bf16[8,256,128]{2,1,0:T(8,128)(2,1)S(1)}, bf16[8,256,128]{2,1,0:T(8,128)(2,1)S(1)}) fusion(bf16[8,384,256]{2,1,0:T(8,128)(2,1)} %bitcast.60), kind=kLoop, calls=%fused_computation.61 | loop fusion | bytes 2097152 | tf_op jit(solution)/shard_map/slice | solution.py:104
  78.2 0.2 fusion.23
  78.5 1.4 %fusion.2 = f32[8,8,256]{2,0,1:T(8,128)S(1)} fusion(bf16[2048,128]{1,0:T(8,128)(2,1)S(1)} %bitcast.58, bf16[8,384,256]{2,1,0:T(8,128)(2,1)} %bitcast.61, f32[8,128]{1,0:T(8,128)S(1)} %fusion.23, bf16[16,8,128]{2,1,0:T(8,128)(2,1)S(1)} %bitcast_reduce_fusion.1, bf16[8,2048]{1,0:T(8,128)(2,1)S(1)} %copy-done.3, f32[2048]{0:T(1024)S(1)} %convert_element_type.94, ...), kind=kOutput, calls=%fused_computation.5 | convolution fusion | flops 8493056 | bytes 1191968 | tf_op jit(solution)/shard_map/feed_forward/rh,jhc->rjc/dot_general | solution.py:197
  79.9 0.1 reshape.192
  80.1 0.2 copy.139
  80.2 0.2 reshape.200
  80.4 14.5 %all_to_all.15 = f32[64,1,256]{2,1,0:T(1,128)S(1)} all-to-all(f32[64,1,256]{2,1,0:T(1,128)S(1)} %reshape.200), channel_id=1, replica_groups=mesh['seq'=16,'mlp'=8,'tp'=4] {'seq','tp'}, dimensions={0} | all-to-all | bytes 131072 | tf_op jit(solution)/shard_map/down_reduction/all_to_all | solution.py:203
  94.9 0.5 broadcast.107
  95.4 0.8 reduce.2
  96.2 0.1 reshape.201
  96.3 0.1 reduce_sum.82
  96.4 0.7 reshape.202
  97.1 5.3 %all-to-all-start.2 = ((bf16[64,2,128]{2,1,0:T(2,128)(2,1)}), bf16[64,2,128]{2,1,0:T(2,128)(2,1)S(1)}, u32[]{:S(2)}, u32[]{:S(2)}) async-start(bf16[64,2,128]{2,1,0:T(2,128)(2,1)} %reshape.202), calls=%async_computation.2 | async-start | bytes 65536 | tf_op jit(solution)/shard_map/down_reduction/all_to_all | solution.py:79
  102.5 0.7 convert_element_type.102
  103.1 8.6 %all-to-all-done.2 = bf16[64,2,128]{2,1,0:T(2,128)(2,1)S(1)} async-done(((bf16[64,2,128]{2,1,0:T(2,128)(2,1)}), bf16[64,2,128]{2,1,0:T(2,128)(2,1)S(1)}, u32[]{:S(2)}, u32[]{:S(2)}) %all-to-all-start.2) | async-done | bytes 32800 | tf_op jit(solution)/shard_map/down_reduction/all_to_all | solution.py:79
  111.7 0.1 reshape.203
  111.9 0.1 copy.140
  111.9 0.1 reshape.195
  112.1 0.6 add_convert_fusion
  (30 shorter events, 0.2 us)
Async XLA Ops:
  7.2 52.6 %copy-start = (bf16[512,128]{1,0:T(8,128)(2,1)S(1)}, bf16[512,128]{1,0:T(8,128)(2,1)}, u32[]{:S(2)}) copy-start(bf16[512,128]{1,0:T(8,128)(2,1)} %param.21) | copy-start | bytes 393220
  7.2 30.8 %copy-start.7 = (s32[8]{0:T(128)S(1)}, s32[8]{0:T(128)}, u32[]{:S(2)}) copy-start(s32[8]{0:T(128)} %param.14) | copy-start | bytes 100
  7.2 30.9 %copy-start.1 = (bf16[8,512,128]{2,1,0:T(8,128)(2,1)S(1)}, bf16[8,512,128]{2,1,0:T(8,128)(2,1)}, u32[]{:S(2)}) copy-start(bf16[8,512,128]{2,1,0:T(8,128)(2,1)} %param.19) | copy-start | bytes 3145732
  7.2 69.7 %all-gather.5.cloned.1.call-start = ((), (), s32[]{:S(2)}) async-start(), calls=%async_computation.3 | async-start | bytes 1769472 | tf_op jit(solution)/shard_map/mlp_weight_gather/all_gather | solution.py:102
  37.9 1.4 %copy-start.4 = (f32[8,768]{1,0:T(8,128)}, f32[8,768]{1,0:T(8,128)S(1)}, u32[]{:S(2)}) copy-start(f32[8,768]{1,0:T(8,128)S(1)} %bitcast_reduce_fusion) | copy-start | bytes 73732
  37.9 21.0 %copy-start.5 = (bf16[8,128]{1,0:T(8,128)(2,1)}, bf16[8,128]{1,0:T(8,128)(2,1)S(1)}, u32[]{:S(2)}) copy-start(bf16[8,128]{1,0:T(8,128)(2,1)S(1)} %slice.81) | copy-start | bytes 6148
  38.1 1.6 %copy-start.2 = (bf16[8,512,128]{2,1,0:T(8,128)(2,1)S(1)}, bf16[8,512,128]{2,1,0:T(8,128)(2,1)}, u32[]{:S(2)}) copy-start(bf16[8,512,128]{2,1,0:T(8,128)(2,1)} %param.20) | copy-start | bytes 3145732
  40.2 16.8 %slice-start = ((f32[8,768]{1,0:T(8,128)}), f32[8,128]{1,0:T(8,128)S(1)}, s32[]{:S(2)}) async-start(f32[8,768]{1,0:T(8,128)} %copy-done.4), calls=%async_computation.4 | async-start | bytes 8192 | tf_op jit(solution)/shard_map/slice | solution.py:119
  57.8 8.9 %copy-start.6 = (bf16[2048]{0:T(1024)(128)(2,1)S(1)}, bf16[2048]{0:T(1024)(128)(2,1)}, u32[]{:S(2)}) copy-start(bf16[2048]{0:T(1024)(128)(2,1)} %param.22) | copy-start | bytes 12292
  57.8 19.0 %copy-start.3 = (bf16[8,2048]{1,0:T(8,128)(2,1)S(1)}, bf16[8,2048]{1,0:T(8,128)(2,1)}, u32[]{:S(2)}) copy-start(bf16[8,2048]{1,0:T(8,128)(2,1)} %hidden_ref.1) | copy-start | bytes 98308
  60.6 16.2 %all-to-all-start = ((bf16[64,8,128]{2,1,0:T(8,128)(2,1)}), bf16[64,8,128]{2,1,0:T(8,128)(2,1)S(1)}, u32[]{:S(2)}, u32[]{:S(2)}) async-start(bf16[64,8,128]{2,1,0:T(8,128)(2,1)} %broadcast_in_dim.31), calls=%async_computation | async-start | bytes 262144 | tf_op jit(solution)/shard_map/output_projection/all_to_all | solution.py:79
  97.1 14.6 %all-to-all-start.2 = ((bf16[64,2,128]{2,1,0:T(2,128)(2,1)}), bf16[64,2,128]{2,1,0:T(2,128)(2,1)S(1)}, u32[]{:S(2)}, u32[]{:S(2)}) async-start(bf16[64,2,128]{2,1,0:T(2,128)(2,1)} %reshape.202), calls=%async_computation.2 | async-start | bytes 65536 | tf_op jit(solution)/shard_map/down_reduction/all_to_all | solution.py:79
Sparse Core Ops, SparseCore 0:
  10.1 43.2 all-gather.4

commit v8 on v7

--- a/solution.py
+++ b/solution.py
@@ -30,14 +30,16 @@
     )
 
 
-def projection_kernel(block_ref, hidden_ref, gain_ref, query_ref, key_ref, value_ref, out_ref):
+def projection_kernel(
+    block_ref, hidden_ref, gain_ref, query_ref, key_ref, value_ref, out_ref, normed_ref
+):
     width = query_ref.shape[0]
     offset = pl.multiple_of(block_ref[0] * width, width)
     stream = hidden_ref[...].astype(jnp.float32)
     mean_square = jnp.mean(stream * stream, axis=-1, keepdims=True)
-    columns = hidden_ref[:, pl.ds(offset, width)].astype(jnp.float32)
-    gains = gain_ref[:, pl.ds(offset, width)].astype(jnp.float32)
-    normed = (columns * lax.rsqrt(mean_square + 1e-05) * gains).astype(jnp.bfloat16)
+    gains = gain_ref[...].astype(jnp.float32)[None, :]
+    normed_ref[...] = (stream * lax.rsqrt(mean_square + 1e-05) * gains).astype(jnp.bfloat16)
+    normed = normed_ref[:, pl.ds(offset, width)]
     query_width = query_ref.shape[1]
     key_width = key_ref.shape[1]
     out_ref[:, :query_width] = jnp.dot(normed, query_ref[...], preferred_element_type=jnp.float32)
@@ -59,12 +61,13 @@
         out_shape=jax.ShapeDtypeStruct((rows, total), jnp.float32),
         in_specs=[pl.BlockSpec(memory_space=pltpu.SMEM)] + [vmem] * 5,
         out_specs=vmem,
+        scratch_shapes=[pltpu.VMEM((rows, features), jnp.bfloat16)],
         cost_estimate=pl.CostEstimate(
             flops=2 * rows * width * total,
             bytes_accessed=2 * (rows * features + features + width * total) + 4 * rows * total,
             transcendentals=rows,
         ),
-    )(block, hidden, gain.reshape(1, features), query_weight, key_weight, value_weight)
+    )(block, hidden, gain, query_weight, key_weight, value_weight)
 
 
 def gathered_sum(x, axis):

time: 120 us -> 119 us (level)
  local copies, waits for them, and re-layouts: 9.1 us -> 7.81 us
    reshape x1 -> x0, local copies, waits for them, and re-layouts: 1.29 us -> none  [partial_projection(): gain.reshape(1, features)]
  transfers between devices with their start and end apart: 3 -> 3, of which waited for: 2 -> 2; matrix products, arithmetic and copies ran while one was open for 7% -> 6% of each run, Pallas kernels for 2% -> 2%
where the time goes in v8:
time: 119 us; the launch traced here: 118 us
  blocking collectives  56.2 us (47%)
  waiting for transfers between devices  18.6 us (16%)
  between operations  14.4 us (12%)
  starting transfers between devices  11.5 us (10%)
  local copies, waits for them, and re-layouts  7.81 us (7%)
  other arithmetic  5.32 us (4%)
  matrix products  2.63 us (2%)
  Pallas kernels  1.82 us (2%)
    all_gather x1, blocking collectives, gathered_sum(): return jnp.sum(lax.all_gather(x, axis), axis=0)  25.8 us
    all_to_all x2, waiting for transfers between devices, gather_by_exchange(): return lax.all_to_all(copies, axes, 0, 0, tiled=True)  18.6 us
    all_gather x1, blocking collectives, per_device(): every_state = lax.all_gather(state, 'seq')  15.9 us
    all_to_all x1, blocking collectives, per_device(): lax.all_to_all(pieces, ('seq', 'tp'), 0, 0, tiled=True).sum(axis=0)  14.5 us
    all_to_all x2, starting transfers between devices, gather_by_exchange(): return lax.all_to_all(copies, axes, 0, 0, tiled=True)  11.5 us
    unnamed x23, local copies, waits for them, and re-layouts  2.68 us
  transfers between devices with their start and end apart: 3, of which 2 were waited for; matrix products, arithmetic and copies ran while one was open for 6% of the time, Pallas kernels for 2%

profile of v8, /device:TPU:1, one launch (start us, length us, event | category | flops | bytes accessed | tf_op | source)
XLA Modules:
  0.0 118.3 jit_solution(9642576544237356133)
XLA Ops:
  7.2 0.0 copy-start
  7.2 0.0 all-gather.5.cloned.1.call-start
  7.2 1.7 %pad_maximum_fusion = bf16[384,256]{1,0:T(8,128)(2,1)} fusion(bf16[128,256]{1,0:T(8,128)(2,1)} %param.25, bf16[256,128]{1,0:T(8,128)(2,1)} %param.24, bf16[256,128]{1,0:T(8,128)(2,1)} %param.23), kind=kLoop, calls=%fused_computation.12 | loop fusion | flops 589824 | bytes 393216 | tf_op jit(solution)/shard_map/mlp_weight_gather/concatenate | solution.py:102
  8.9 0.0 all-gather.5.cloned.1.call-update
  9.0 1.8 %qkv_projection.1 = f32[8,768]{1,0:T(8,128)} custom-call(s32[1]{0:T(128)} %bitcast.block_ref, bf16[8,2048]{1,0:T(8,128)(2,1)} %hidden_ref.1, bf16[2048]{0:T(1024)(128)(2,1)} %gain_ref.1, bf16[128,512]{1,0:T(8,128)(2,1)} %query_ref.1, bf16[128,128]{1,0:T(8,128)(2,1)} %key_ref.1, bf16[128,128]{1,0:T(8,128)(2,1)} %value_ref.1), custom_call_target="tpu_custom_call" | custom-call | flops 1572864 | bytes 258048 | tf_op jit(solution)/shard_map/qkv_projection/pallas_call | solution.py:59
  10.8 25.8 %all-gather = f32[128,768]{1,0:T(8,128)S(1)} all-gather(f32[8,768]{1,0:T(8,128)} %qkv_projection.1), channel_id=2, replica_groups=mesh['seq'=16,'mlp'=8,'tp'=4] {'seq'}, dimensions={0}, use_global_device_ids=true | all-gather | bytes 417792 | tf_op jit(solution)/shard_map/qkv_projection/all_gather | solution.py:74
  36.6 0.0 copy-start.4
  36.6 0.0 copy-start.5
  36.7 0.1 reshape.181
  36.7 0.1 broadcast_compare_fusion
  36.8 0.5 copy.124
  37.4 0.1 multiply_cosine_fusion
  37.5 0.1 subtract_convert_fusion
  37.6 0.4 select_reduce_fusion
  38.0 0.2 fusion.6
  38.2 0.2 copy.129
  38.4 0.5 copy.127
  38.9 0.0 slice-start
  38.9 0.4 fusion.7
  39.4 0.2 copy.128
  39.6 0.1 pad_maximum_fusion.1
  39.7 15.9 %all-gather.1 = f32[128,2,4,66]{3,2,1,0:T(4,128)S(1)} all-gather(f32[8,2,4,66]{3,2,1,0:T(4,128)S(1)} %pad_maximum_fusion.1), channel_id=3, replica_groups=mesh['seq'=16,'mlp'=8,'tp'=4] {'seq'}, dimensions={0}, use_global_device_ids=true | all-gather | bytes 287232 | tf_op jit(solution)/shard_map/softmax_merge/all_gather | solution.py:158
  55.6 0.1 copy.149
  55.7 0.1 reshape.184
  55.8 0.1 multiply_subtract_fusion
  55.9 0.1 fusion.25
  56.0 0.2 multiply_reduce_fusion.1
  56.1 0.1 copy.133
  56.2 0.3 fusion.27
  56.5 0.0 copy-start.6
  56.5 0.5 copy.146
  57.0 0.5 copy.136
  57.5 0.1 exponential_bitcast_fusion
  57.6 0.1 copy.134
  57.6 0.1 reshape.189
  57.7 0.2 fusion.14
  57.9 0.3 fusion.4
  58.3 0.1 divide_convert_fusion
  58.4 0.1 convert_element_type.89
  58.5 0.1 convolution_convert_fusion
  58.6 0.7 broadcast_in_dim.31
  59.3 6.1 %all-to-all-start = ((bf16[64,8,128]{2,1,0:T(8,128)(2,1)}), bf16[64,8,128]{2,1,0:T(8,128)(2,1)S(1)}, u32[]{:S(2)}, u32[]{:S(2)}) async-start(bf16[64,8,128]{2,1,0:T(8,128)(2,1)} %broadcast_in_dim.31), calls=%async_computation | async-start | bytes 262144 | tf_op jit(solution)/shard_map/output_projection/all_to_all | solution.py:82
  65.4 10.0 %all-to-all-done = bf16[64,8,128]{2,1,0:T(8,128)(2,1)S(1)} async-done(((bf16[64,8,128]{2,1,0:T(8,128)(2,1)}), bf16[64,8,128]{2,1,0:T(8,128)(2,1)S(1)}, u32[]{:S(2)}, u32[]{:S(2)}) %all-to-all-start) | async-done | bytes 131104 | tf_op jit(solution)/shard_map/output_projection/all_to_all | solution.py:82
  75.5 0.1 multiply_reduce_fusion
  75.6 0.0 all-gather.5.cloned.1.call-done
  75.7 1.3 %fusion.26 = (bf16[8,256,128]{2,1,0:T(8,128)(2,1)S(1)}, bf16[8,256,128]{2,1,0:T(8,128)(2,1)S(1)}) fusion(bf16[8,384,256]{2,1,0:T(8,128)(2,1)} %bitcast.60), kind=kLoop, calls=%fused_computation.61 | loop fusion | bytes 2097152 | tf_op jit(solution)/shard_map/slice | solution.py:107
  77.0 0.2 fusion.23
  77.2 1.4 %fusion.2 = f32[8,8,256]{2,0,1:T(8,128)S(1)} fusion(bf16[2048,128]{1,0:T(8,128)(2,1)S(1)} %bitcast.58, bf16[8,384,256]{2,1,0:T(8,128)(2,1)} %bitcast.61, f32[8,128]{1,0:T(8,128)S(1)} %fusion.23, bf16[16,8,128]{2,1,0:T(8,128)(2,1)S(1)} %bitcast_reduce_fusion.1, bf16[8,2048]{1,0:T(8,128)(2,1)S(1)} %copy-done.3, f32[2048]{0:T(1024)S(1)} %convert_element_type.94, ...), kind=kOutput, calls=%fused_computation.5 | convolution fusion | flops 8493056 | bytes 1191968 | tf_op jit(solution)/shard_map/feed_forward/rh,jhc->rjc/dot_general | solution.py:200
  78.7 0.1 reshape.188
  78.8 0.2 copy.139
  78.9 0.2 reshape.196
  79.1 14.5 %all_to_all.15 = f32[64,1,256]{2,1,0:T(1,128)S(1)} all-to-all(f32[64,1,256]{2,1,0:T(1,128)S(1)} %reshape.196), channel_id=1, replica_groups=mesh['seq'=16,'mlp'=8,'tp'=4] {'seq','tp'}, dimensions={0} | all-to-all | bytes 131072 | tf_op jit(solution)/shard_map/down_reduction/all_to_all | solution.py:206
  93.6 0.5 broadcast.107
  94.1 0.8 reduce.2
  94.9 0.1 reshape.197
  95.0 0.1 reduce_sum.82
  95.1 0.7 reshape.198
  95.9 5.3 %all-to-all-start.2 = ((bf16[64,2,128]{2,1,0:T(2,128)(2,1)}), bf16[64,2,128]{2,1,0:T(2,128)(2,1)S(1)}, u32[]{:S(2)}, u32[]{:S(2)}) async-start(bf16[64,2,128]{2,1,0:T(2,128)(2,1)} %reshape.198), calls=%async_computation.2 | async-start | bytes 65536 | tf_op jit(solution)/shard_map/down_reduction/all_to_all | solution.py:82
  101.2 0.7 convert_element_type.102
  101.9 8.6 %all-to-all-done.2 = bf16[64,2,128]{2,1,0:T(2,128)(2,1)S(1)} async-done(((bf16[64,2,128]{2,1,0:T(2,128)(2,1)}), bf16[64,2,128]{2,1,0:T(2,128)(2,1)S(1)}, u32[]{:S(2)}, u32[]{:S(2)}) %all-to-all-start.2) | async-done | bytes 32800 | tf_op jit(solution)/shard_map/down_reduction/all_to_all | solution.py:82
  110.4 0.1 reshape.199
  110.6 0.1 copy.140
  110.6 0.1 reshape.191
  110.8 0.6 add_convert_fusion
  (29 shorter events, 0.2 us)
Async XLA Ops:
  7.2 51.3 %copy-start = (bf16[512,128]{1,0:T(8,128)(2,1)S(1)}, bf16[512,128]{1,0:T(8,128)(2,1)}, u32[]{:S(2)}) copy-start(bf16[512,128]{1,0:T(8,128)(2,1)} %param.21) | copy-start | bytes 393220
  7.2 29.5 %copy-start.7 = (s32[8]{0:T(128)S(1)}, s32[8]{0:T(128)}, u32[]{:S(2)}) copy-start(s32[8]{0:T(128)} %param.14) | copy-start | bytes 100
  7.2 29.6 %copy-start.1 = (bf16[8,512,128]{2,1,0:T(8,128)(2,1)S(1)}, bf16[8,512,128]{2,1,0:T(8,128)(2,1)}, u32[]{:S(2)}) copy-start(bf16[8,512,128]{2,1,0:T(8,128)(2,1)} %param.19) | copy-start | bytes 3145732
  7.2 68.5 %all-gather.5.cloned.1.call-start = ((), (), s32[]{:S(2)}) async-start(), calls=%async_computation.3 | async-start | bytes 1769472 | tf_op jit(solution)/shard_map/mlp_weight_gather/all_gather | solution.py:105
  36.6 1.4 %copy-start.4 = (f32[8,768]{1,0:T(8,128)}, f32[8,768]{1,0:T(8,128)S(1)}, u32[]{:S(2)}) copy-start(f32[8,768]{1,0:T(8,128)S(1)} %bitcast_reduce_fusion) | copy-start | bytes 73732
  36.6 21.0 %copy-start.5 = (bf16[8,128]{1,0:T(8,128)(2,1)}, bf16[8,128]{1,0:T(8,128)(2,1)S(1)}, u32[]{:S(2)}) copy-start(bf16[8,128]{1,0:T(8,128)(2,1)S(1)} %slice.81) | copy-start | bytes 6148
  36.8 1.6 %copy-start.2 = (bf16[8,512,128]{2,1,0:T(8,128)(2,1)S(1)}, bf16[8,512,128]{2,1,0:T(8,128)(2,1)}, u32[]{:S(2)}) copy-start(bf16[8,512,128]{2,1,0:T(8,128)(2,1)} %param.20) | copy-start | bytes 3145732
  38.9 16.8 %slice-start = ((f32[8,768]{1,0:T(8,128)}), f32[8,128]{1,0:T(8,128)S(1)}, s32[]{:S(2)}) async-start(f32[8,768]{1,0:T(8,128)} %copy-done.4), calls=%async_computation.4 | async-start | bytes 8192 | tf_op jit(solution)/shard_map/slice | solution.py:122
  56.5 8.9 %copy-start.6 = (bf16[2048]{0:T(1024)(128)(2,1)S(1)}, bf16[2048]{0:T(1024)(128)(2,1)}, u32[]{:S(2)}) copy-start(bf16[2048]{0:T(1024)(128)(2,1)} %param.22) | copy-start | bytes 12292
  56.5 19.0 %copy-start.3 = (bf16[8,2048]{1,0:T(8,128)(2,1)S(1)}, bf16[8,2048]{1,0:T(8,128)(2,1)}, u32[]{:S(2)}) copy-start(bf16[8,2048]{1,0:T(8,128)(2,1)} %hidden_ref.1) | copy-start | bytes 98308
  59.3 16.2 %all-to-all-start = ((bf16[64,8,128]{2,1,0:T(8,128)(2,1)}), bf16[64,8,128]{2,1,0:T(8,128)(2,1)S(1)}, u32[]{:S(2)}, u32[]{:S(2)}) async-start(bf16[64,8,128]{2,1,0:T(8,128)(2,1)} %broadcast_in_dim.31), calls=%async_computation | async-start | bytes 262144 | tf_op jit(solution)/shard_map/output_projection/all_to_all | solution.py:82
  95.9 14.6 %all-to-all-start.2 = ((bf16[64,2,128]{2,1,0:T(2,128)(2,1)}), bf16[64,2,128]{2,1,0:T(2,128)(2,1)S(1)}, u32[]{:S(2)}, u32[]{:S(2)}) async-start(bf16[64,2,128]{2,1,0:T(2,128)(2,1)} %reshape.198), calls=%async_computation.2 | async-start | bytes 65536 | tf_op jit(solution)/shard_map/down_reduction/all_to_all | solution.py:82
Sparse Core Ops, SparseCore 0:
  10.1 43.1 all-gather.4

commit v9 on v8

--- a/solution.py
+++ b/solution.py
@@ -31,8 +31,23 @@
 
 
 def projection_kernel(
-    block_ref, hidden_ref, gain_ref, query_ref, key_ref, value_ref, out_ref, normed_ref
+    block_ref,
+    hidden_ref,
+    gain_ref,
+    query_ref,
+    key_ref,
+    value_ref,
+    gate_ref,
+    up_ref,
+    down_ref,
+    out_ref,
+    slab_ref,
+    normed_ref,
 ):
+    slab_rows, hidden_units = gate_ref.shape
+    slab_ref[:slab_rows, :hidden_units] = gate_ref[...]
+    slab_ref[:slab_rows, hidden_units:] = up_ref[...]
+    slab_ref[slab_rows:, :] = down_ref[...]
     width = query_ref.shape[0]
     offset = pl.multiple_of(block_ref[0] * width, width)
     stream = hidden_ref[...].astype(jnp.float32)
@@ -51,23 +66,29 @@
     )
 
 
-def partial_projection(block, hidden, gain, query_weight, key_weight, value_weight):
+def partial_projection(block, hidden, gain, query_weight, key_weight, value_weight, gate, up, down):
     rows, features = hidden.shape
     width = query_weight.shape[0]
     total = query_weight.shape[1] + key_weight.shape[1] + value_weight.shape[1]
+    slab_shape = (gate.shape[0] + down.shape[0], gate.shape[1] + up.shape[1])
     vmem = pl.BlockSpec(memory_space=pltpu.VMEM)
     return pl.pallas_call(
         projection_kernel,
-        out_shape=jax.ShapeDtypeStruct((rows, total), jnp.float32),
-        in_specs=[pl.BlockSpec(memory_space=pltpu.SMEM)] + [vmem] * 5,
-        out_specs=vmem,
+        out_shape=(
+            jax.ShapeDtypeStruct((rows, total), jnp.float32),
+            jax.ShapeDtypeStruct(slab_shape, gate.dtype),
+        ),
+        in_specs=[pl.BlockSpec(memory_space=pltpu.SMEM)] + [vmem] * 8,
+        out_specs=(vmem, vmem),
         scratch_shapes=[pltpu.VMEM((rows, features), jnp.bfloat16)],
         cost_estimate=pl.CostEstimate(
             flops=2 * rows * width * total,
-            bytes_accessed=2 * (rows * features + features + width * total) + 4 * rows * total,
+            bytes_accessed=2 * (rows * features + features + width * total)
+            + 4 * rows * total
+            + 4 * slab_shape[0] * slab_shape[1],
             transcendentals=rows,
         ),
-    )(block, hidden, gain, query_weight, key_weight, value_weight)
+    )(block, hidden, gain, query_weight, key_weight, value_weight, gate, up, down)
 
 
 def gathered_sum(x, axis):
@@ -97,26 +118,31 @@
     up_weight,
     down_weight,
 ):
+    requests = hidden.shape[0]
+    stream = hidden.astype(jnp.float32)
+    query_width = query_weight.shape[1]
+    key_width = key_weight.shape[1]
     slab_rows, hidden_units = gate_weight.shape
+    with jax.named_scope("qkv_projection"):
+        block = lax.axis_index("seq").astype(jnp.int32).reshape(1)
+        partial, slab = partial_projection(
+            block,
+            hidden,
+            attention_gain,
+            query_weight,
+            key_weight,
+            value_weight,
+            gate_weight,
+            up_weight,
+            down_weight,
+        )
     with jax.named_scope("mlp_weight_gather"):
-        slab = jnp.concatenate(
-            [jnp.concatenate([gate_weight, up_weight], axis=1), down_weight], axis=0
-        )
         blocks = lax.all_gather(slab, "mlp")
     slabs = blocks.shape[0]
     gate_full = blocks[:, :slab_rows, :hidden_units].reshape(slabs * slab_rows, hidden_units)
     up_full = blocks[:, :slab_rows, hidden_units:].reshape(slabs * slab_rows, hidden_units)
     down_blocks = blocks[:, slab_rows:, :]
-
-    requests = hidden.shape[0]
-    stream = hidden.astype(jnp.float32)
-    query_width = query_weight.shape[1]
-    key_width = key_weight.shape[1]
     with jax.named_scope("qkv_projection"):
-        block = lax.axis_index("seq").astype(jnp.int32).reshape(1)
-        partial = partial_projection(
-            block, hidden, attention_gain, query_weight, key_weight, value_weight
-        )
         total = gathered_sum(partial, "seq")
     queries_raw = total[:, :query_width]
     keys_raw = total[:, query_width : query_width + key_width]

time: 119 us -> 117 us (0.983)
  other arithmetic: 5.32 us -> 3.65 us
    concatenate x1 -> x0, other arithmetic: 1.68 us -> none  [per_device(): jnp.concatenate([jnp.concatenate([gate_weight, up_weight], axis=1), down_...]
  transfers between devices with their start and end apart: 3 -> 3, of which waited for: 2 -> 2; matrix products, arithmetic and copies ran while one was open for 6% -> 6% of each run, Pallas kernels for 2% -> 0%
where the time goes in v9:
time: 117 us
  blocking collectives  56.2 us (48%)
  waiting for transfers between devices  18.6 us (16%)
  between operations  14.4 us (12%)
  starting transfers between devices  11.5 us (10%)
  local copies, waits for them, and re-layouts  7.81 us (7%)
  other arithmetic  3.65 us (3%)
  matrix products  2.63 us (2%)
  Pallas kernels  1.97 us (2%)
    all_gather x1, blocking collectives, gathered_sum(): return jnp.sum(lax.all_gather(x, axis), axis=0)  25.8 us
    all_to_all x2, waiting for transfers between devices, gather_by_exchange(): return lax.all_to_all(copies, axes, 0, 0, tiled=True)  18.6 us
    all_gather x1, blocking collectives, per_device(): every_state = lax.all_gather(state, 'seq')  15.9 us
    all_to_all x1, blocking collectives, per_device(): lax.all_to_all(pieces, ('seq', 'tp'), 0, 0, tiled=True).sum(axis=0)  14.5 us
    all_to_all x2, starting transfers between devices, gather_by_exchange(): return lax.all_to_all(copies, axes, 0, 0, tiled=True)  11.5 us
    unnamed x23, local copies, waits for them, and re-layouts  2.68 us
  transfers between devices with their start and end apart: 3, of which 2 were waited for; matrix products, arithmetic and copies ran while one was open for 6% of the time, Pallas kernels for 0%

profile of v9, /device:TPU:1, one launch (start us, length us, event | category | flops | bytes accessed | tf_op | source)
XLA Modules:
  0.0 116.8 jit_solution(4742620819953819362)
XLA Ops:
  7.2 0.0 copy-start
  7.2 0.0 all-gather.5.cloned.1.call-start
  7.3 2.0 %qkv_projection.1 = (f32[8,768]{1,0:T(8,128)}, bf16[384,256]{1,0:T(8,128)(2,1)}) custom-call(s32[1]{0:T(128)} %bitcast.block_ref, bf16[8,2048]{1,0:T(8,128)(2,1)} %hidden_ref.1, bf16[2048]{0:T(1024)(128)(2,1)} %gain_ref.1, bf16[128,512]{1,0:T(8,128)(2,1)} %query_ref.1, bf16[128,128]{1,0:T(8,128)(2,1)} %key_ref.1, bf16[128,128]{1,0:T(8,128)(2,1)} %value_ref.1, ...), custom_call_target="tpu_custom_call" | custom-call | flops 1572864 | bytes 651264 | tf_op jit(solution)/shard_map/qkv_projection/pallas_call | solution.py:75
  9.2 0.0 all-gather.5.cloned.1.call-update
  9.3 25.8 %all-gather = f32[128,768]{1,0:T(8,128)S(1)} all-gather(f32[8,768]{1,0:T(8,128)} %get-tuple-element.5), channel_id=2, replica_groups=mesh['seq'=16,'mlp'=8,'tp'=4] {'seq'}, dimensions={0}, use_global_device_ids=true | all-gather | bytes 417792 | tf_op jit(solution)/shard_map/qkv_projection/all_gather | solution.py:95
  35.1 0.0 copy-start.4
  35.1 0.0 copy-start.5
  35.1 0.1 reshape.181
  35.2 0.1 broadcast_compare_fusion
  35.3 0.5 copy.124
  35.8 0.1 multiply_cosine_fusion
  36.0 0.1 subtract_convert_fusion
  36.1 0.4 select_reduce_fusion
  36.5 0.2 fusion.6
  36.7 0.2 copy.129
  36.9 0.5 copy.127
  37.4 0.0 slice-start
  37.4 0.4 fusion.7
  37.9 0.2 copy.128
  38.1 0.1 pad_maximum_fusion
  38.2 15.9 %all-gather.1 = f32[128,2,4,66]{3,2,1,0:T(4,128)S(1)} all-gather(f32[8,2,4,66]{3,2,1,0:T(4,128)S(1)} %pad_maximum_fusion), channel_id=3, replica_groups=mesh['seq'=16,'mlp'=8,'tp'=4] {'seq'}, dimensions={0}, use_global_device_ids=true | all-gather | bytes 287232 | tf_op jit(solution)/shard_map/softmax_merge/all_gather | solution.py:184
  54.1 0.1 copy.149
  54.2 0.1 reshape.184
  54.3 0.1 multiply_subtract_fusion
  54.4 0.1 fusion.25
  54.5 0.2 multiply_reduce_fusion.1
  54.6 0.1 copy.133
  54.7 0.3 fusion.27
  55.0 0.0 copy-start.6
  55.0 0.0 copy-start.3
  55.0 0.5 copy.136
  55.5 0.5 copy.146
  56.0 0.1 exponential_bitcast_fusion
  56.1 0.1 copy.134
  56.1 0.1 reshape.189
  56.2 0.2 fusion.14
  56.4 0.3 fusion.4
  56.8 0.1 divide_convert_fusion
  56.9 0.1 convert_element_type.89
  57.0 0.1 convolution_convert_fusion
  57.1 0.7 broadcast_in_dim.31
  57.8 6.1 %all-to-all-start = ((bf16[64,8,128]{2,1,0:T(8,128)(2,1)}), bf16[64,8,128]{2,1,0:T(8,128)(2,1)S(1)}, u32[]{:S(2)}, u32[]{:S(2)}) async-start(bf16[64,8,128]{2,1,0:T(8,128)(2,1)} %broadcast_in_dim.31), calls=%async_computation | async-start | bytes 262144 | tf_op jit(solution)/shard_map/output_projection/all_to_all | solution.py:103
  63.9 10.0 %all-to-all-done = bf16[64,8,128]{2,1,0:T(8,128)(2,1)S(1)} async-done(((bf16[64,8,128]{2,1,0:T(8,128)(2,1)}), bf16[64,8,128]{2,1,0:T(8,128)(2,1)S(1)}, u32[]{:S(2)}, u32[]{:S(2)}) %all-to-all-start) | async-done | bytes 131104 | tf_op jit(solution)/shard_map/output_projection/all_to_all | solution.py:103
  74.0 0.1 multiply_reduce_fusion
  74.1 0.0 all-gather.5.cloned.1.call-done
  74.2 1.3 %fusion.26 = (bf16[8,256,128]{2,1,0:T(8,128)(2,1)S(1)}, bf16[8,256,128]{2,1,0:T(8,128)(2,1)S(1)}) fusion(bf16[8,384,256]{2,1,0:T(8,128)(2,1)} %bitcast.60), kind=kLoop, calls=%fused_computation.60 | loop fusion | bytes 2097152 | tf_op jit(solution)/shard_map/slice | solution.py:142
  75.4 0.2 fusion.23
  75.7 1.4 %fusion.2 = f32[8,8,256]{2,0,1:T(8,128)S(1)} fusion(bf16[2048,128]{1,0:T(8,128)(2,1)S(1)} %bitcast.58, bf16[8,384,256]{2,1,0:T(8,128)(2,1)} %bitcast.61, f32[8,128]{1,0:T(8,128)S(1)} %fusion.23, bf16[16,8,128]{2,1,0:T(8,128)(2,1)S(1)} %bitcast_reduce_fusion.1, bf16[8,2048]{1,0:T(8,128)(2,1)S(1)} %copy-done.3, f32[2048]{0:T(1024)S(1)} %convert_element_type.94, ...), kind=kOutput, calls=%fused_computation.5 | convolution fusion | flops 8493056 | bytes 1191968 | tf_op jit(solution)/shard_map/feed_forward/rh,jhc->rjc/dot_general | solution.py:226
  77.2 0.1 reshape.188
  77.3 0.2 copy.139
  77.4 0.2 reshape.196
  77.6 14.5 %all_to_all.15 = f32[64,1,256]{2,1,0:T(1,128)S(1)} all-to-all(f32[64,1,256]{2,1,0:T(1,128)S(1)} %reshape.196), channel_id=1, replica_groups=mesh['seq'=16,'mlp'=8,'tp'=4] {'seq','tp'}, dimensions={0} | all-to-all | bytes 131072 | tf_op jit(solution)/shard_map/down_reduction/all_to_all | solution.py:232
  92.1 0.5 broadcast.107
  92.6 0.8 reduce.2
  93.4 0.1 reshape.197
  93.5 0.1 reduce_sum.82
  93.6 0.7 reshape.198
  94.4 5.3 %all-to-all-start.2 = ((bf16[64,2,128]{2,1,0:T(2,128)(2,1)}), bf16[64,2,128]{2,1,0:T(2,128)(2,1)S(1)}, u32[]{:S(2)}, u32[]{:S(2)}) async-start(bf16[64,2,128]{2,1,0:T(2,128)(2,1)} %reshape.198), calls=%async_computation.2 | async-start | bytes 65536 | tf_op jit(solution)/shard_map/down_reduction/all_to_all | solution.py:103
  99.7 0.7 convert_element_type.102
  100.4 8.6 %all-to-all-done.2 = bf16[64,2,128]{2,1,0:T(2,128)(2,1)S(1)} async-done(((bf16[64,2,128]{2,1,0:T(2,128)(2,1)}), bf16[64,2,128]{2,1,0:T(2,128)(2,1)S(1)}, u32[]{:S(2)}, u32[]{:S(2)}) %all-to-all-start.2) | async-done | bytes 32800 | tf_op jit(solution)/shard_map/down_reduction/all_to_all | solution.py:103
  108.9 0.1 reshape.199
  109.1 0.1 copy.140
  109.1 0.1 reshape.191
  109.3 0.6 add_convert_fusion
  (28 shorter events, 0.2 us)
Async XLA Ops:
  7.2 49.8 %copy-start = (bf16[512,128]{1,0:T(8,128)(2,1)S(1)}, bf16[512,128]{1,0:T(8,128)(2,1)}, u32[]{:S(2)}) copy-start(bf16[512,128]{1,0:T(8,128)(2,1)} %param.21) | copy-start | bytes 393220
  7.2 28.0 %copy-start.7 = (s32[8]{0:T(128)S(1)}, s32[8]{0:T(128)}, u32[]{:S(2)}) copy-start(s32[8]{0:T(128)} %param.14) | copy-start | bytes 100
  7.2 28.1 %copy-start.1 = (bf16[8,512,128]{2,1,0:T(8,128)(2,1)S(1)}, bf16[8,512,128]{2,1,0:T(8,128)(2,1)}, u32[]{:S(2)}) copy-start(bf16[8,512,128]{2,1,0:T(8,128)(2,1)} %param.19) | copy-start | bytes 3145732
  7.2 67.0 %all-gather.5.cloned.1.call-start = ((), (), s32[]{:S(2)}) async-start(), calls=%async_computation.3 | async-start | bytes 1769472 | tf_op jit(solution)/shard_map/mlp_weight_gather/all_gather | solution.py:140
  35.1 1.4 %copy-start.4 = (f32[8,768]{1,0:T(8,128)}, f32[8,768]{1,0:T(8,128)S(1)}, u32[]{:S(2)}) copy-start(f32[8,768]{1,0:T(8,128)S(1)} %bitcast_reduce_fusion) | copy-start | bytes 73732
  35.1 21.0 %copy-start.5 = (bf16[8,128]{1,0:T(8,128)(2,1)}, bf16[8,128]{1,0:T(8,128)(2,1)S(1)}, u32[]{:S(2)}) copy-start(bf16[8,128]{1,0:T(8,128)(2,1)S(1)} %slice.81) | copy-start | bytes 6148
  35.3 1.6 %copy-start.2 = (bf16[8,512,128]{2,1,0:T(8,128)(2,1)S(1)}, bf16[8,512,128]{2,1,0:T(8,128)(2,1)}, u32[]{:S(2)}) copy-start(bf16[8,512,128]{2,1,0:T(8,128)(2,1)} %param.20) | copy-start | bytes 3145732
  37.4 16.8 %slice-start = ((f32[8,768]{1,0:T(8,128)}), f32[8,128]{1,0:T(8,128)S(1)}, s32[]{:S(2)}) async-start(f32[8,768]{1,0:T(8,128)} %copy-done.4), calls=%async_computation.4 | async-start | bytes 8192 | tf_op jit(solution)/shard_map/slice | solution.py:148
  55.0 8.9 %copy-start.6 = (bf16[2048]{0:T(1024)(128)(2,1)S(1)}, bf16[2048]{0:T(1024)(128)(2,1)}, u32[]{:S(2)}) copy-start(bf16[2048]{0:T(1024)(128)(2,1)} %param.22) | copy-start | bytes 12292
  55.0 19.0 %copy-start.3 = (bf16[8,2048]{1,0:T(8,128)(2,1)S(1)}, bf16[8,2048]{1,0:T(8,128)(2,1)}, u32[]{:S(2)}) copy-start(bf16[8,2048]{1,0:T(8,128)(2,1)} %hidden_ref.1) | copy-start | bytes 98308
  57.8 16.2 %all-to-all-start = ((bf16[64,8,128]{2,1,0:T(8,128)(2,1)}), bf16[64,8,128]{2,1,0:T(8,128)(2,1)S(1)}, u32[]{:S(2)}, u32[]{:S(2)}) async-start(bf16[64,8,128]{2,1,0:T(8,128)(2,1)} %broadcast_in_dim.31), calls=%async_computation | async-start | bytes 262144 | tf_op jit(solution)/shard_map/output_projection/all_to_all | solution.py:103
  94.4 14.6 %all-to-all-start.2 = ((bf16[64,2,128]{2,1,0:T(2,128)(2,1)}), bf16[64,2,128]{2,1,0:T(2,128)(2,1)S(1)}, u32[]{:S(2)}, u32[]{:S(2)}) async-start(bf16[64,2,128]{2,1,0:T(2,128)(2,1)} %reshape.198), calls=%async_computation.2 | async-start | bytes 65536 | tf_op jit(solution)/shard_map/down_reduction/all_to_all | solution.py:103
Sparse Core Ops, SparseCore 0:
  10.1 43.2 all-gather.4

commit v10 on v9

--- a/solution.py
+++ b/solution.py
@@ -89,6 +89,46 @@
             transcendentals=rows,
         ),
     )(block, hidden, gain, query_weight, key_weight, value_weight, gate, up, down)
+
+
+def feed_forward_kernel(input_ref, blocks_ref, out_ref):
+    slabs = blocks_ref.shape[0]
+    slab_rows = blocks_ref.shape[1] - blocks_ref.shape[2] // 2
+    hidden_units = blocks_ref.shape[2] // 2
+    gate = None
+    upward = None
+    for j in range(slabs):
+        rows = input_ref[:, j * slab_rows : (j + 1) * slab_rows]
+        gate_part = jnp.dot(
+            rows, blocks_ref[j, :slab_rows, :hidden_units], preferred_element_type=jnp.float32
+        )
+        up_part = jnp.dot(
+            rows, blocks_ref[j, :slab_rows, hidden_units:], preferred_element_type=jnp.float32
+        )
+        gate = gate_part if gate is None else gate + gate_part
+        upward = up_part if upward is None else upward + up_part
+    activated = (jax.nn.silu(gate) * upward).astype(jnp.bfloat16)
+    for j in range(slabs):
+        out_ref[:, j * slab_rows : (j + 1) * slab_rows] = jnp.dot(
+            activated, blocks_ref[j, slab_rows:, :], preferred_element_type=jnp.float32
+        )
+
+
+def feed_forward(mlp_input, blocks):
+    rows, features = mlp_input.shape
+    slabs, slab_height, slab_width = blocks.shape
+    vmem = pl.BlockSpec(memory_space=pltpu.VMEM)
+    return pl.pallas_call(
+        feed_forward_kernel,
+        out_shape=jax.ShapeDtypeStruct((rows, features), jnp.float32),
+        in_specs=[vmem, vmem],
+        out_specs=vmem,
+        cost_estimate=pl.CostEstimate(
+            flops=2 * rows * slabs * slab_height * slab_width,
+            bytes_accessed=2 * rows * features + 2 * slabs * slab_height * slab_width + 4 * rows * features,
+            transcendentals=rows * slab_width // 2,
+        ),
+    )(mlp_input, blocks)
 
 
 def gathered_sum(x, axis):
@@ -138,10 +178,6 @@
         )
     with jax.named_scope("mlp_weight_gather"):
         blocks = lax.all_gather(slab, "mlp")
-    slabs = blocks.shape[0]
-    gate_full = blocks[:, :slab_rows, :hidden_units].reshape(slabs * slab_rows, hidden_units)
-    up_full = blocks[:, :slab_rows, hidden_units:].reshape(slabs * slab_rows, hidden_units)
-    down_blocks = blocks[:, slab_rows:, :]
     with jax.named_scope("qkv_projection"):
         total = gathered_sum(partial, "seq")
     queries_raw = total[:, :query_width]
@@ -220,12 +256,7 @@
     mixed_stream = stream + projected.astype(jnp.float32)
     mlp_input = rms_norm(mixed_stream, feedforward_gain).astype(jnp.bfloat16)
     with jax.named_scope("feed_forward"):
-        gate = jnp.dot(mlp_input, gate_full, preferred_element_type=jnp.float32)
-        upward = jnp.dot(mlp_input, up_full, preferred_element_type=jnp.float32)
-        activated = (jax.nn.silu(gate) * upward).astype(jnp.bfloat16)
-        down_part = jnp.einsum(
-            "rh,jhc->rjc", activated, down_blocks, preferred_element_type=jnp.float32
-        ).reshape(requests, slabs * slab_rows)
+        down_part = feed_forward(mlp_input, blocks)
     with jax.named_scope("down_reduction"):
         reducers = lax.axis_size("seq") * lax.axis_size("tp")
         pieces = down_part.reshape(requests, reducers, -1).transpose(1, 0, 2)

time: 117 us -> 118 us (level)
  Pallas kernels: 1.97 us -> 4.44 us
  matrix products: 2.63 us -> 0.96 us
    pallas_call x0 -> x1, Pallas kernels: none -> 2.47 us  [feed_forward(): pl.pallas_call(feed_forward_kernel, out_shape=jax.ShapeDtypeStruct((rows,...]
    dot_general x2 -> x0, matrix products: 1.67 us -> none  [the longest x1 1.44 us: per_device(): jnp.einsum('rh,jhc->rjc', activated, down_blocks, preferred_element_type=...]
    slice x1 -> x0, local copies, waits for them, and re-layouts: 1.28 us -> none  [per_device(): blocks[:, :slab_rows, :hidden_units]]
  transfers between devices with their start and end apart: 3 -> 3, of which waited for: 2 -> 2; matrix products, arithmetic and copies ran while one was open for 6% -> 7% of each run, Pallas kernels for 0% -> 0%
where the time goes in v10:
time: 118 us
  blocking collectives  56.2 us (48%)
  waiting for transfers between devices  18.6 us (16%)
  between operations  14.4 us (12%)
  starting transfers between devices  11.5 us (10%)
  local copies, waits for them, and re-layouts  7.35 us (6%)
  Pallas kernels  4.44 us (4%)
  other arithmetic  4.35 us (4%)
    all_gather x1, blocking collectives, gathered_sum(): return jnp.sum(lax.all_gather(x, axis), axis=0)  25.8 us
    all_to_all x2, waiting for transfers between devices, gather_by_exchange(): return lax.all_to_all(copies, axes, 0, 0, tiled=True)  18.6 us
    all_gather x1, blocking collectives, per_device(): every_state = lax.all_gather(state, 'seq')  15.9 us
    all_to_all x1, blocking collectives, per_device(): lax.all_to_all(pieces, ('seq', 'tp'), 0, 0, tiled=True).sum(axis=0)  14.5 us
    all_to_all x2, starting transfers between devices, gather_by_exchange(): return lax.all_to_all(copies, axes, 0, 0, tiled=True)  11.5 us
    unnamed x23, local copies, waits for them, and re-layouts  2.68 us
    pallas_call x1, Pallas kernels, feed_forward(): pl.pallas_call(feed_forward_kernel, out_shape=jax.ShapeDtypeStruct((rows,...  2.47 us
  transfers between devices with their start and end apart: 3, of which 2 were waited for; matrix products, arithmetic and copies ran while one was open for 7% of the time, Pallas kernels for 0%

profile of v10, /device:TPU:1, one launch (start us, length us, event | category | flops | bytes accessed | tf_op | source)
XLA Modules:
  0.0 117.8 jit_solution(11315635852240803045)
XLA Ops:
  7.2 0.0 copy-start
  7.2 0.0 all-gather.5.cloned.1.call-start
  7.3 2.0 %qkv_projection.1 = (f32[8,768]{1,0:T(8,128)}, bf16[384,256]{1,0:T(8,128)(2,1)}) custom-call(s32[1]{0:T(128)} %bitcast.block_ref, bf16[8,2048]{1,0:T(8,128)(2,1)} %hidden_ref.1, bf16[2048]{0:T(1024)(128)(2,1)} %gain_ref.1, bf16[128,512]{1,0:T(8,128)(2,1)} %query_ref.1, bf16[128,128]{1,0:T(8,128)(2,1)} %key_ref.1, bf16[128,128]{1,0:T(8,128)(2,1)} %value_ref.1, ...), custom_call_target="tpu_custom_call" | custom-call | flops 1572864 | bytes 651264 | tf_op jit(solution)/shard_map/qkv_projection/pallas_call | solution.py:75
  9.2 0.0 all-gather.5.cloned.1.call-update
  9.3 25.8 %all-gather = f32[128,768]{1,0:T(8,128)S(1)} all-gather(f32[8,768]{1,0:T(8,128)} %get-tuple-element.5), channel_id=2, replica_groups=mesh['seq'=16,'mlp'=8,'tp'=4] {'seq'}, dimensions={0}, use_global_device_ids=true | all-gather | bytes 417792 | tf_op jit(solution)/shard_map/qkv_projection/all_gather | solution.py:135
  35.1 0.0 copy-start.4
  35.1 0.0 copy-start.5
  35.1 0.1 reshape.175
  35.2 0.1 broadcast_compare_fusion
  35.3 0.0 copy-done.1
  35.3 0.5 copy.117
  35.8 0.1 multiply_cosine_fusion
  36.0 0.1 subtract_convert_fusion
  36.1 0.4 select_reduce_fusion
  36.5 0.2 fusion.2
  36.7 0.2 copy.122
  36.9 0.5 copy.120
  37.4 0.0 slice-start
  37.4 0.4 fusion.3
  37.9 0.2 copy.121
  38.1 0.1 pad_maximum_fusion
  38.2 15.9 %all-gather.1 = f32[128,2,4,66]{3,2,1,0:T(4,128)S(1)} all-gather(f32[8,2,4,66]{3,2,1,0:T(4,128)S(1)} %pad_maximum_fusion), channel_id=3, replica_groups=mesh['seq'=16,'mlp'=8,'tp'=4] {'seq'}, dimensions={0}, use_global_device_ids=true | all-gather | bytes 287232 | tf_op jit(solution)/shard_map/softmax_merge/all_gather | solution.py:220
  54.1 0.1 copy.141
  54.2 0.1 reshape.178
  54.3 0.1 multiply_subtract_fusion
  54.4 0.1 fusion.13
  54.5 0.2 multiply_reduce_fusion.1
  54.6 0.1 copy.126
  54.7 0.3 fusion.14
  55.0 0.0 copy-start.6
  55.0 0.0 copy-start.3
  55.0 0.5 copy.129
  55.5 0.5 copy.138
  56.0 0.1 exponential_bitcast_fusion
  56.1 0.1 copy.127
  56.1 0.0 copy-done.5
  56.1 0.1 reshape.181
  56.2 0.2 fusion.10
  56.4 0.3 fusion
  56.8 0.1 divide_convert_fusion
  56.9 0.1 convert_element_type.86
  57.0 0.1 convolution_convert_fusion
  57.1 0.7 broadcast_in_dim.31
  57.8 6.1 %all-to-all-start = ((bf16[64,8,128]{2,1,0:T(8,128)(2,1)}), bf16[64,8,128]{2,1,0:T(8,128)(2,1)S(1)}, u32[]{:S(2)}, u32[]{:S(2)}) async-start(bf16[64,8,128]{2,1,0:T(8,128)(2,1)} %broadcast_in_dim.31), calls=%async_computation | async-start | bytes 262144 | tf_op jit(solution)/shard_map/output_projection/all_to_all | solution.py:143
  63.9 10.0 %all-to-all-done = bf16[64,8,128]{2,1,0:T(8,128)(2,1)S(1)} async-done(((bf16[64,8,128]{2,1,0:T(8,128)(2,1)}), bf16[64,8,128]{2,1,0:T(8,128)(2,1)S(1)}, u32[]{:S(2)}, u32[]{:S(2)}) %all-to-all-start) | async-done | bytes 131104 | tf_op jit(solution)/shard_map/output_projection/all_to_all | solution.py:143
  74.0 0.1 multiply_reduce_fusion
  74.1 0.7 multiply_convert_fusion.input_ref
  74.8 2.5 %feed_forward.1 = f32[8,2048]{1,0:T(8,128)} custom-call(bf16[8,2048]{1,0:T(8,128)(2,1)} %multiply_convert_fusion.input_ref, bf16[8,384,256]{2,1,0:T(8,128)(2,1)} %bitcast.47), custom_call_target="tpu_custom_call" | custom-call | flops 12582912 | bytes 1671168 | tf_op jit(solution)/shard_map/feed_forward/pallas_call | solution.py:121
  77.3 1.0 reshape.180
  78.3 0.2 copy.131
  78.4 0.2 reshape.187
  78.6 14.5 %all_to_all.15 = f32[64,1,256]{2,1,0:T(1,128)S(1)} all-to-all(f32[64,1,256]{2,1,0:T(1,128)S(1)} %reshape.187), channel_id=1, replica_groups=mesh['seq'=16,'mlp'=8,'tp'=4] {'seq','tp'}, dimensions={0} | all-to-all | bytes 131072 | tf_op jit(solution)/shard_map/down_reduction/all_to_all | solution.py:263
  93.1 0.5 broadcast.105
  93.6 0.8 reduce.2
  94.4 0.1 reshape.188
  94.5 0.1 reduce_sum.82
  94.6 0.7 reshape.189
  95.4 5.3 %all-to-all-start.2 = ((bf16[64,2,128]{2,1,0:T(2,128)(2,1)}), bf16[64,2,128]{2,1,0:T(2,128)(2,1)S(1)}, u32[]{:S(2)}, u32[]{:S(2)}) async-start(bf16[64,2,128]{2,1,0:T(2,128)(2,1)} %reshape.189), calls=%async_computation.2 | async-start | bytes 65536 | tf_op jit(solution)/shard_map/down_reduction/all_to_all | solution.py:143
  100.7 0.7 convert_element_type.98
  101.4 8.6 %all-to-all-done.2 = bf16[64,2,128]{2,1,0:T(2,128)(2,1)S(1)} async-done(((bf16[64,2,128]{2,1,0:T(2,128)(2,1)}), bf16[64,2,128]{2,1,0:T(2,128)(2,1)S(1)}, u32[]{:S(2)}, u32[]{:S(2)}) %all-to-all-start.2) | async-done | bytes 32800 | tf_op jit(solution)/shard_map/down_reduction/all_to_all | solution.py:143
  109.9 0.1 reshape.190
  110.1 0.1 copy.132
  110.1 0.1 reshape.183
  110.3 0.6 add_convert_fusion
  (26 shorter events, 0.2 us)
Async XLA Ops:
  7.2 49.8 %copy-start = (bf16[512,128]{1,0:T(8,128)(2,1)S(1)}, bf16[512,128]{1,0:T(8,128)(2,1)}, u32[]{:S(2)}) copy-start(bf16[512,128]{1,0:T(8,128)(2,1)} %param.21) | copy-start | bytes 393220
  7.2 28.0 %copy-start.7 = (s32[8]{0:T(128)S(1)}, s32[8]{0:T(128)}, u32[]{:S(2)}) copy-start(s32[8]{0:T(128)} %param.14) | copy-start | bytes 100
  7.2 28.1 %copy-start.1 = (bf16[8,512,128]{2,1,0:T(8,128)(2,1)S(1)}, bf16[8,512,128]{2,1,0:T(8,128)(2,1)}, u32[]{:S(2)}) copy-start(bf16[8,512,128]{2,1,0:T(8,128)(2,1)} %param.19) | copy-start | bytes 3145732
  7.2 67.6 %all-gather.5.cloned.1.call-start = ((), (), s32[]{:S(2)}) async-start(), calls=%async_computation.3 | async-start | bytes 1769472 | tf_op jit(solution)/shard_map/mlp_weight_gather/all_gather | solution.py:180
  35.1 1.4 %copy-start.4 = (f32[8,768]{1,0:T(8,128)}, f32[8,768]{1,0:T(8,128)S(1)}, u32[]{:S(2)}) copy-start(f32[8,768]{1,0:T(8,128)S(1)} %bitcast_reduce_fusion) | copy-start | bytes 73732
  35.1 21.0 %copy-start.5 = (bf16[8,128]{1,0:T(8,128)(2,1)}, bf16[8,128]{1,0:T(8,128)(2,1)S(1)}, u32[]{:S(2)}) copy-start(bf16[8,128]{1,0:T(8,128)(2,1)S(1)} %slice.64) | copy-start | bytes 6148
  35.3 1.6 %copy-start.2 = (bf16[8,512,128]{2,1,0:T(8,128)(2,1)S(1)}, bf16[8,512,128]{2,1,0:T(8,128)(2,1)}, u32[]{:S(2)}) copy-start(bf16[8,512,128]{2,1,0:T(8,128)(2,1)} %param.20) | copy-start | bytes 3145732
  37.4 16.8 %slice-start = ((f32[8,768]{1,0:T(8,128)}), f32[8,128]{1,0:T(8,128)S(1)}, s32[]{:S(2)}) async-start(f32[8,768]{1,0:T(8,128)} %copy-done.4), calls=%async_computation.4 | async-start | bytes 8192 | tf_op jit(solution)/shard_map/slice | solution.py:184
  55.0 8.9 %copy-start.6 = (bf16[2048]{0:T(1024)(128)(2,1)S(1)}, bf16[2048]{0:T(1024)(128)(2,1)}, u32[]{:S(2)}) copy-start(bf16[2048]{0:T(1024)(128)(2,1)} %param.22) | copy-start | bytes 12292
  55.0 19.0 %copy-start.3 = (bf16[8,2048]{1,0:T(8,128)(2,1)S(1)}, bf16[8,2048]{1,0:T(8,128)(2,1)}, u32[]{:S(2)}) copy-start(bf16[8,2048]{1,0:T(8,128)(2,1)} %hidden_ref.1) | copy-start | bytes 98308
  57.8 16.2 %all-to-all-start = ((bf16[64,8,128]{2,1,0:T(8,128)(2,1)}), bf16[64,8,128]{2,1,0:T(8,128)(2,1)S(1)}, u32[]{:S(2)}, u32[]{:S(2)}) async-start(bf16[64,8,128]{2,1,0:T(8,128)(2,1)} %broadcast_in_dim.31), calls=%async_computation | async-start | bytes 262144 | tf_op jit(solution)/shard_map/output_projection/all_to_all | solution.py:143
  95.4 14.6 %all-to-all-start.2 = ((bf16[64,2,128]{2,1,0:T(2,128)(2,1)}), bf16[64,2,128]{2,1,0:T(2,128)(2,1)S(1)}, u32[]{:S(2)}, u32[]{:S(2)}) async-start(bf16[64,2,128]{2,1,0:T(2,128)(2,1)} %reshape.189), calls=%async_computation.2 | async-start | bytes 65536 | tf_op jit(solution)/shard_map/down_reduction/all_to_all | solution.py:143
Sparse Core Ops, SparseCore 0:
  10.1 43.2 all-gather.4

commit v11 on v9

--- a/solution.py
+++ b/solution.py
@@ -89,6 +89,49 @@
             transcendentals=rows,
         ),
     )(block, hidden, gain, query_weight, key_weight, value_weight, gate, up, down)
+
+
+def combine_kernel(state_ref, self_ref, values_ref, weight_ref, out_ref):
+    head_dim = values_ref.shape[-1]
+    state = state_ref[...]
+    block_max = state[..., head_dim : head_dim + 1]
+    block_sum = state[..., head_dim + 1 : head_dim + 2]
+    block_acc = state[..., :head_dim]
+    self_score = self_ref[...]
+    overall_max = jnp.maximum(jnp.max(block_max, axis=0), self_score)
+    rescale = jnp.exp(block_max - overall_max[None])
+    self_weight = jnp.exp(self_score - overall_max)
+    total_weight = jnp.sum(block_sum * rescale, axis=0) + self_weight
+    weighted_sum = jnp.sum(block_acc * rescale, axis=0) + self_weight * values_ref[...]
+    attended = (weighted_sum / total_weight).astype(jnp.bfloat16)
+    projected = None
+    for head in range(attended.shape[0]):
+        term = jnp.dot(
+            attended[head],
+            weight_ref[head * head_dim : (head + 1) * head_dim, :],
+            preferred_element_type=jnp.float32,
+        )
+        projected = term if projected is None else projected + term
+    out_ref[...] = jnp.broadcast_to(projected.astype(out_ref.dtype)[None], out_ref.shape)
+
+
+def combine_and_project(every_state, self_score, head_values, output_weight, copies):
+    blocks, heads, rows, lanes = every_state.shape
+    width = output_weight.shape[1]
+    vmem = pl.BlockSpec(memory_space=pltpu.VMEM)
+    return pl.pallas_call(
+        combine_kernel,
+        out_shape=jax.ShapeDtypeStruct((copies, rows, width), jnp.bfloat16),
+        in_specs=[vmem] * 4,
+        out_specs=vmem,
+        cost_estimate=pl.CostEstimate(
+            flops=2 * rows * output_weight.shape[0] * width + 4 * blocks * heads * rows * lanes,
+            bytes_accessed=4 * blocks * heads * rows * lanes
+            + 2 * output_weight.size
+            + 2 * copies * rows * width,
+            transcendentals=blocks * heads * rows,
+        ),
+    )(every_state, self_score, head_values, output_weight)
 
 
 def gathered_sum(x, axis):
@@ -180,11 +223,17 @@
             preferred_element_type=jnp.float32,
         )
     with jax.named_scope("softmax_merge"):
-        state = jnp.concatenate([block_max[..., None], block_sum[..., None], block_acc], axis=-1)
+        lanes = 2 * HD
+        state = jnp.concatenate(
+            [
+                block_acc.transpose(1, 2, 0, 3).reshape(local_heads, requests, HD),
+                block_max.transpose(1, 2, 0).reshape(local_heads, requests, 1),
+                block_sum.transpose(1, 2, 0).reshape(local_heads, requests, 1),
+                jnp.zeros((local_heads, requests, lanes - HD - 2), jnp.float32),
+            ],
+            axis=-1,
+        )
         every_state = lax.all_gather(state, "seq")
-        every_max = every_state[..., 0]
-        every_sum = every_state[..., 1]
-        every_acc = every_state[..., 2:]
         query_float = grouped.astype(jnp.float32)
         self_score = (
             jnp.sum(
@@ -193,21 +242,20 @@
             )
             * score_scale
         )
-        overall_max = jnp.maximum(jnp.max(every_max, axis=0), self_score)
-        rescale = jnp.exp(every_max - overall_max[None])
-        self_weight = jnp.exp(self_score - overall_max)
-        total_weight = jnp.sum(every_sum * rescale, axis=0) + self_weight
-        weighted_sum = jnp.sum(every_acc * rescale[..., None], axis=0) + self_weight[
-            ..., None
-        ] * new_values.astype(jnp.float32).reshape(requests, key_heads, 1, HD)
-        attended = (
-            (weighted_sum / total_weight[..., None])
-            .reshape(requests, local_heads * HD)
-            .astype(jnp.bfloat16)
-        )
+        self_score = self_score.transpose(1, 2, 0).reshape(local_heads, requests, 1)
+        head_values = jnp.broadcast_to(
+            new_values.astype(jnp.float32).reshape(requests, key_heads, 1, HD),
+            (requests, key_heads, group_size, HD),
+        ).transpose(1, 2, 0, 3).reshape(local_heads, requests, HD)
     with jax.named_scope("output_projection"):
-        partial_output = jnp.dot(attended, output_weight, preferred_element_type=jnp.float32)
-        every_partial = gather_by_exchange(partial_output.astype(jnp.bfloat16), ("seq", "tp"))
+        copies = lax.axis_size("seq") * lax.axis_size("tp")
+        every_partial = lax.all_to_all(
+            combine_and_project(every_state, self_score, head_values, output_weight, copies),
+            ("seq", "tp"),
+            0,
+            0,
+            tiled=True,
+        )
         column_blocks = lax.axis_size("seq")
         projected = (
             every_partial.reshape(column_blocks, lax.axis_size("tp"), requests, -1)

time: 117 us -> 121 us (1.034)
  Pallas kernels: 1.97 us -> 4.32 us
  blocking collectives: 56.2 us -> 57.7 us
    all_to_all x0 -> x1, waiting for transfers between devices: none -> 10 us  [per_device(): lax.all_to_all(combine_and_project(every_state, self_score, head_values,...]
    all_to_all x2 -> x1, waiting for transfers between devices: 18.6 us -> 8.57 us  [gather_by_exchange(): return lax.all_to_all(copies, axes, 0, 0, tiled=True)]
    all_to_all x2 -> x1, starting transfers between devices: 11.5 us -> 5.34 us  [gather_by_exchange(): return lax.all_to_all(copies, axes, 0, 0, tiled=True)]
    all_to_all x0 -> x1, starting transfers between devices: none -> 6.13 us  [per_device(): lax.all_to_all(combine_and_project(every_state, self_score, head_values,...]
    pallas_call x0 -> x1, Pallas kernels: none -> 2.35 us  [combine_and_project(): pl.pallas_call(combine_kernel, out_shape=jax.ShapeDtypeStruct((copies, ro...]
    all_gather x1, blocking collectives: 15.9 us -> 17.3 us  [per_device(): every_state = lax.all_gather(state, 'seq')]
    unnamed x23 -> x18, local copies, waits for them, and re-layouts: 2.68 us -> 2.2 us
  transfers between devices with their start and end apart: 3 -> 3, of which waited for: 2 -> 2; matrix products, arithmetic and copies ran while one was open for 6% -> 6% of each run, Pallas kernels for 0% -> 2%
where the time goes in v11:
time: 121 us; the launch traced here: 120 us
  blocking collectives  57.7 us (48%)
  waiting for transfers between devices  18.6 us (15%)
  between operations  14.3 us (12%)
  starting transfers between devices  11.5 us (10%)
  local copies, waits for them, and re-layouts  7.39 us (6%)
  Pallas kernels  4.32 us (4%)
  other arithmetic  3.94 us (3%)
  matrix products  2.5 us (2%)
    all_gather x1, blocking collectives, gathered_sum(): return jnp.sum(lax.all_gather(x, axis), axis=0)  25.9 us
    all_gather x1, blocking collectives, per_device(): every_state = lax.all_gather(state, 'seq')  17.3 us
    all_to_all x1, blocking collectives, per_device(): lax.all_to_all(pieces, ('seq', 'tp'), 0, 0, tiled=True).sum(axis=0)  14.5 us
    all_to_all x1, waiting for transfers between devices, per_device(): lax.all_to_all(combine_and_project(every_state, self_score, head_values,...  10 us
    all_to_all x1, waiting for transfers between devices, gather_by_exchange(): return lax.all_to_all(copies, axes, 0, 0, tiled=True)  8.57 us
    all_to_all x1, starting transfers between devices, per_device(): lax.all_to_all(combine_and_project(every_state, self_score, head_values,...  6.13 us
    all_to_all x1, starting transfers between devices, gather_by_exchange(): return lax.all_to_all(copies, axes, 0, 0, tiled=True)  5.34 us
  transfers between devices with their start and end apart: 3, of which 2 were waited for; matrix products, arithmetic and copies ran while one was open for 6% of the time, Pallas kernels for 2%

profile of v11, /device:TPU:1, one launch (start us, length us, event | category | flops | bytes accessed | tf_op | source)
XLA Modules:
  0.0 120.3 jit_solution(4295323015729339873)
XLA Ops:
  7.2 0.0 copy-start
  7.2 0.0 all-gather.5.cloned.1.call-start
  7.2 2.0 %qkv_projection.1 = (f32[8,768]{1,0:T(8,128)}, bf16[384,256]{1,0:T(8,128)(2,1)}) custom-call(s32[1]{0:T(128)} %bitcast.block_ref, bf16[8,2048]{1,0:T(8,128)(2,1)} %hidden_ref.1, bf16[2048]{0:T(1024)(128)(2,1)} %gain_ref.1, bf16[128,512]{1,0:T(8,128)(2,1)} %query_ref.1, bf16[128,128]{1,0:T(8,128)(2,1)} %key_ref.1, bf16[128,128]{1,0:T(8,128)(2,1)} %value_ref.1, ...), custom_call_target="tpu_custom_call" | custom-call | flops 1572864 | bytes 651264 | tf_op jit(solution)/shard_map/qkv_projection/pallas_call | solution.py:75
  9.2 0.0 all-gather.5.cloned.1.call-update
  9.2 0.0 copy-start.1
  9.2 25.9 %all-gather = f32[128,768]{1,0:T(8,128)S(1)} all-gather(f32[8,768]{1,0:T(8,128)} %get-tuple-element.5), channel_id=2, replica_groups=mesh['seq'=16,'mlp'=8,'tp'=4] {'seq'}, dimensions={0}, use_global_device_ids=true | all-gather | bytes 417792 | tf_op jit(solution)/shard_map/qkv_projection/all_gather | solution.py:138
  35.2 0.7 convert_element_type.74
  35.8 0.7 broadcast_compare_fusion
  36.6 0.1 multiply_cosine_fusion
  36.7 0.0 copy-start.3
  36.7 0.0 copy-start.4
  36.8 0.1 reshape.165
  36.8 0.0 copy-done
  36.8 0.5 copy.33
  37.4 0.0 copy-done.1
  37.4 0.5 copy.34
  37.9 0.0 copy-done.3
  37.9 0.0 slice-start
  37.9 0.1 subtract_convert_fusion
  38.0 0.4 select_reduce_fusion
  38.4 0.4 fusion.6
  38.9 0.2 fusion.4
  39.1 0.1 copy.36
  39.2 0.1 copy.39
  39.3 0.1 copy.35
  39.4 0.1 copy.38
  39.5 0.0 slice-done
  39.6 0.1 reshape.171
  39.6 0.1 multiply_subtract_fusion
  39.7 0.1 fusion.20
  39.8 0.2 multiply_reduce_fusion.1
  40.0 0.1 copy.40
  40.1 0.7 copy.42.self_ref
  40.8 0.0 copy-done.4
  40.8 0.1 reshape.178
  40.9 0.1 pad.5.clone
  41.0 0.1 maximum_maximum_fusion
  41.1 17.3 %all-gather.1 = f32[128,8,128]{2,1,0:T(8,128)} all-gather(f32[8,8,128]{2,1,0:T(8,128)S(1)} %maximum_maximum_fusion), channel_id=3, replica_groups=mesh['seq'=16,'mlp'=8,'tp'=4] {'seq'}, dimensions={0}, use_global_device_ids=true | all-gather | bytes 557056 | tf_op jit(solution)/shard_map/softmax_merge/all_gather | solution.py:236
  58.4 0.6 broadcast_in_dim.57
  59.0 2.4 %output_projection.1 = bf16[64,8,128]{2,1,0:T(8,128)(2,1)} custom-call(f32[16,8,8,128]{3,2,1,0:T(8,128)} %bitcast.51, f32[8,8,1]{2,1,0:T(8,128)} %copy.42.self_ref, f32[8,8,64]{2,1,0:T(8,128)} %bitcast.62, bf16[512,128]{1,0:T(8,128)(2,1)} %weight_ref.1), custom_call_target="tpu_custom_call" | custom-call | flops 1572864 | bytes 786432 | tf_op jit(solution)/shard_map/output_projection/pallas_call | solution.py:122
  61.3 6.1 %all-to-all-start = ((bf16[64,8,128]{2,1,0:T(8,128)(2,1)}), bf16[64,8,128]{2,1,0:T(8,128)(2,1)S(1)}, u32[]{:S(2)}, u32[]{:S(2)}) async-start(bf16[64,8,128]{2,1,0:T(8,128)(2,1)} %output_projection.1), calls=%async_computation | async-start | bytes 262144 | tf_op jit(solution)/shard_map/output_projection/all_to_all | solution.py:252
  67.5 0.0 copy-done.5
  67.5 10.0 %all-to-all-done = bf16[64,8,128]{2,1,0:T(8,128)(2,1)S(1)} async-done(((bf16[64,8,128]{2,1,0:T(8,128)(2,1)}), bf16[64,8,128]{2,1,0:T(8,128)(2,1)S(1)}, u32[]{:S(2)}, u32[]{:S(2)}) %all-to-all-start) | async-done | bytes 131104 | tf_op jit(solution)/shard_map/output_projection/all_to_all | solution.py:252
  77.6 0.1 multiply_reduce_fusion
  77.7 0.0 all-gather.5.cloned.1.call-done
  77.7 1.3 %fusion.21 = (bf16[8,256,128]{2,1,0:T(8,128)(2,1)S(1)}, bf16[8,256,128]{2,1,0:T(8,128)(2,1)S(1)}) fusion(bf16[8,384,256]{2,1,0:T(8,128)(2,1)} %bitcast.54), kind=kLoop, calls=%fused_computation.47 | loop fusion | bytes 2097152 | tf_op jit(solution)/shard_map/slice | solution.py:185
  79.0 0.2 fusion.19
  79.2 1.4 %fusion.2 = f32[8,8,256]{2,0,1:T(8,128)S(1)} fusion(bf16[2048,128]{1,0:T(8,128)(2,1)S(1)} %bitcast.52, bf16[8,384,256]{2,1,0:T(8,128)(2,1)} %bitcast.55, f32[8,128]{1,0:T(8,128)S(1)} %fusion.19, bf16[16,8,128]{2,1,0:T(8,128)(2,1)S(1)} %bitcast_reduce_fusion.1, bf16[8,2048]{1,0:T(8,128)(2,1)S(1)} %copy-done.2, f32[2048]{0:T(1024)S(1)} %convert_element_type.82, ...), kind=kOutput, calls=%fused_computation.4 | convolution fusion | flops 8493056 | bytes 1191968 | tf_op jit(solution)/shard_map/feed_forward/rh,jhc->rjc/dot_general | solution.py:274
  80.7 0.1 reshape.177
  80.8 0.2 copy.44
  81.0 0.2 reshape.185
  81.2 14.5 %all_to_all.15 = f32[64,1,256]{2,1,0:T(1,128)S(1)} all-to-all(f32[64,1,256]{2,1,0:T(1,128)S(1)} %reshape.185), channel_id=1, replica_groups=mesh['seq'=16,'mlp'=8,'tp'=4] {'seq','tp'}, dimensions={0} | all-to-all | bytes 131072 | tf_op jit(solution)/shard_map/down_reduction/all_to_all | solution.py:280
  95.6 0.5 broadcast.96
  96.1 0.8 reduce.1
  97.0 0.1 reshape.186
  97.1 0.1 reduce_sum.62
  97.2 0.7 reshape.187
  97.9 5.3 %all-to-all-start.2 = ((bf16[64,2,128]{2,1,0:T(2,128)(2,1)}), bf16[64,2,128]{2,1,0:T(2,128)(2,1)S(1)}, u32[]{:S(2)}, u32[]{:S(2)}) async-start(bf16[64,2,128]{2,1,0:T(2,128)(2,1)} %reshape.187), calls=%async_computation.2 | async-start | bytes 65536 | tf_op jit(solution)/shard_map/down_reduction/all_to_all | solution.py:146
  103.3 0.7 convert_element_type.90
  103.9 8.6 %all-to-all-done.2 = bf16[64,2,128]{2,1,0:T(2,128)(2,1)S(1)} async-done(((bf16[64,2,128]{2,1,0:T(2,128)(2,1)}), bf16[64,2,128]{2,1,0:T(2,128)(2,1)S(1)}, u32[]{:S(2)}, u32[]{:S(2)}) %all-to-all-start.2) | async-done | bytes 32800 | tf_op jit(solution)/shard_map/down_reduction/all_to_all | solution.py:146
  112.5 0.1 reshape.188
  112.6 0.1 copy.45
  112.7 0.1 reshape.180
  112.8 0.6 add_convert_fusion
  (18 shorter events, 0.2 us)
Async XLA Ops:
  7.2 29.7 %copy-start = (bf16[8,512,128]{2,1,0:T(8,128)(2,1)S(1)}, bf16[8,512,128]{2,1,0:T(8,128)(2,1)}, u32[]{:S(2)}) copy-start(bf16[8,512,128]{2,1,0:T(8,128)(2,1)} %param.19) | copy-start | bytes 3145732
  7.2 70.5 %all-gather.5.cloned.1.call-start = ((), (), s32[]{:S(2)}) async-start(), calls=%async_computation.3 | async-start | bytes 1769472 | tf_op jit(solution)/shard_map/mlp_weight_gather/all_gather | solution.py:183
  9.2 28.2 %copy-start.1 = (bf16[8,512,128]{2,1,0:T(8,128)(2,1)S(1)}, bf16[8,512,128]{2,1,0:T(8,128)(2,1)}, u32[]{:S(2)}) copy-start(bf16[8,512,128]{2,1,0:T(8,128)(2,1)} %param.20) | copy-start | bytes 3145732
  36.7 1.2 %copy-start.3 = (f32[8,768]{1,0:T(8,128)}, f32[8,768]{1,0:T(8,128)S(1)}, u32[]{:S(2)}) copy-start(f32[8,768]{1,0:T(8,128)S(1)} %bitcast_reduce_fusion) | copy-start | bytes 73732
  36.7 4.1 %copy-start.4 = (bf16[8,128]{1,0:T(8,128)(2,1)}, bf16[8,128]{1,0:T(8,128)(2,1)S(1)}, u32[]{:S(2)}) copy-start(bf16[8,128]{1,0:T(8,128)(2,1)S(1)} %slice.62) | copy-start | bytes 6148
  37.9 1.6 %slice-start = ((f32[8,768]{1,0:T(8,128)}), f32[8,128]{1,0:T(8,128)S(1)}, s32[]{:S(2)}) async-start(f32[8,768]{1,0:T(8,128)} %copy-done.3), calls=%async_computation.4 | async-start | bytes 8192 | tf_op jit(solution)/shard_map/slice | solution.py:191
  38.4 29.1 %copy-start.5 = (bf16[2048]{0:T(1024)(128)(2,1)S(1)}, bf16[2048]{0:T(1024)(128)(2,1)}, u32[]{:S(2)}) copy-start(bf16[2048]{0:T(1024)(128)(2,1)} %param.22) | copy-start | bytes 12292
  38.9 38.7 %copy-start.2 = (bf16[8,2048]{1,0:T(8,128)(2,1)S(1)}, bf16[8,2048]{1,0:T(8,128)(2,1)}, u32[]{:S(2)}) copy-start(bf16[8,2048]{1,0:T(8,128)(2,1)} %hidden_ref.1) | copy-start | bytes 98308
  61.3 16.2 %all-to-all-start = ((bf16[64,8,128]{2,1,0:T(8,128)(2,1)}), bf16[64,8,128]{2,1,0:T(8,128)(2,1)S(1)}, u32[]{:S(2)}, u32[]{:S(2)}) async-start(bf16[64,8,128]{2,1,0:T(8,128)(2,1)} %output_projection.1), calls=%async_computation | async-start | bytes 262144 | tf_op jit(solution)/shard_map/output_projection/all_to_all | solution.py:252
  97.9 14.6 %all-to-all-start.2 = ((bf16[64,2,128]{2,1,0:T(2,128)(2,1)}), bf16[64,2,128]{2,1,0:T(2,128)(2,1)S(1)}, u32[]{:S(2)}, u32[]{:S(2)}) async-start(bf16[64,2,128]{2,1,0:T(2,128)(2,1)} %reshape.187), calls=%async_computation.2 | async-start | bytes 65536 | tf_op jit(solution)/shard_map/down_reduction/all_to_all | solution.py:146
Sparse Core Ops, SparseCore 0:
  10.1 43.2 all-gather.4

commit v12 on v9

--- a/solution.py
+++ b/solution.py
@@ -229,7 +229,11 @@
     with jax.named_scope("down_reduction"):
         reducers = lax.axis_size("seq") * lax.axis_size("tp")
         pieces = down_part.reshape(requests, reducers, -1).transpose(1, 0, 2)
-        own_piece = lax.all_to_all(pieces, ("seq", "tp"), 0, 0, tiled=True).sum(axis=0)
+        own_piece = (
+            lax.all_to_all(pieces.astype(jnp.bfloat16), ("seq", "tp"), 0, 0, tiled=True)
+            .astype(jnp.float32)
+            .sum(axis=0)
+        )
         every_piece = gather_by_exchange(own_piece.astype(jnp.bfloat16), ("seq", "tp"))
         down_total = every_piece.transpose(1, 0, 2).reshape(requests, -1)
     updated_hidden = (mixed_stream + down_total.astype(jnp.float32)).astype(jnp.bfloat16)

time: 117 us -> 115 us (0.983)
  no operation moved by 1% of the time
where the time goes in v12:
time: 115 us
  blocking collectives  56.1 us (49%)
  waiting for transfers between devices  18.6 us (16%)
  between operations  14.4 us (13%)
  starting transfers between devices  11.1 us (10%)
  local copies, waits for them, and re-layouts  7.21 us (6%)
  other arithmetic  2.85 us (2%)
  matrix products  2.63 us (2%)
  Pallas kernels  1.97 us (2%)
    all_gather x1, blocking collectives, gathered_sum(): return jnp.sum(lax.all_gather(x, axis), axis=0)  25.8 us
    all_to_all x2, waiting for transfers between devices, gather_by_exchange(): return lax.all_to_all(copies, axes, 0, 0, tiled=True)  18.6 us
    all_gather x1, blocking collectives, per_device(): every_state = lax.all_gather(state, 'seq')  15.9 us
    all_to_all x1, blocking collectives, per_device(): lax.all_to_all(pieces.astype(jnp.bfloat16), ('seq', 'tp'), 0, 0, tiled=True)  14.4 us
    all_to_all x2, starting transfers between devices, gather_by_exchange(): return lax.all_to_all(copies, axes, 0, 0, tiled=True)  11.1 us
    unnamed x23, local copies, waits for them, and re-layouts  2.64 us
  transfers between devices with their start and end apart: 3, of which 2 were waited for; matrix products, arithmetic and copies ran while one was open for 6% of the time, Pallas kernels for 0%

profile of v12, /device:TPU:1, one launch (start us, length us, event | category | flops | bytes accessed | tf_op | source)
XLA Modules:
  0.0 114.9 jit_solution(3958209036609567719)
XLA Ops:
  7.2 0.0 copy-start
  7.2 0.0 all-gather.5.cloned.1.call-start
  7.3 2.0 %qkv_projection.1 = (f32[8,768]{1,0:T(8,128)}, bf16[384,256]{1,0:T(8,128)(2,1)}) custom-call(s32[1]{0:T(128)} %bitcast.block_ref, bf16[8,2048]{1,0:T(8,128)(2,1)} %hidden_ref.1, bf16[2048]{0:T(1024)(128)(2,1)} %gain_ref.1, bf16[128,512]{1,0:T(8,128)(2,1)} %query_ref.1, bf16[128,128]{1,0:T(8,128)(2,1)} %key_ref.1, bf16[128,128]{1,0:T(8,128)(2,1)} %value_ref.1, ...), custom_call_target="tpu_custom_call" | custom-call | flops 1572864 | bytes 651264 | tf_op jit(solution)/shard_map/qkv_projection/pallas_call | solution.py:75
  9.2 0.0 all-gather.5.cloned.1.call-update
  9.3 25.8 %all-gather = f32[128,768]{1,0:T(8,128)S(1)} all-gather(f32[8,768]{1,0:T(8,128)} %get-tuple-element.5), channel_id=2, replica_groups=mesh['seq'=16,'mlp'=8,'tp'=4] {'seq'}, dimensions={0}, use_global_device_ids=true | all-gather | bytes 417792 | tf_op jit(solution)/shard_map/qkv_projection/all_gather | solution.py:95
  35.1 0.0 copy-start.4
  35.1 0.0 copy-start.5
  35.1 0.1 reshape.178
  35.2 0.0 copy-done.7
  35.2 0.1 broadcast_compare_fusion
  35.3 0.5 copy.124
  35.8 0.1 multiply_cosine_fusion
  36.0 0.1 subtract_convert_fusion
  36.1 0.4 select_reduce_fusion
  36.5 0.2 fusion.5
  36.7 0.2 copy.129
  36.9 0.5 copy.127
  37.4 0.0 slice-start
  37.4 0.4 fusion.6
  37.9 0.2 copy.128
  38.1 0.1 pad_maximum_fusion
  38.2 15.9 %all-gather.1 = f32[128,2,4,66]{3,2,1,0:T(4,128)S(1)} all-gather(f32[8,2,4,66]{3,2,1,0:T(4,128)S(1)} %pad_maximum_fusion), channel_id=3, replica_groups=mesh['seq'=16,'mlp'=8,'tp'=4] {'seq'}, dimensions={0}, use_global_device_ids=true | all-gather | bytes 287232 | tf_op jit(solution)/shard_map/softmax_merge/all_gather | solution.py:184
  54.1 0.1 copy.149
  54.2 0.1 reshape.181
  54.3 0.1 multiply_subtract_fusion
  54.4 0.1 fusion.24
  54.5 0.2 multiply_reduce_fusion.1
  54.6 0.1 copy.133
  54.7 0.3 fusion.26
  55.0 0.0 copy-start.6
  55.0 0.0 copy-start.3
  55.0 0.5 copy.136
  55.5 0.5 copy.146
  56.0 0.1 exponential_bitcast_fusion
  56.1 0.1 copy.134
  56.1 0.0 copy-done.5
  56.1 0.1 reshape.185
  56.2 0.2 fusion.13
  56.4 0.3 fusion.3
  56.8 0.1 divide_convert_fusion
  56.9 0.1 convert_element_type.93
  57.0 0.1 convolution_convert_fusion.1
  57.1 0.7 broadcast_in_dim.31
  57.8 6.1 %all-to-all-start = ((bf16[64,8,128]{2,1,0:T(8,128)(2,1)}), bf16[64,8,128]{2,1,0:T(8,128)(2,1)S(1)}, u32[]{:S(2)}, u32[]{:S(2)}) async-start(bf16[64,8,128]{2,1,0:T(8,128)(2,1)} %broadcast_in_dim.31), calls=%async_computation | async-start | bytes 262144 | tf_op jit(solution)/shard_map/output_projection/all_to_all | solution.py:103
  63.9 10.0 %all-to-all-done = bf16[64,8,128]{2,1,0:T(8,128)(2,1)S(1)} async-done(((bf16[64,8,128]{2,1,0:T(8,128)(2,1)}), bf16[64,8,128]{2,1,0:T(8,128)(2,1)S(1)}, u32[]{:S(2)}, u32[]{:S(2)}) %all-to-all-start) | async-done | bytes 131104 | tf_op jit(solution)/shard_map/output_projection/all_to_all | solution.py:103
  74.0 0.1 multiply_reduce_fusion
  74.1 0.0 all-gather.5.cloned.1.call-done
  74.2 1.3 %fusion.25 = (bf16[8,256,128]{2,1,0:T(8,128)(2,1)S(1)}, bf16[8,256,128]{2,1,0:T(8,128)(2,1)S(1)}) fusion(bf16[8,384,256]{2,1,0:T(8,128)(2,1)} %bitcast.60), kind=kLoop, calls=%fused_computation.60 | loop fusion | bytes 2097152 | tf_op jit(solution)/shard_map/slice | solution.py:142
  75.4 0.2 fusion.22
  75.7 1.4 %convolution_convert_fusion = bf16[8,8,256]{2,0,1:T(8,128)(2,1)S(1)} fusion(bf16[2048,128]{1,0:T(8,128)(2,1)S(1)} %bitcast.58, bf16[8,384,256]{2,1,0:T(8,128)(2,1)} %bitcast.61, f32[8,128]{1,0:T(8,128)S(1)} %fusion.22, bf16[16,8,128]{2,1,0:T(8,128)(2,1)S(1)} %bitcast_reduce_fusion.1, bf16[8,2048]{1,0:T(8,128)(2,1)S(1)} %copy-done.3, ...), kind=kOutput, calls=%fused_computation.1 | convolution fusion | flops 8509440 | bytes 1159200 | tf_op jit(solution)/shard_map/feed_forward/rh,jhc->rjc/dot_general | solution.py:226
  77.1 0.1 convert_element_type.102
  77.3 0.1 copy.139
  77.4 0.1 reshape.192
  77.5 14.4 %all_to_all.15 = bf16[64,2,128]{2,1,0:T(2,128)(2,1)S(1)} all-to-all(bf16[64,2,128]{2,1,0:T(2,128)(2,1)S(1)} %reshape.192), channel_id=1, replica_groups=mesh['seq'=16,'mlp'=8,'tp'=4] {'seq','tp'}, dimensions={0} | all-to-all | bytes 65536 | tf_op jit(solution)/shard_map/down_reduction/all_to_all | solution.py:233
  91.9 0.1 reshape.193
  92.0 0.1 reduce_sum.85
  92.1 0.7 reshape.194
  92.9 4.9 %all-to-all-start.2 = ((bf16[64,2,128]{2,1,0:T(2,128)(2,1)}), bf16[64,2,128]{2,1,0:T(2,128)(2,1)S(1)}, u32[]{:S(2)}, u32[]{:S(2)}) async-start(bf16[64,2,128]{2,1,0:T(2,128)(2,1)} %reshape.194), calls=%async_computation.2 | async-start | bytes 65536 | tf_op jit(solution)/shard_map/down_reduction/all_to_all | solution.py:103
  97.8 0.7 convert_element_type.108
  98.5 8.6 %all-to-all-done.2 = bf16[64,2,128]{2,1,0:T(2,128)(2,1)S(1)} async-done(((bf16[64,2,128]{2,1,0:T(2,128)(2,1)}), bf16[64,2,128]{2,1,0:T(2,128)(2,1)S(1)}, u32[]{:S(2)}, u32[]{:S(2)}) %all-to-all-start.2) | async-done | bytes 32800 | tf_op jit(solution)/shard_map/down_reduction/all_to_all | solution.py:103
  107.1 0.1 reshape.195
  107.2 0.1 copy.140
  107.3 0.1 reshape.187
  107.4 0.6 add_convert_fusion
  (26 shorter events, 0.2 us)
Async XLA Ops:
  7.2 49.8 %copy-start = (bf16[512,128]{1,0:T(8,128)(2,1)S(1)}, bf16[512,128]{1,0:T(8,128)(2,1)}, u32[]{:S(2)}) copy-start(bf16[512,128]{1,0:T(8,128)(2,1)} %param.21) | copy-start | bytes 393220
  7.2 28.0 %copy-start.7 = (s32[8]{0:T(128)S(1)}, s32[8]{0:T(128)}, u32[]{:S(2)}) copy-start(s32[8]{0:T(128)} %param.14) | copy-start | bytes 100
  7.2 28.1 %copy-start.1 = (bf16[8,512,128]{2,1,0:T(8,128)(2,1)S(1)}, bf16[8,512,128]{2,1,0:T(8,128)(2,1)}, u32[]{:S(2)}) copy-start(bf16[8,512,128]{2,1,0:T(8,128)(2,1)} %param.19) | copy-start | bytes 3145732
  7.2 67.0 %all-gather.5.cloned.1.call-start = ((), (), s32[]{:S(2)}) async-start(), calls=%async_computation.3 | async-start | bytes 1769472 | tf_op jit(solution)/shard_map/mlp_weight_gather/all_gather | solution.py:140
  35.1 1.4 %copy-start.4 = (f32[8,768]{1,0:T(8,128)}, f32[8,768]{1,0:T(8,128)S(1)}, u32[]{:S(2)}) copy-start(f32[8,768]{1,0:T(8,128)S(1)} %bitcast_reduce_fusion) | copy-start | bytes 73732
  35.1 21.0 %copy-start.5 = (bf16[8,128]{1,0:T(8,128)(2,1)}, bf16[8,128]{1,0:T(8,128)(2,1)S(1)}, u32[]{:S(2)}) copy-start(bf16[8,128]{1,0:T(8,128)(2,1)S(1)} %slice.81) | copy-start | bytes 6148
  35.3 1.6 %copy-start.2 = (bf16[8,512,128]{2,1,0:T(8,128)(2,1)S(1)}, bf16[8,512,128]{2,1,0:T(8,128)(2,1)}, u32[]{:S(2)}) copy-start(bf16[8,512,128]{2,1,0:T(8,128)(2,1)} %param.20) | copy-start | bytes 3145732
  37.4 16.8 %slice-start = ((f32[8,768]{1,0:T(8,128)}), f32[8,128]{1,0:T(8,128)S(1)}, s32[]{:S(2)}) async-start(f32[8,768]{1,0:T(8,128)} %copy-done.4), calls=%async_computation.4 | async-start | bytes 8192 | tf_op jit(solution)/shard_map/slice | solution.py:148
  55.0 8.9 %copy-start.6 = (bf16[2048]{0:T(1024)(128)(2,1)S(1)}, bf16[2048]{0:T(1024)(128)(2,1)}, u32[]{:S(2)}) copy-start(bf16[2048]{0:T(1024)(128)(2,1)} %param.22) | copy-start | bytes 12292
  55.0 19.0 %copy-start.3 = (bf16[8,2048]{1,0:T(8,128)(2,1)S(1)}, bf16[8,2048]{1,0:T(8,128)(2,1)}, u32[]{:S(2)}) copy-start(bf16[8,2048]{1,0:T(8,128)(2,1)} %hidden_ref.1) | copy-start | bytes 98308
  57.8 16.2 %all-to-all-start = ((bf16[64,8,128]{2,1,0:T(8,128)(2,1)}), bf16[64,8,128]{2,1,0:T(8,128)(2,1)S(1)}, u32[]{:S(2)}, u32[]{:S(2)}) async-start(bf16[64,8,128]{2,1,0:T(8,128)(2,1)} %broadcast_in_dim.31), calls=%async_computation | async-start | bytes 262144 | tf_op jit(solution)/shard_map/output_projection/all_to_all | solution.py:103
  92.9 14.2 %all-to-all-start.2 = ((bf16[64,2,128]{2,1,0:T(2,128)(2,1)}), bf16[64,2,128]{2,1,0:T(2,128)(2,1)S(1)}, u32[]{:S(2)}, u32[]{:S(2)}) async-start(bf16[64,2,128]{2,1,0:T(2,128)(2,1)} %reshape.194), calls=%async_computation.2 | async-start | bytes 65536 | tf_op jit(solution)/shard_map/down_reduction/all_to_all | solution.py:103
Sparse Core Ops, SparseCore 0:
  10.1 43.2 all-gather.4

commit v13 on v12

--- a/solution.py
+++ b/solution.py
@@ -159,47 +159,55 @@
     new_values = values_raw.astype(jnp.bfloat16)
     grouped = queries.reshape(requests, key_heads, group_size, HD)
     block_span = cached_keys.shape[1]
-    key_blocks = cached_keys.reshape(requests, block_span, key_heads, HD)
-    value_blocks = cached_values.reshape(requests, block_span, key_heads, HD)
     score_scale = HD ** (-0.5)
     first_position = lax.axis_index("seq") * block_span
     positions = first_position + jnp.arange(block_span, dtype=jnp.int32)
-    valid_mask = (positions[None, :] < lengths[:, None])[:, None, None, :]
+    valid_mask = (positions[None, :] < lengths[:, None])[:, None, :]
+    own_head = jnp.arange(key_heads)[:, None] == jnp.arange(key_heads)[None, :]
     with jax.named_scope("local_attention"):
+        padded_queries = jnp.where(
+            own_head[None, :, None, :, None],
+            grouped[:, :, :, None, :],
+            jnp.zeros((), grouped.dtype),
+        ).reshape(requests, key_heads * group_size, key_heads * HD)
         scores = (
-            jnp.einsum("rgqd,rpgd->rgqp", grouped, key_blocks, preferred_element_type=jnp.float32)
+            jnp.einsum(
+                "rmk,rpk->rmp", padded_queries, cached_keys, preferred_element_type=jnp.float32
+            )
             * score_scale
         )
         block_max = jnp.max(jnp.where(valid_mask, scores, -1e30), axis=-1)
         exp_weights = jnp.where(valid_mask, jnp.exp(scores - block_max[..., None]), 0.0)
         block_sum = jnp.sum(exp_weights, axis=-1)
-        block_acc = jnp.einsum(
-            "rgqp,rpgd->rgqd",
+        every_head_acc = jnp.einsum(
+            "rmp,rpk->rmk",
             exp_weights.astype(jnp.bfloat16),
-            value_blocks,
+            cached_values,
             preferred_element_type=jnp.float32,
-        )
+        ).reshape(requests, key_heads * group_size, key_heads, HD)
+        own_block = jnp.repeat(own_head, group_size, axis=0)
+        block_acc = jnp.sum(jnp.where(own_block[None, :, :, None], every_head_acc, 0.0), axis=2)
     with jax.named_scope("softmax_merge"):
         state = jnp.concatenate([block_max[..., None], block_sum[..., None], block_acc], axis=-1)
         every_state = lax.all_gather(state, "seq")
         every_max = every_state[..., 0]
         every_sum = every_state[..., 1]
         every_acc = every_state[..., 2:]
-        query_float = grouped.astype(jnp.float32)
-        self_score = (
-            jnp.sum(
-                query_float * new_keys.astype(jnp.float32).reshape(requests, key_heads, 1, HD),
-                axis=-1,
-            )
-            * score_scale
-        )
+        query_float = grouped.astype(jnp.float32).reshape(requests, local_heads, HD)
+        head_keys = jnp.repeat(
+            new_keys.astype(jnp.float32).reshape(requests, key_heads, HD), group_size, axis=1
+        )
+        head_values = jnp.repeat(
+            new_values.astype(jnp.float32).reshape(requests, key_heads, HD), group_size, axis=1
+        )
+        self_score = jnp.sum(query_float * head_keys, axis=-1) * score_scale
         overall_max = jnp.maximum(jnp.max(every_max, axis=0), self_score)
         rescale = jnp.exp(every_max - overall_max[None])
         self_weight = jnp.exp(self_score - overall_max)
         total_weight = jnp.sum(every_sum * rescale, axis=0) + self_weight
-        weighted_sum = jnp.sum(every_acc * rescale[..., None], axis=0) + self_weight[
-            ..., None
-        ] * new_values.astype(jnp.float32).reshape(requests, key_heads, 1, HD)
+        weighted_sum = (
+            jnp.sum(every_acc * rescale[..., None], axis=0) + self_weight[..., None] * head_values
+        )
         attended = (
             (weighted_sum / total_weight[..., None])
             .reshape(requests, local_heads * HD)

time: 115 us -> 116 us (level)
    unnamed x23 -> x19, local copies, waits for them, and re-layouts: 2.64 us -> 1.6 us
  transfers between devices with their start and end apart: 3 -> 3, of which waited for: 2 -> 2; matrix products, arithmetic and copies ran while one was open for 6% -> 7% of each run, Pallas kernels for 0% -> 0%
where the time goes in v13:
time: 116 us; the launch traced here: 115 us
  blocking collectives  56.1 us (48%)
  waiting for transfers between devices  18.6 us (16%)
  between operations  14.4 us (12%)
  starting transfers between devices  11.1 us (10%)
  local copies, waits for them, and re-layouts  6.85 us (6%)
  other arithmetic  3.5 us (3%)
  matrix products  2.57 us (2%)
  Pallas kernels  2.02 us (2%)
    all_gather x1, blocking collectives, gathered_sum(): return jnp.sum(lax.all_gather(x, axis), axis=0)  25.8 us
    all_to_all x2, waiting for transfers between devices, gather_by_exchange(): return lax.all_to_all(copies, axes, 0, 0, tiled=True)  18.6 us
    all_gather x1, blocking collectives, per_device(): every_state = lax.all_gather(state, 'seq')  15.9 us
    all_to_all x1, blocking collectives, per_device(): lax.all_to_all(pieces.astype(jnp.bfloat16), ('seq', 'tp'), 0, 0, tiled=True)  14.4 us
    all_to_all x2, starting transfers between devices, gather_by_exchange(): return lax.all_to_all(copies, axes, 0, 0, tiled=True)  11.1 us
  transfers between devices with their start and end apart: 3, of which 2 were waited for; matrix products, arithmetic and copies ran while one was open for 7% of the time, Pallas kernels for 0%

profile of v13, /device:TPU:1, one launch (start us, length us, event | category | flops | bytes accessed | tf_op | source)
XLA Modules:
  0.0 115.2 jit_solution(3929808938719782579)
XLA Ops:
  7.2 0.0 all-gather.5.cloned.1.call-start
  7.3 2.0 %qkv_projection.1 = (f32[8,768]{1,0:T(8,128)}, bf16[384,256]{1,0:T(8,128)(2,1)}) custom-call(s32[1]{0:T(128)} %bitcast.block_ref, bf16[8,2048]{1,0:T(8,128)(2,1)} %hidden_ref.1, bf16[2048]{0:T(1024)(128)(2,1)} %gain_ref.1, bf16[128,512]{1,0:T(8,128)(2,1)} %query_ref.1, bf16[128,128]{1,0:T(8,128)(2,1)} %key_ref.1, bf16[128,128]{1,0:T(8,128)(2,1)} %value_ref.1, ...), custom_call_target="tpu_custom_call" | custom-call | flops 1572864 | bytes 651264 | tf_op jit(solution)/shard_map/qkv_projection/pallas_call | solution.py:75
  9.3 25.8 %all-gather = f32[128,768]{1,0:T(8,128)S(1)} all-gather(f32[8,768]{1,0:T(8,128)} %get-tuple-element.5), channel_id=2, replica_groups=mesh['seq'=16,'mlp'=8,'tp'=4] {'seq'}, dimensions={0}, use_global_device_ids=true | all-gather | bytes 417792 | tf_op jit(solution)/shard_map/qkv_projection/all_gather | solution.py:95
  35.2 0.1 reshape.225
  35.3 0.7 convert_element_type.86
  35.9 0.1 reshape.223
  36.0 0.1 multiply_cosine_fusion
  36.1 0.1 multiply_subtract_fusion
  36.2 0.1 subtract_convert_fusion
  36.3 0.1 fusion.28
  36.4 0.2 multiply_reduce_fusion.1
  36.6 0.1 broadcast_in_dim.111
  36.7 0.1 broadcast_compare_fusion
  36.8 0.1 copy.86
  36.9 0.1 broadcast_in_dim.107
  37.0 0.1 broadcast_in_dim.108
  37.0 0.5 select_reduce_fusion
  37.5 0.3 fusion.6
  37.8 0.1 reshape.224
  37.9 0.2 fusion.5
  38.1 0.1 copy.89
  38.2 0.1 copy.88
  38.4 0.1 copy.92
  38.5 0.1 copy.93
  38.5 0.2 select_reduce_fusion.1
  38.7 0.1 pad_maximum_fusion
  38.8 15.9 %all-gather.1 = f32[128,8,66]{2,1,0:T(8,128)S(1)} all-gather(f32[8,8,66]{2,1,0:T(8,128)S(1)} %pad_maximum_fusion), channel_id=3, replica_groups=mesh['seq'=16,'mlp'=8,'tp'=4] {'seq'}, dimensions={0}, use_global_device_ids=true | all-gather | bytes 287232 | tf_op jit(solution)/shard_map/softmax_merge/all_gather | solution.py:192
  54.7 0.3 slice_reduce_fusion
  55.0 0.5 copy.102
  55.5 0.1 exponential_bitcast_fusion
  55.6 0.1 copy.94
  55.7 0.3 fusion.3
  56.0 0.1 reduce_sum.94
  56.1 0.5 copy.96
  56.6 0.2 fusion.13
  56.8 0.1 div.26
  56.8 0.1 div.27
  56.9 0.1 mul.194
  57.0 0.1 mul.195
  57.1 0.1 reshape.233
  57.2 0.1 reshape.228
  57.2 0.1 convolution_convert_fusion.1
  57.4 0.7 broadcast_in_dim.123
  58.1 6.1 %all-to-all-start = ((bf16[64,8,128]{2,1,0:T(8,128)(2,1)}), bf16[64,8,128]{2,1,0:T(8,128)(2,1)S(1)}, u32[]{:S(2)}, u32[]{:S(2)}) async-start(bf16[64,8,128]{2,1,0:T(8,128)(2,1)} %broadcast_in_dim.123), calls=%async_computation | async-start | bytes 262144 | tf_op jit(solution)/shard_map/output_projection/all_to_all | solution.py:103
  64.2 10.0 %all-to-all-done = bf16[64,8,128]{2,1,0:T(8,128)(2,1)S(1)} async-done(((bf16[64,8,128]{2,1,0:T(8,128)(2,1)}), bf16[64,8,128]{2,1,0:T(8,128)(2,1)S(1)}, u32[]{:S(2)}, u32[]{:S(2)}) %all-to-all-start) | async-done | bytes 131104 | tf_op jit(solution)/shard_map/output_projection/all_to_all | solution.py:103
  74.3 0.1 multiply_reduce_fusion
  74.4 0.0 all-gather.5.cloned.1.call-done
  74.4 1.3 %fusion.29 = (bf16[8,256,128]{2,1,0:T(8,128)(2,1)S(1)}, bf16[8,256,128]{2,1,0:T(8,128)(2,1)S(1)}) fusion(bf16[8,384,256]{2,1,0:T(8,128)(2,1)} %bitcast.56), kind=kLoop, calls=%fused_computation.65 | loop fusion | bytes 2097152 | tf_op jit(solution)/shard_map/slice | solution.py:142
  75.7 0.2 fusion.26
  76.0 1.4 %convolution_convert_fusion = bf16[8,8,256]{2,0,1:T(8,128)(2,1)S(1)} fusion(bf16[2048,128]{1,0:T(8,128)(2,1)S(1)} %bitcast.54, bf16[8,384,256]{2,1,0:T(8,128)(2,1)} %bitcast.57, f32[8,128]{1,0:T(8,128)S(1)} %fusion.26, bf16[16,8,128]{2,1,0:T(8,128)(2,1)S(1)} %bitcast_reduce_fusion.1, bf16[8,2048]{1,0:T(8,128)(2,1)S(1)} %copy-done.2, ...), kind=kOutput, calls=%fused_computation.1 | convolution fusion | flops 8509440 | bytes 1159200 | tf_op jit(solution)/shard_map/feed_forward/rh,jhc->rjc/dot_general | solution.py:234
  77.4 0.1 convert_element_type.100
  77.6 0.1 copy.98
  77.7 0.1 reshape.240
  77.8 14.4 %all_to_all.15 = bf16[64,2,128]{2,1,0:T(2,128)(2,1)S(1)} all-to-all(bf16[64,2,128]{2,1,0:T(2,128)(2,1)S(1)} %reshape.240), channel_id=1, replica_groups=mesh['seq'=16,'mlp'=8,'tp'=4] {'seq','tp'}, dimensions={0} | all-to-all | bytes 65536 | tf_op jit(solution)/shard_map/down_reduction/all_to_all | solution.py:241
  92.2 0.1 reshape.241
  92.3 0.1 reduce_sum.98
  92.4 0.7 reshape.242
  93.1 4.9 %all-to-all-start.2 = ((bf16[64,2,128]{2,1,0:T(2,128)(2,1)}), bf16[64,2,128]{2,1,0:T(2,128)(2,1)S(1)}, u32[]{:S(2)}, u32[]{:S(2)}) async-start(bf16[64,2,128]{2,1,0:T(2,128)(2,1)} %reshape.242), calls=%async_computation.2 | async-start | bytes 65536 | tf_op jit(solution)/shard_map/down_reduction/all_to_all | solution.py:103
  98.1 0.7 convert_element_type.106
  98.8 8.6 %all-to-all-done.2 = bf16[64,2,128]{2,1,0:T(2,128)(2,1)S(1)} async-done(((bf16[64,2,128]{2,1,0:T(2,128)(2,1)}), bf16[64,2,128]{2,1,0:T(2,128)(2,1)S(1)}, u32[]{:S(2)}, u32[]{:S(2)}) %all-to-all-start.2) | async-done | bytes 32800 | tf_op jit(solution)/shard_map/down_reduction/all_to_all | solution.py:103
  107.3 0.1 reshape.243
  107.5 0.1 copy.99
  107.5 0.1 reshape.235
  107.7 0.6 add_convert_fusion
  (34 shorter events, 0.3 us)
Async XLA Ops:
  7.2 29.9 %copy-start = (bf16[8,512,128]{2,1,0:T(8,128)(2,1)S(1)}, bf16[8,512,128]{2,1,0:T(8,128)(2,1)}, u32[]{:S(2)}) copy-start(bf16[8,512,128]{2,1,0:T(8,128)(2,1)} %param.19) | copy-start | bytes 3145732
  7.2 29.5 %copy-start.6 = (s32[8]{0:T(128)S(1)}, s32[8]{0:T(128)}, u32[]{:S(2)}) copy-start(s32[8]{0:T(128)} %param.14) | copy-start | bytes 100
  7.2 67.2 %all-gather.5.cloned.1.call-start = ((), (), s32[]{:S(2)}) async-start(), calls=%async_computation.3 | async-start | bytes 1769472 | tf_op jit(solution)/shard_map/mlp_weight_gather/all_gather | solution.py:140
  7.2 30.3 %copy-start.1 = (bf16[8,512,128]{2,1,0:T(8,128)(2,1)S(1)}, bf16[8,512,128]{2,1,0:T(8,128)(2,1)}, u32[]{:S(2)}) copy-start(bf16[8,512,128]{2,1,0:T(8,128)(2,1)} %param.20) | copy-start | bytes 3145732
  37.8 19.2 %copy-start.4 = (bf16[8,128]{1,0:T(8,128)(2,1)}, bf16[8,128]{1,0:T(8,128)(2,1)S(1)}, u32[]{:S(2)}) copy-start(bf16[8,128]{1,0:T(8,128)(2,1)S(1)} %slice.81) | copy-start | bytes 6148
  55.0 2.3 %copy-start.3 = (bf16[512,128]{1,0:T(8,128)(2,1)S(1)}, bf16[512,128]{1,0:T(8,128)(2,1)}, u32[]{:S(2)}) copy-start(bf16[512,128]{1,0:T(8,128)(2,1)} %param.21) | copy-start | bytes 393220
  55.0 9.2 %copy-start.5 = (bf16[2048]{0:T(1024)(128)(2,1)S(1)}, bf16[2048]{0:T(1024)(128)(2,1)}, u32[]{:S(2)}) copy-start(bf16[2048]{0:T(1024)(128)(2,1)} %param.22) | copy-start | bytes 12292
  55.0 19.3 %copy-start.2 = (bf16[8,2048]{1,0:T(8,128)(2,1)S(1)}, bf16[8,2048]{1,0:T(8,128)(2,1)}, u32[]{:S(2)}) copy-start(bf16[8,2048]{1,0:T(8,128)(2,1)} %hidden_ref.1) | copy-start | bytes 98308
  58.1 16.2 %all-to-all-start = ((bf16[64,8,128]{2,1,0:T(8,128)(2,1)}), bf16[64,8,128]{2,1,0:T(8,128)(2,1)S(1)}, u32[]{:S(2)}, u32[]{:S(2)}) async-start(bf16[64,8,128]{2,1,0:T(8,128)(2,1)} %broadcast_in_dim.123), calls=%async_computation | async-start | bytes 262144 | tf_op jit(solution)/shard_map/output_projection/all_to_all | solution.py:103
  93.1 14.2 %all-to-all-start.2 = ((bf16[64,2,128]{2,1,0:T(2,128)(2,1)}), bf16[64,2,128]{2,1,0:T(2,128)(2,1)S(1)}, u32[]{:S(2)}, u32[]{:S(2)}) async-start(bf16[64,2,128]{2,1,0:T(2,128)(2,1)} %reshape.242), calls=%async_computation.2 | async-start | bytes 65536 | tf_op jit(solution)/shard_map/down_reduction/all_to_all | solution.py:103
Sparse Core Ops, SparseCore 0:
  10.1 43.2 all-gather.4

commit v14 on v12

--- a/solution.py
+++ b/solution.py
@@ -228,14 +228,22 @@
         ).reshape(requests, slabs * slab_rows)
     with jax.named_scope("down_reduction"):
         reducers = lax.axis_size("seq") * lax.axis_size("tp")
-        pieces = down_part.reshape(requests, reducers, -1).transpose(1, 0, 2)
+        lanes = 128
+        pieces = (
+            down_part.reshape(requests, reducers, -1)
+            .transpose(1, 0, 2)
+            .reshape(reducers, -1, lanes)
+            .astype(jnp.bfloat16)
+        )
         own_piece = (
-            lax.all_to_all(pieces.astype(jnp.bfloat16), ("seq", "tp"), 0, 0, tiled=True)
+            lax.all_to_all(pieces, ("seq", "tp"), 0, 0, tiled=True)
             .astype(jnp.float32)
             .sum(axis=0)
         )
         every_piece = gather_by_exchange(own_piece.astype(jnp.bfloat16), ("seq", "tp"))
-        down_total = every_piece.transpose(1, 0, 2).reshape(requests, -1)
+        down_total = (
+            every_piece.reshape(reducers, requests, -1).transpose(1, 0, 2).reshape(requests, -1)
+        )
     updated_hidden = (mixed_stream + down_total.astype(jnp.float32)).astype(jnp.bfloat16)
     return (updated_hidden, new_keys, new_values)
 

time: 115 us -> 115 us (level)
    unnamed x23 -> x19, local copies, waits for them, and re-layouts: 2.64 us -> 1.56 us
where the time goes in v14:
time: 115 us
  blocking collectives  56.1 us (49%)
  waiting for transfers between devices  18.6 us (16%)
  between operations  14.4 us (13%)
  starting transfers between devices  11.1 us (10%)
  local copies, waits for them, and re-layouts  7.06 us (6%)
  other arithmetic  2.84 us (2%)
  matrix products  2.63 us (2%)
  Pallas kernels  1.97 us (2%)
    all_gather x1, blocking collectives, gathered_sum(): return jnp.sum(lax.all_gather(x, axis), axis=0)  25.8 us
    all_to_all x2, waiting for transfers between devices, gather_by_exchange(): return lax.all_to_all(copies, axes, 0, 0, tiled=True)  18.6 us
    all_gather x1, blocking collectives, per_device(): every_state = lax.all_gather(state, 'seq')  15.9 us
    all_to_all x1, blocking collectives, per_device(): lax.all_to_all(pieces, ('seq', 'tp'), 0, 0, tiled=True).astype(jnp.float32)  14.4 us
    all_to_all x2, starting transfers between devices, gather_by_exchange(): return lax.all_to_all(copies, axes, 0, 0, tiled=True)  11.1 us
  transfers between devices with their start and end apart: 3, of which 2 were waited for; matrix products, arithmetic and copies ran while one was open for 6% of the time, Pallas kernels for 0%

profile of v14, /device:TPU:1, one launch (start us, length us, event | category | flops | bytes accessed | tf_op | source)
XLA Modules:
  0.0 114.7 jit_solution(852723105155082324)
XLA Ops:
  7.2 0.0 copy-start
  7.2 0.0 copy-start.7
  7.2 0.0 copy-start.1
  7.2 0.0 all-gather.5.cloned.1.call-start
  7.3 2.0 %qkv_projection.1 = (f32[8,768]{1,0:T(8,128)}, bf16[384,256]{1,0:T(8,128)(2,1)}) custom-call(s32[1]{0:T(128)} %bitcast.block_ref, bf16[8,2048]{1,0:T(8,128)(2,1)} %hidden_ref.1, bf16[2048]{0:T(1024)(128)(2,1)} %gain_ref.1, bf16[128,512]{1,0:T(8,128)(2,1)} %query_ref.1, bf16[128,128]{1,0:T(8,128)(2,1)} %key_ref.1, bf16[128,128]{1,0:T(8,128)(2,1)} %value_ref.1, ...), custom_call_target="tpu_custom_call" | custom-call | flops 1572864 | bytes 651264 | tf_op jit(solution)/shard_map/qkv_projection/pallas_call | solution.py:75
  9.2 0.0 all-gather.5.cloned.1.call-update
  9.3 25.8 %all-gather = f32[128,768]{1,0:T(8,128)S(1)} all-gather(f32[8,768]{1,0:T(8,128)} %get-tuple-element.5), channel_id=2, replica_groups=mesh['seq'=16,'mlp'=8,'tp'=4] {'seq'}, dimensions={0}, use_global_device_ids=true | all-gather | bytes 417792 | tf_op jit(solution)/shard_map/qkv_projection/all_gather | solution.py:95
  35.1 0.0 copy-start.4
  35.1 0.0 copy-start.5
  35.1 0.1 reshape.183
  35.2 0.1 broadcast_compare_fusion
  35.3 0.5 copy.138
  35.8 0.1 multiply_cosine_fusion
  36.0 0.1 subtract_convert_fusion
  36.1 0.4 select_reduce_fusion
  36.5 0.2 fusion.5
  36.7 0.2 copy.143
  36.9 0.5 copy.141
  37.4 0.0 slice-start
  37.4 0.4 fusion.6
  37.9 0.2 copy.142
  38.1 0.1 pad_maximum_fusion
  38.2 15.9 %all-gather.1 = f32[128,2,4,66]{3,2,1,0:T(4,128)S(1)} all-gather(f32[8,2,4,66]{3,2,1,0:T(4,128)S(1)} %pad_maximum_fusion), channel_id=3, replica_groups=mesh['seq'=16,'mlp'=8,'tp'=4] {'seq'}, dimensions={0}, use_global_device_ids=true | all-gather | bytes 287232 | tf_op jit(solution)/shard_map/softmax_merge/all_gather | solution.py:184
  54.1 0.1 copy.165
  54.2 0.1 reshape.186
  54.3 0.1 multiply_subtract_fusion
  54.4 0.1 fusion.24
  54.5 0.2 multiply_reduce_fusion.1
  54.6 0.1 copy.147
  54.7 0.3 fusion.26
  55.0 0.0 copy-start.6
  55.0 0.0 copy-start.3
  55.0 0.5 copy.150
  55.5 0.5 copy.162
  56.0 0.1 exponential_bitcast_fusion
  56.1 0.1 copy.148
  56.1 0.0 copy-done.5
  56.1 0.1 reshape.190
  56.2 0.2 fusion.13
  56.4 0.3 fusion.3
  56.8 0.1 divide_convert_fusion
  56.9 0.1 convert_element_type.99
  57.0 0.1 convolution_convert_fusion.1
  57.1 0.7 broadcast_in_dim.31
  57.8 6.1 %all-to-all-start = ((bf16[64,8,128]{2,1,0:T(8,128)(2,1)}), bf16[64,8,128]{2,1,0:T(8,128)(2,1)S(1)}, u32[]{:S(2)}, u32[]{:S(2)}) async-start(bf16[64,8,128]{2,1,0:T(8,128)(2,1)} %broadcast_in_dim.31), calls=%async_computation | async-start | bytes 262144 | tf_op jit(solution)/shard_map/output_projection/all_to_all | solution.py:103
  63.9 10.0 %all-to-all-done = bf16[64,8,128]{2,1,0:T(8,128)(2,1)S(1)} async-done(((bf16[64,8,128]{2,1,0:T(8,128)(2,1)}), bf16[64,8,128]{2,1,0:T(8,128)(2,1)S(1)}, u32[]{:S(2)}, u32[]{:S(2)}) %all-to-all-start) | async-done | bytes 131104 | tf_op jit(solution)/shard_map/output_projection/all_to_all | solution.py:103
  74.0 0.1 multiply_reduce_fusion
  74.1 0.0 all-gather.5.cloned.1.call-done
  74.2 1.3 %fusion.25 = (bf16[8,256,128]{2,1,0:T(8,128)(2,1)S(1)}, bf16[8,256,128]{2,1,0:T(8,128)(2,1)S(1)}) fusion(bf16[8,384,256]{2,1,0:T(8,128)(2,1)} %bitcast.63), kind=kLoop, calls=%fused_computation.60 | loop fusion | bytes 2097152 | tf_op jit(solution)/shard_map/slice | solution.py:142
  75.4 0.2 fusion.22
  75.7 1.4 %convolution_convert_fusion = bf16[8,8,256]{2,0,1:T(8,128)(2,1)S(1)} fusion(bf16[2048,128]{1,0:T(8,128)(2,1)S(1)} %bitcast.61, bf16[8,384,256]{2,1,0:T(8,128)(2,1)} %bitcast.64, f32[8,128]{1,0:T(8,128)S(1)} %fusion.22, bf16[16,8,128]{2,1,0:T(8,128)(2,1)S(1)} %bitcast_reduce_fusion.1, bf16[8,2048]{1,0:T(8,128)(2,1)S(1)} %copy-done.3, ...), kind=kOutput, calls=%fused_computation.1 | convolution fusion | flops 8509440 | bytes 1159200 | tf_op jit(solution)/shard_map/feed_forward/rh,jhc->rjc/dot_general | solution.py:226
  77.1 0.1 convert_element_type.108
  77.3 0.1 copy.153
  77.4 0.1 copy.154
  77.5 14.4 %all_to_all.15 = bf16[64,2,128]{2,1,0:T(2,128)(2,1)S(1)} all-to-all(bf16[64,2,128]{2,1,0:T(2,128)(2,1)S(1)} %copy.154), channel_id=1, replica_groups=mesh['seq'=16,'mlp'=8,'tp'=4] {'seq','tp'}, dimensions={0} | all-to-all | bytes 65536 | tf_op jit(solution)/shard_map/down_reduction/all_to_all | solution.py:239
  91.9 0.1 reduce_sum.85
  92.0 0.6 broadcast_in_dim.32
  92.6 4.9 %all-to-all-start.2 = ((bf16[64,2,128]{2,1,0:T(2,128)(2,1)}), bf16[64,2,128]{2,1,0:T(2,128)(2,1)S(1)}, u32[]{:S(2)}, u32[]{:S(2)}) async-start(bf16[64,2,128]{2,1,0:T(2,128)(2,1)} %broadcast_in_dim.32), calls=%async_computation.2 | async-start | bytes 65536 | tf_op jit(solution)/shard_map/down_reduction/all_to_all | solution.py:103
  97.6 0.7 convert_element_type.116
  98.2 8.6 %all-to-all-done.2 = bf16[64,2,128]{2,1,0:T(2,128)(2,1)S(1)} async-done(((bf16[64,2,128]{2,1,0:T(2,128)(2,1)}), bf16[64,2,128]{2,1,0:T(2,128)(2,1)S(1)}, u32[]{:S(2)}, u32[]{:S(2)}) %all-to-all-start.2) | async-done | bytes 32800 | tf_op jit(solution)/shard_map/down_reduction/all_to_all | solution.py:103
  106.8 0.1 copy.155
  107.0 0.1 copy.156
  107.1 0.1 reshape.192
  107.2 0.6 add_convert_fusion
  (24 shorter events, 0.2 us)
Async XLA Ops:
  7.2 49.8 %copy-start = (bf16[512,128]{1,0:T(8,128)(2,1)S(1)}, bf16[512,128]{1,0:T(8,128)(2,1)}, u32[]{:S(2)}) copy-start(bf16[512,128]{1,0:T(8,128)(2,1)} %param.21) | copy-start | bytes 393220
  7.2 28.0 %copy-start.7 = (s32[8]{0:T(128)S(1)}, s32[8]{0:T(128)}, u32[]{:S(2)}) copy-start(s32[8]{0:T(128)} %param.14) | copy-start | bytes 100
  7.2 28.1 %copy-start.1 = (bf16[8,512,128]{2,1,0:T(8,128)(2,1)S(1)}, bf16[8,512,128]{2,1,0:T(8,128)(2,1)}, u32[]{:S(2)}) copy-start(bf16[8,512,128]{2,1,0:T(8,128)(2,1)} %param.19) | copy-start | bytes 3145732
  7.2 67.0 %all-gather.5.cloned.1.call-start = ((), (), s32[]{:S(2)}) async-start(), calls=%async_computation.3 | async-start | bytes 1769472 | tf_op jit(solution)/shard_map/mlp_weight_gather/all_gather | solution.py:140
  35.1 1.4 %copy-start.4 = (f32[8,768]{1,0:T(8,128)}, f32[8,768]{1,0:T(8,128)S(1)}, u32[]{:S(2)}) copy-start(f32[8,768]{1,0:T(8,128)S(1)} %bitcast_reduce_fusion) | copy-start | bytes 73732
  35.1 21.0 %copy-start.5 = (bf16[8,128]{1,0:T(8,128)(2,1)}, bf16[8,128]{1,0:T(8,128)(2,1)S(1)}, u32[]{:S(2)}) copy-start(bf16[8,128]{1,0:T(8,128)(2,1)S(1)} %slice.81) | copy-start | bytes 6148
  35.3 1.6 %copy-start.2 = (bf16[8,512,128]{2,1,0:T(8,128)(2,1)S(1)}, bf16[8,512,128]{2,1,0:T(8,128)(2,1)}, u32[]{:S(2)}) copy-start(bf16[8,512,128]{2,1,0:T(8,128)(2,1)} %param.20) | copy-start | bytes 3145732
  37.4 16.8 %slice-start = ((f32[8,768]{1,0:T(8,128)}), f32[8,128]{1,0:T(8,128)S(1)}, s32[]{:S(2)}) async-start(f32[8,768]{1,0:T(8,128)} %copy-done.4), calls=%async_computation.4 | async-start | bytes 8192 | tf_op jit(solution)/shard_map/slice | solution.py:148
  55.0 8.9 %copy-start.6 = (bf16[2048]{0:T(1024)(128)(2,1)S(1)}, bf16[2048]{0:T(1024)(128)(2,1)}, u32[]{:S(2)}) copy-start(bf16[2048]{0:T(1024)(128)(2,1)} %param.22) | copy-start | bytes 12292
  55.0 19.0 %copy-start.3 = (bf16[8,2048]{1,0:T(8,128)(2,1)S(1)}, bf16[8,2048]{1,0:T(8,128)(2,1)}, u32[]{:S(2)}) copy-start(bf16[8,2048]{1,0:T(8,128)(2,1)} %hidden_ref.1) | copy-start | bytes 98308
  57.8 16.2 %all-to-all-start = ((bf16[64,8,128]{2,1,0:T(8,128)(2,1)}), bf16[64,8,128]{2,1,0:T(8,128)(2,1)S(1)}, u32[]{:S(2)}, u32[]{:S(2)}) async-start(bf16[64,8,128]{2,1,0:T(8,128)(2,1)} %broadcast_in_dim.31), calls=%async_computation | async-start | bytes 262144 | tf_op jit(solution)/shard_map/output_projection/all_to_all | solution.py:103
  92.6 14.2 %all-to-all-start.2 = ((bf16[64,2,128]{2,1,0:T(2,128)(2,1)}), bf16[64,2,128]{2,1,0:T(2,128)(2,1)S(1)}, u32[]{:S(2)}, u32[]{:S(2)}) async-start(bf16[64,2,128]{2,1,0:T(2,128)(2,1)} %broadcast_in_dim.32), calls=%async_computation.2 | async-start | bytes 65536 | tf_op jit(solution)/shard_map/down_reduction/all_to_all | solution.py:103
Sparse Core Ops, SparseCore 0:
  10.1 43.2 all-gather.4

commit v15 on v14

--- a/solution.py
+++ b/solution.py
@@ -181,7 +181,9 @@
         )
     with jax.named_scope("softmax_merge"):
         state = jnp.concatenate([block_max[..., None], block_sum[..., None], block_acc], axis=-1)
-        every_state = lax.all_gather(state, "seq")
+        every_state = lax.all_gather(
+            state.reshape(requests, local_heads, HD + 2), "seq"
+        ).reshape((-1,) + state.shape)
         every_max = every_state[..., 0]
         every_sum = every_state[..., 1]
         every_acc = every_state[..., 2:]

time: 115 us -> 118 us (1.026)
  other arithmetic: 2.84 us -> 4.54 us
    all_gather x1, local copies, waits for them, and re-layouts: 0.1 us -> 2.02 us  [per_device(): lax.all_gather(state.reshape(requests, local_heads, HD + 2), 'seq')]
  transfers between devices with their start and end apart: 3 -> 3, of which waited for: 2 -> 2; matrix products, arithmetic and copies ran while one was open for 6% -> 9% of each run, Pallas kernels for 0% -> 0%
where the time goes in v15:
time: 118 us; the launch traced here: 117 us
  blocking collectives  56.1 us (48%)
  waiting for transfers between devices  18.6 us (16%)
  between operations  14.3 us (12%)
  starting transfers between devices  11.1 us (9%)
  local copies, waits for them, and re-layouts  8.14 us (7%)
  other arithmetic  4.54 us (4%)
  matrix products  2.63 us (2%)
  Pallas kernels  1.97 us (2%)
    all_gather x1, blocking collectives, gathered_sum(): return jnp.sum(lax.all_gather(x, axis), axis=0)  25.8 us
    all_to_all x2, waiting for transfers between devices, gather_by_exchange(): return lax.all_to_all(copies, axes, 0, 0, tiled=True)  18.6 us
    all_gather x1, blocking collectives, per_device(): lax.all_gather(state.reshape(requests, local_heads, HD + 2), 'seq')  15.9 us
    all_to_all x1, blocking collectives, per_device(): lax.all_to_all(pieces, ('seq', 'tp'), 0, 0, tiled=True).astype(jnp.float32)  14.4 us
    all_to_all x2, starting transfers between devices, gather_by_exchange(): return lax.all_to_all(copies, axes, 0, 0, tiled=True)  11.1 us
  transfers between devices with their start and end apart: 3, of which 2 were waited for; matrix products, arithmetic and copies ran while one was open for 9% of the time, Pallas kernels for 0%

profile of v15, /device:TPU:1, one launch (start us, length us, event | category | flops | bytes accessed | tf_op | source)
XLA Modules:
  0.0 117.4 jit_solution(6596153188814344107)
XLA Ops:
  7.2 0.0 copy-start
  7.2 0.0 copy-start.1
  7.2 0.0 all-gather.4.cloned.1.call-start
  7.2 2.0 %qkv_projection.1 = (f32[8,768]{1,0:T(8,128)}, bf16[384,256]{1,0:T(8,128)(2,1)}) custom-call(s32[1]{0:T(128)} %bitcast.block_ref, bf16[8,2048]{1,0:T(8,128)(2,1)} %hidden_ref.1, bf16[2048]{0:T(1024)(128)(2,1)} %gain_ref.1, bf16[128,512]{1,0:T(8,128)(2,1)} %query_ref.1, bf16[128,128]{1,0:T(8,128)(2,1)} %key_ref.1, bf16[128,128]{1,0:T(8,128)(2,1)} %value_ref.1, ...), custom_call_target="tpu_custom_call" | custom-call | flops 1572864 | bytes 651264 | tf_op jit(solution)/shard_map/qkv_projection/pallas_call | solution.py:75
  9.2 0.0 all-gather.4.cloned.1.call-update
  9.3 25.8 %all-gather = f32[128,768]{1,0:T(8,128)S(1)} all-gather(f32[8,768]{1,0:T(8,128)} %get-tuple-element.5), channel_id=2, replica_groups=mesh['seq'=16,'mlp'=8,'tp'=4] {'seq'}, dimensions={0}, use_global_device_ids=true | all-gather | bytes 417792 | tf_op jit(solution)/shard_map/qkv_projection/all_gather | solution.py:95
  35.1 0.0 copy-start.4
  35.1 0.1 reshape.192
  35.2 0.7 convert_element_type.93
  35.9 0.7 broadcast_compare_fusion
  36.7 0.0 copy-done.1
  36.7 0.5 copy.98
  37.2 0.1 multiply_cosine_fusion
  37.3 0.1 subtract_convert_fusion
  37.4 0.4 select_reduce_fusion
  37.8 0.1 copy.99
  37.9 0.2 fusion.5
  38.1 0.1 copy.100
  38.2 0.1 copy.103
  38.3 0.5 copy.101
  38.9 0.4 fusion.6
  39.3 0.1 copy.102
  39.4 0.1 pad_maximum_fusion
  39.5 15.9 %all_gather.17 = f32[16,8,8,66]{3,2,1,0:T(8,128)S(1)} all-gather(f32[1,8,8,66]{3,2,1,0:T(8,128)S(1)} %pad_maximum_fusion), channel_id=1, replica_groups=mesh['seq'=16,'mlp'=8,'tp'=4] {'seq'}, dimensions={0}, use_global_device_ids=true | all-gather | bytes 287232 | tf_op jit(solution)/shard_map/softmax_merge/all_gather | solution.py:184
  55.5 0.0 slice-start
  55.5 2.0 %copy.104 = f32[16,8,8,66]{0,1,2,3:T(8,128)S(1)} copy(f32[16,8,8,66]{3,2,1,0:T(8,128)S(1)} %all_gather.17) | data formatting | bytes 540672 | tf_op jit(solution)/shard_map/softmax_merge/all_gather | solution.py:184
  57.5 0.0 copy-start.6
  57.5 0.0 copy-start.3
  57.5 0.1 reshape.196
  57.6 0.1 multiply_subtract_fusion
  57.7 0.1 fusion.24
  57.8 0.2 multiply_reduce_fusion.1
  58.0 0.1 copy.105
  58.1 0.1 slice_reduce_fusion
  58.2 0.1 exponential_bitcast_fusion
  58.3 0.8 fusion
  59.1 0.1 copy.107
  59.2 0.0 copy-done.5
  59.2 0.1 reshape.200
  59.3 0.2 fusion.12
  59.5 0.1 divide_convert_fusion
  59.6 0.1 convert_element_type.99
  59.7 0.1 convolution_convert_fusion.1
  59.8 0.7 broadcast_in_dim.25
  60.5 6.1 %all-to-all-start = ((bf16[64,8,128]{2,1,0:T(8,128)(2,1)}), bf16[64,8,128]{2,1,0:T(8,128)(2,1)S(1)}, u32[]{:S(2)}, u32[]{:S(2)}) async-start(bf16[64,8,128]{2,1,0:T(8,128)(2,1)} %broadcast_in_dim.25), calls=%async_computation | async-start | bytes 262144 | tf_op jit(solution)/shard_map/output_projection/all_to_all | solution.py:103
  66.7 10.0 %all-to-all-done = bf16[64,8,128]{2,1,0:T(8,128)(2,1)S(1)} async-done(((bf16[64,8,128]{2,1,0:T(8,128)(2,1)}), bf16[64,8,128]{2,1,0:T(8,128)(2,1)S(1)}, u32[]{:S(2)}, u32[]{:S(2)}) %all-to-all-start) | async-done | bytes 131104 | tf_op jit(solution)/shard_map/output_projection/all_to_all | solution.py:103
  76.7 0.1 multiply_reduce_fusion
  76.9 0.0 all-gather.4.cloned.1.call-done
  76.9 1.3 %fusion.25 = (bf16[8,256,128]{2,1,0:T(8,128)(2,1)S(1)}, bf16[8,256,128]{2,1,0:T(8,128)(2,1)S(1)}) fusion(bf16[8,384,256]{2,1,0:T(8,128)(2,1)} %bitcast.66), kind=kLoop, calls=%fused_computation.60 | loop fusion | bytes 2097152 | tf_op jit(solution)/shard_map/slice | solution.py:142
  78.2 0.2 fusion.22
  78.4 1.4 %convolution_convert_fusion = bf16[8,8,256]{2,0,1:T(8,128)(2,1)S(1)} fusion(bf16[2048,128]{1,0:T(8,128)(2,1)S(1)} %bitcast.64, bf16[8,384,256]{2,1,0:T(8,128)(2,1)} %bitcast.67, f32[8,128]{1,0:T(8,128)S(1)} %fusion.22, bf16[16,8,128]{2,1,0:T(8,128)(2,1)S(1)} %bitcast_reduce_fusion.1, bf16[8,2048]{1,0:T(8,128)(2,1)S(1)} %copy-done.3, ...), kind=kOutput, calls=%fused_computation.3 | convolution fusion | flops 8509440 | bytes 1159200 | tf_op jit(solution)/shard_map/feed_forward/rh,jhc->rjc/dot_general | solution.py:228
  79.9 0.1 convert_element_type.108
  80.0 0.1 copy.110
  80.1 0.1 copy.111
  80.2 14.4 %all_to_all.15 = bf16[64,2,128]{2,1,0:T(2,128)(2,1)S(1)} all-to-all(bf16[64,2,128]{2,1,0:T(2,128)(2,1)S(1)} %copy.111), channel_id=1, replica_groups=mesh['seq'=16,'mlp'=8,'tp'=4] {'seq','tp'}, dimensions={0} | all-to-all | bytes 65536 | tf_op jit(solution)/shard_map/down_reduction/all_to_all | solution.py:241
  94.6 0.1 reduce_sum.85
  94.7 0.6 broadcast_in_dim.26
  95.4 4.9 %all-to-all-start.2 = ((bf16[64,2,128]{2,1,0:T(2,128)(2,1)}), bf16[64,2,128]{2,1,0:T(2,128)(2,1)S(1)}, u32[]{:S(2)}, u32[]{:S(2)}) async-start(bf16[64,2,128]{2,1,0:T(2,128)(2,1)} %broadcast_in_dim.26), calls=%async_computation.2 | async-start | bytes 65536 | tf_op jit(solution)/shard_map/down_reduction/all_to_all | solution.py:103
  100.3 0.7 convert_element_type.116
  101.0 8.6 %all-to-all-done.2 = bf16[64,2,128]{2,1,0:T(2,128)(2,1)S(1)} async-done(((bf16[64,2,128]{2,1,0:T(2,128)(2,1)}), bf16[64,2,128]{2,1,0:T(2,128)(2,1)S(1)}, u32[]{:S(2)}, u32[]{:S(2)}) %all-to-all-start.2) | async-done | bytes 32800 | tf_op jit(solution)/shard_map/down_reduction/all_to_all | solution.py:103
  109.5 0.1 copy.112
  109.7 0.1 copy.113
  109.8 0.1 reshape.202
  110.0 0.6 add_convert_fusion
  (22 shorter events, 0.2 us)
Async XLA Ops:
  7.2 52.5 %copy-start = (bf16[512,128]{1,0:T(8,128)(2,1)S(1)}, bf16[512,128]{1,0:T(8,128)(2,1)}, u32[]{:S(2)}) copy-start(bf16[512,128]{1,0:T(8,128)(2,1)} %param.21) | copy-start | bytes 393220
  7.2 29.5 %copy-start.1 = (bf16[8,512,128]{2,1,0:T(8,128)(2,1)S(1)}, bf16[8,512,128]{2,1,0:T(8,128)(2,1)}, u32[]{:S(2)}) copy-start(bf16[8,512,128]{2,1,0:T(8,128)(2,1)} %param.19) | copy-start | bytes 3145732
  7.2 69.7 %all-gather.4.cloned.1.call-start = ((), (), s32[]{:S(2)}) async-start(), calls=%async_computation.3 | async-start | bytes 1769472 | tf_op jit(solution)/shard_map/mlp_weight_gather/all_gather | solution.py:140
  35.1 3.3 %copy-start.2 = (bf16[8,512,128]{2,1,0:T(8,128)(2,1)S(1)}, bf16[8,512,128]{2,1,0:T(8,128)(2,1)}, u32[]{:S(2)}) copy-start(bf16[8,512,128]{2,1,0:T(8,128)(2,1)} %param.20) | copy-start | bytes 3145732
  35.1 20.4 %copy-start.4 = (f32[8,768]{1,0:T(8,128)}, f32[8,768]{1,0:T(8,128)S(1)}, u32[]{:S(2)}) copy-start(f32[8,768]{1,0:T(8,128)S(1)} %bitcast_reduce_fusion) | copy-start | bytes 73732
  55.5 3.7 %copy-start.5 = (bf16[8,128]{1,0:T(8,128)(2,1)}, bf16[8,128]{1,0:T(8,128)(2,1)S(1)}, u32[]{:S(2)}) copy-start(bf16[8,128]{1,0:T(8,128)(2,1)S(1)} %slice.88) | copy-start | bytes 6148
  55.5 2.0 %slice-start = ((f32[8,768]{1,0:T(8,128)}), f32[8,128]{1,0:T(8,128)S(1)}, s32[]{:S(2)}) async-start(f32[8,768]{1,0:T(8,128)} %copy-done.4), calls=%async_computation.4 | async-start | bytes 8192 | tf_op jit(solution)/shard_map/slice | solution.py:148
  57.5 9.2 %copy-start.6 = (bf16[2048]{0:T(1024)(128)(2,1)S(1)}, bf16[2048]{0:T(1024)(128)(2,1)}, u32[]{:S(2)}) copy-start(bf16[2048]{0:T(1024)(128)(2,1)} %param.22) | copy-start | bytes 12292
  57.5 19.2 %copy-start.3 = (bf16[8,2048]{1,0:T(8,128)(2,1)S(1)}, bf16[8,2048]{1,0:T(8,128)(2,1)}, u32[]{:S(2)}) copy-start(bf16[8,2048]{1,0:T(8,128)(2,1)} %hidden_ref.1) | copy-start | bytes 98308
  60.5 16.2 %all-to-all-start = ((bf16[64,8,128]{2,1,0:T(8,128)(2,1)}), bf16[64,8,128]{2,1,0:T(8,128)(2,1)S(1)}, u32[]{:S(2)}, u32[]{:S(2)}) async-start(bf16[64,8,128]{2,1,0:T(8,128)(2,1)} %broadcast_in_dim.25), calls=%async_computation | async-start | bytes 262144 | tf_op jit(solution)/shard_map/output_projection/all_to_all | solution.py:103
  95.4 14.2 %all-to-all-start.2 = ((bf16[64,2,128]{2,1,0:T(2,128)(2,1)}), bf16[64,2,128]{2,1,0:T(2,128)(2,1)S(1)}, u32[]{:S(2)}, u32[]{:S(2)}) async-start(bf16[64,2,128]{2,1,0:T(2,128)(2,1)} %broadcast_in_dim.26), calls=%async_computation.2 | async-start | bytes 65536 | tf_op jit(solution)/shard_map/down_reduction/all_to_all | solution.py:103
Sparse Core Ops, SparseCore 0:
  10.1 43.1 all-gather.3

commit v16 on v14

--- a/solution.py
+++ b/solution.py
@@ -240,11 +240,13 @@
             .astype(jnp.float32)
             .sum(axis=0)
         )
-        every_piece = gather_by_exchange(own_piece.astype(jnp.bfloat16), ("seq", "tp"))
-        down_total = (
-            every_piece.reshape(reducers, requests, -1).transpose(1, 0, 2).reshape(requests, -1)
-        )
-    updated_hidden = (mixed_stream + down_total.astype(jnp.float32)).astype(jnp.bfloat16)
+        piece_width = down_part.shape[1] // reducers
+        me = lax.axis_index("seq") * lax.axis_size("tp") + lax.axis_index("tp")
+        own_stream = lax.dynamic_slice_in_dim(mixed_stream, me * piece_width, piece_width, 1)
+        own_down = own_piece.astype(jnp.bfloat16).reshape(requests, piece_width)
+        own_updated = (own_stream + own_down.astype(jnp.float32)).astype(jnp.bfloat16)
+        every_piece = gather_by_exchange(own_updated, ("seq", "tp"))
+    updated_hidden = every_piece.transpose(1, 0, 2).reshape(requests, -1)
     return (updated_hidden, new_keys, new_values)
 
 

time: 115 us -> 117 us (1.017)
  blocking collectives: 56.1 us -> 41.7 us
  waiting for transfers between devices: 18.6 us -> 27.8 us
  starting transfers between devices: 11.1 us -> 17 us
  local copies, waits for them, and re-layouts: 7.06 us -> 8.41 us
    all_to_all x1 -> x0, blocking collectives: 14.4 us -> none  [per_device(): lax.all_to_all(pieces, ('seq', 'tp'), 0, 0, tiled=True).astype(jnp.float32)]
    all_to_all x0 -> x1, waiting for transfers between devices: none -> 9.22 us  [per_device(): lax.all_to_all(pieces, ('seq', 'tp'), 0, 0, tiled=True).astype(jnp.float32)]
    all_to_all x0 -> x1, starting transfers between devices: none -> 5.89 us  [per_device(): lax.all_to_all(pieces, ('seq', 'tp'), 0, 0, tiled=True).astype(jnp.float32)]
    unnamed x19 -> x23, local copies, waits for them, and re-layouts: 1.56 us -> 2.42 us
  transfers between devices with their start and end apart: 3 -> 4, of which waited for: 2 -> 3; matrix products, arithmetic and copies ran while one was open for 6% -> 7% of each run, Pallas kernels for 0% -> 0%
where the time goes in v16:
time: 117 us
  blocking collectives  41.7 us (36%)
  waiting for transfers between devices  27.8 us (24%)
  starting transfers between devices  17 us (15%)
  between operations  14.4 us (12%)
  local copies, waits for them, and re-layouts  8.41 us (7%)
  other arithmetic  2.93 us (3%)
  matrix products  2.63 us (2%)
  Pallas kernels  1.97 us (2%)
    all_gather x1, blocking collectives, gathered_sum(): return jnp.sum(lax.all_gather(x, axis), axis=0)  25.8 us
    all_to_all x2, waiting for transfers between devices, gather_by_exchange(): return lax.all_to_all(copies, axes, 0, 0, tiled=True)  18.6 us
    all_gather x1, blocking collectives, per_device(): every_state = lax.all_gather(state, 'seq')  15.9 us
    all_to_all x2, starting transfers between devices, gather_by_exchange(): return lax.all_to_all(copies, axes, 0, 0, tiled=True)  11.1 us
    all_to_all x1, waiting for transfers between devices, per_device(): lax.all_to_all(pieces, ('seq', 'tp'), 0, 0, tiled=True).astype(jnp.float32)  9.22 us
    all_to_all x1, starting transfers between devices, per_device(): lax.all_to_all(pieces, ('seq', 'tp'), 0, 0, tiled=True).astype(jnp.float32)  5.89 us
    unnamed x23, local copies, waits for them, and re-layouts  2.42 us
  transfers between devices with their start and end apart: 4, of which 3 were waited for; matrix products, arithmetic and copies ran while one was open for 7% of the time, Pallas kernels for 0%

profile of v16, /device:TPU:1, one launch (start us, length us, event | category | flops | bytes accessed | tf_op | source)
XLA Modules:
  0.0 116.9 jit_solution(6643788302515988236)
XLA Ops:
  7.2 0.0 copy-start
  7.2 0.0 copy-start.8
  7.2 0.0 all-gather.5.cloned.1.call-start
  7.3 2.0 %qkv_projection.1 = (f32[8,768]{1,0:T(8,128)}, bf16[384,256]{1,0:T(8,128)(2,1)}) custom-call(s32[1]{0:T(128)} %bitcast.block_ref, bf16[8,2048]{1,0:T(8,128)(2,1)} %hidden_ref.1, bf16[2048]{0:T(1024)(128)(2,1)} %gain_ref.1, bf16[128,512]{1,0:T(8,128)(2,1)} %query_ref.1, bf16[128,128]{1,0:T(8,128)(2,1)} %key_ref.1, bf16[128,128]{1,0:T(8,128)(2,1)} %value_ref.1, ...), custom_call_target="tpu_custom_call" | custom-call | flops 1572864 | bytes 651264 | tf_op jit(solution)/shard_map/qkv_projection/pallas_call | solution.py:75
  9.2 0.0 all-gather.5.cloned.1.call-update
  9.3 25.8 %all-gather = f32[128,768]{1,0:T(8,128)S(1)} all-gather(f32[8,768]{1,0:T(8,128)} %get-tuple-element.5), channel_id=2, replica_groups=mesh['seq'=16,'mlp'=8,'tp'=4] {'seq'}, dimensions={0}, use_global_device_ids=true | all-gather | bytes 417792 | tf_op jit(solution)/shard_map/qkv_projection/all_gather | solution.py:95
  35.1 0.0 copy-start.4
  35.1 0.1 reshape.183
  35.2 0.7 convert_element_type.87
  35.9 0.1 broadcast_compare_fusion
  35.9 0.5 copy.131
  36.5 0.1 multiply_cosine_fusion
  36.6 0.1 subtract_convert_fusion
  36.7 0.4 select_reduce_fusion
  37.1 0.2 fusion.5
  37.3 0.2 copy.136
  37.5 0.5 copy.134
  38.1 0.0 copy-start.5
  38.1 0.4 fusion.6
  38.5 0.2 copy.135
  38.7 0.1 reshape.186
  38.8 0.1 multiply_subtract_fusion
  38.9 0.1 pad_maximum_fusion
  39.0 15.9 %all-gather.1 = f32[128,2,4,66]{3,2,1,0:T(4,128)S(1)} all-gather(f32[8,2,4,66]{3,2,1,0:T(4,128)S(1)} %pad_maximum_fusion), channel_id=3, replica_groups=mesh['seq'=16,'mlp'=8,'tp'=4] {'seq'}, dimensions={0}, use_global_device_ids=true | all-gather | bytes 287232 | tf_op jit(solution)/shard_map/softmax_merge/all_gather | solution.py:184
  54.9 0.1 copy.157
  55.0 0.1 fusion.24
  55.1 0.2 multiply_reduce_fusion.1
  55.3 0.1 copy.140
  55.4 0.3 fusion.26
  55.7 0.0 copy-start.7
  55.7 0.0 copy-start.3
  55.7 0.5 copy.143
  56.1 0.5 copy.154
  56.6 0.1 exponential_bitcast_fusion
  56.7 0.1 copy.141
  56.8 0.0 copy-done.6
  56.8 0.1 reshape.191
  56.9 0.2 fusion.13
  57.0 0.3 fusion.3
  57.4 0.1 divide_convert_fusion
  57.5 0.1 convert_element_type.93
  57.6 0.1 convolution_convert_fusion.1
  57.7 0.7 broadcast_in_dim.31
  58.4 6.1 %all-to-all-start = ((bf16[64,8,128]{2,1,0:T(8,128)(2,1)}), bf16[64,8,128]{2,1,0:T(8,128)(2,1)S(1)}, u32[]{:S(2)}, u32[]{:S(2)}) async-start(bf16[64,8,128]{2,1,0:T(8,128)(2,1)} %broadcast_in_dim.31), calls=%async_computation | async-start | bytes 262144 | tf_op jit(solution)/shard_map/output_projection/all_to_all | solution.py:103
  64.6 10.0 %all-to-all-done = bf16[64,8,128]{2,1,0:T(8,128)(2,1)S(1)} async-done(((bf16[64,8,128]{2,1,0:T(8,128)(2,1)}), bf16[64,8,128]{2,1,0:T(8,128)(2,1)S(1)}, u32[]{:S(2)}, u32[]{:S(2)}) %all-to-all-start) | async-done | bytes 131104 | tf_op jit(solution)/shard_map/output_projection/all_to_all | solution.py:103
  74.6 0.1 bitcast_add_fusion
  74.8 0.0 all-gather.5.cloned.1.call-done
  74.8 1.3 %fusion.25 = (bf16[8,256,128]{2,1,0:T(8,128)(2,1)S(1)}, bf16[8,256,128]{2,1,0:T(8,128)(2,1)S(1)}) fusion(bf16[8,384,256]{2,1,0:T(8,128)(2,1)} %bitcast.58), kind=kLoop, calls=%fused_computation.59 | loop fusion | bytes 2097152 | tf_op jit(solution)/shard_map/slice | solution.py:142
  76.1 0.2 fusion.22
  76.3 1.4 %convolution_convert_fusion = bf16[8,8,256]{2,0,1:T(8,128)(2,1)S(1)} fusion(bf16[2048,128]{1,0:T(8,128)(2,1)S(1)} %bitcast.56, bf16[8,384,256]{2,1,0:T(8,128)(2,1)} %bitcast.59, f32[8,128]{1,0:T(8,128)S(1)} %fusion.22, f32[2048]{0:T(1024)S(1)} %convert_element_type.98, f32[8]{0:T(128)S(1)} %add_rsqrt_fusion, ...), kind=kOutput, calls=%fused_computation.1 | convolution fusion | flops 8509440 | bytes 1159200 | tf_op jit(solution)/shard_map/feed_forward/rh,jhc->rjc/dot_general | solution.py:226
  77.8 0.1 convert_element_type.102
  77.9 0.1 copy.146
  78.0 0.7 copy.147
  78.7 5.9 %all-to-all-start.1 = ((bf16[64,2,128]{2,1,0:T(2,128)(2,1)}), bf16[64,2,128]{2,1,0:T(2,128)(2,1)S(1)}, u32[]{:S(2)}, u32[]{:S(2)}) async-start(bf16[64,2,128]{2,1,0:T(2,128)(2,1)} %copy.147), calls=%async_computation.1 | async-start | bytes 65536 | tf_op jit(solution)/shard_map/down_reduction/all_to_all | solution.py:239
  84.7 9.2 %all-to-all-done.1 = bf16[64,2,128]{2,1,0:T(2,128)(2,1)S(1)} async-done(((bf16[64,2,128]{2,1,0:T(2,128)(2,1)}), bf16[64,2,128]{2,1,0:T(2,128)(2,1)S(1)}, u32[]{:S(2)}, u32[]{:S(2)}) %all-to-all-start.1) | async-done | bytes 32800 | tf_op jit(solution)/shard_map/down_reduction/all_to_all | solution.py:239
  93.9 0.1 reduce_sum.85
  94.0 0.1 reshape.193
  94.0 0.1 add_convert_fusion.1
  94.1 0.7 reshape.198
  94.9 4.9 %all-to-all-start.2 = ((bf16[64,2,128]{2,1,0:T(2,128)(2,1)}), bf16[64,2,128]{2,1,0:T(2,128)(2,1)S(1)}, u32[]{:S(2)}, u32[]{:S(2)}) async-start(bf16[64,2,128]{2,1,0:T(2,128)(2,1)} %reshape.198), calls=%async_computation.2 | async-start | bytes 65536 | tf_op jit(solution)/shard_map/down_reduction/all_to_all | solution.py:103
  99.8 0.7 convert_element_type.108
  100.5 8.6 %all-to-all-done.2 = bf16[64,2,128]{2,1,0:T(2,128)(2,1)S(1)} async-done(((bf16[64,2,128]{2,1,0:T(2,128)(2,1)}), bf16[64,2,128]{2,1,0:T(2,128)(2,1)S(1)}, u32[]{:S(2)}, u32[]{:S(2)}) %all-to-all-start.2) | async-done | bytes 32800 | tf_op jit(solution)/shard_map/down_reduction/all_to_all | solution.py:103
  109.1 0.1 reshape.199
  109.2 0.8 reshape.190
  (28 shorter events, 0.2 us)
Async XLA Ops:
  7.2 50.4 %copy-start = (bf16[512,128]{1,0:T(8,128)(2,1)S(1)}, bf16[512,128]{1,0:T(8,128)(2,1)}, u32[]{:S(2)}) copy-start(bf16[512,128]{1,0:T(8,128)(2,1)} %param.21) | copy-start | bytes 393220
  7.2 28.7 %copy-start.8 = (s32[8]{0:T(128)S(1)}, s32[8]{0:T(128)}, u32[]{:S(2)}) copy-start(s32[8]{0:T(128)} %param.14) | copy-start | bytes 100
  7.2 28.8 %copy-start.1 = (bf16[8,512,128]{2,1,0:T(8,128)(2,1)S(1)}, bf16[8,512,128]{2,1,0:T(8,128)(2,1)}, u32[]{:S(2)}) copy-start(bf16[8,512,128]{2,1,0:T(8,128)(2,1)} %param.19) | copy-start | bytes 3145732
  7.2 67.6 %all-gather.5.cloned.1.call-start = ((), (), s32[]{:S(2)}) async-start(), calls=%async_computation.3 | async-start | bytes 1769472 | tf_op jit(solution)/shard_map/mlp_weight_gather/all_gather | solution.py:140
  35.1 2.0 %copy-start.4 = (f32[8,768]{1,0:T(8,128)}, f32[8,768]{1,0:T(8,128)S(1)}, u32[]{:S(2)}) copy-start(f32[8,768]{1,0:T(8,128)S(1)} %bitcast_reduce_fusion) | copy-start | bytes 73732
  35.9 1.6 %copy-start.2 = (bf16[8,512,128]{2,1,0:T(8,128)(2,1)S(1)}, bf16[8,512,128]{2,1,0:T(8,128)(2,1)}, u32[]{:S(2)}) copy-start(bf16[8,512,128]{2,1,0:T(8,128)(2,1)} %param.20) | copy-start | bytes 3145732
  37.5 1.2 %slice-start = ((f32[8,768]{1,0:T(8,128)}), f32[8,128]{1,0:T(8,128)S(1)}, s32[]{:S(2)}) async-start(f32[8,768]{1,0:T(8,128)} %copy-done.4), calls=%async_computation.4 | async-start | bytes 8192 | tf_op jit(solution)/shard_map/slice | solution.py:148
  38.1 16.8 %copy-start.5 = (f32[8,768]{1,0:T(8,128)S(1)}, f32[8,768]{1,0:T(8,128)}, u32[]{:S(2)}) copy-start(f32[8,768]{1,0:T(8,128)} %copy-done.4) | copy-start | bytes 73732
  54.9 1.9 %copy-start.6 = (bf16[8,128]{1,0:T(8,128)(2,1)}, bf16[8,128]{1,0:T(8,128)(2,1)S(1)}, u32[]{:S(2)}) copy-start(bf16[8,128]{1,0:T(8,128)(2,1)S(1)} %slice.81) | copy-start | bytes 6148
  55.7 8.9 %copy-start.7 = (bf16[2048]{0:T(1024)(128)(2,1)S(1)}, bf16[2048]{0:T(1024)(128)(2,1)}, u32[]{:S(2)}) copy-start(bf16[2048]{0:T(1024)(128)(2,1)} %param.22) | copy-start | bytes 12292
  55.7 18.9 %copy-start.3 = (bf16[8,2048]{1,0:T(8,128)(2,1)S(1)}, bf16[8,2048]{1,0:T(8,128)(2,1)}, u32[]{:S(2)}) copy-start(bf16[8,2048]{1,0:T(8,128)(2,1)} %hidden_ref.1) | copy-start | bytes 98308
  58.4 16.2 %all-to-all-start = ((bf16[64,8,128]{2,1,0:T(8,128)(2,1)}), bf16[64,8,128]{2,1,0:T(8,128)(2,1)S(1)}, u32[]{:S(2)}, u32[]{:S(2)}) async-start(bf16[64,8,128]{2,1,0:T(8,128)(2,1)} %broadcast_in_dim.31), calls=%async_computation | async-start | bytes 262144 | tf_op jit(solution)/shard_map/output_projection/all_to_all | solution.py:103
  78.7 15.1 %all-to-all-start.1 = ((bf16[64,2,128]{2,1,0:T(2,128)(2,1)}), bf16[64,2,128]{2,1,0:T(2,128)(2,1)S(1)}, u32[]{:S(2)}, u32[]{:S(2)}) async-start(bf16[64,2,128]{2,1,0:T(2,128)(2,1)} %copy.147), calls=%async_computation.1 | async-start | bytes 65536 | tf_op jit(solution)/shard_map/down_reduction/all_to_all | solution.py:239
  94.9 14.2 %all-to-all-start.2 = ((bf16[64,2,128]{2,1,0:T(2,128)(2,1)}), bf16[64,2,128]{2,1,0:T(2,128)(2,1)S(1)}, u32[]{:S(2)}, u32[]{:S(2)}) async-start(bf16[64,2,128]{2,1,0:T(2,128)(2,1)} %reshape.198), calls=%async_computation.2 | async-start | bytes 65536 | tf_op jit(solution)/shard_map/down_reduction/all_to_all | solution.py:103
Sparse Core Ops, SparseCore 0:
  10.1 43.2 all-gather.4
